TPU v7x, 128 devices: a whole 4x4x4 slice. The times are simulated.
128 devices in a mesh: mp: 2 (over y_hi), gx: 32 (over y_lo, z, x), gy: 2 (over core).
Axes of the slice: x: 4, y: 4 (y_hi: 2, y_lo: 2; y = y_hi * 2 + y_lo), z: 4, core: 2. Of those that a mesh axis runs over, the one named last changes fastest.
Arguments:
- tracers: float32 [16, 60, 512, 512], P(None, None, 'gx', ('mp', 'gy')), may hold values from -6 to 6
- wind_courant: float32 [2, 60, 512, 512], P(None, None, 'gx', ('mp', 'gy')), may hold values from -0.45 to 0.45
- pressure_head: float32 [8, 512, 512], P(None, ('gx', 'gy'), 'mp'), may hold values from -2 to 0.5
- storage: float32 [8, 512, 512], P(None, ('gx', 'gy'), 'mp'), may hold values from 0.05 to 0.5
- soil_type: int32 [512, 512], P(('gx', 'gy'), 'mp'), may hold values from 0 to 11
- land_mask: int32 [512, 512], P(('gx', 'gy'), 'mp'), may hold values 0 or 1
- conductivity_table: float32 [12], replicated, may hold values from 0.3 to 3
- exponent_table: float32 [12], replicated, may hold values from 0.2 to 1
Outputs:
- tracers_out: float32 [16, 60, 512, 512], P(None, None, 'gx', ('mp', 'gy'))
- new_head: float32 [8, 512, 512], P(None, ('gx', 'gy'), 'mp')
All inputs are finite; a program needn't handle non-finite values. No bound on the sum of `land_mask` on one device may be relied on, other than what follows from the above.
Results may differ from a plain program's by a relative error of at most 0.00002.
Values sent between devices are 32-bit elements; how exact they have to be, the bound alone decides.
No kernel may reach another device: no remote copies, remote signals or barrier semaphores. Data moves between devices by JAX's collectives and lax.ppermute only.
A program may use at most 256 MiB of HBM per device.

v0:
```python
import functools
import jax
import jax.numpy as jnp
from jax import lax
from jax.experimental import pallas as pl
from jax.experimental.pallas import tpu as pltpu
from jax.sharding import PartitionSpec as P

SWEEPS = 3
SB = 2
EB = 4


def shift_pairs(count, step):
    if step > 0:
        return [(i, i + 1) for i in range(count - 1)]
    return [(i + 1, i) for i in range(count - 1)]


def edge_kernel(f_ref, rf_ref, rl_ref, cf_ref, cl_ref):
    nb, nlev, rows, cols = f_ref.shape
    lane = lax.broadcasted_iota(jnp.int32, (rows, cols), 1)
    for b in range(nb):
        acc_f = jnp.zeros((rows, cols), jnp.float32)
        acc_l = jnp.zeros((rows, cols), jnp.float32)
        for lev in range(nlev):
            q = f_ref[b, lev]
            rf_ref[b, pl.ds(lev, 1), :] = q[0:1, :]
            rl_ref[b, pl.ds(lev, 1), :] = q[rows - 1:rows, :]
            at_lev = lane == lev
            acc_f = jnp.where(at_lev, pltpu.roll(q, lev, 1) if lev else q, acc_f)
            acc_l = jnp.where(at_lev, pltpu.roll(q, (lev + 1) % cols, 1), acc_l)
        cf_ref[b] = acc_f
        cl_ref[b] = acc_l


def edges(f):
    n, nlev, rows, cols = f.shape
    nb = EB if n % EB == 0 else 1
    row_shape = jax.ShapeDtypeStruct((n, nlev, cols), f.dtype)
    col_shape = jax.ShapeDtypeStruct((n, rows, cols), f.dtype)
    rspec = pl.BlockSpec((nb, nlev, cols), lambda i: (i, 0, 0))
    cspec = pl.BlockSpec((nb, rows, cols), lambda i: (i, 0, 0))
    return pl.pallas_call(
        edge_kernel,
        grid=(n // nb,),
        in_specs=[pl.BlockSpec((nb, nlev, rows, cols), lambda i: (i, 0, 0, 0))],
        out_specs=[rspec, rspec, cspec, cspec],
        out_shape=[row_shape, row_shape, col_shape, col_shape],
        cost_estimate=pl.CostEstimate(flops=4 * f.size, bytes_accessed=4 * f.size, transcendentals=0),
    )(f)


def step_kernel(f_ref, w_ref, ftop_ref, fbot_ref, wtop_ref, wbot_ref,
                fleft_ref, fright_ref, wleft_ref, wright_ref, o_ref):
    nb, nlev, rows, cols = f_ref.shape
    row = lax.broadcasted_iota(jnp.int32, (rows, cols), 0)
    lane = lax.broadcasted_iota(jnp.int32, (rows, cols), 1)
    first_row = row == 0
    last_row = row == rows - 1
    first_lane = lane == 0
    last_lane = lane == cols - 1

    def to_first(x, lev):
        return pltpu.roll(x, (cols - lev) % cols, 1) if lev else x

    def to_last(x, lev):
        s = (cols - 1 - lev) % cols
        return pltpu.roll(x, s, 1) if s else x

    for lev in range(nlev):
        u = w_ref[0, lev]
        v = w_ref[1, lev]
        u_prev = jnp.where(first_row, wtop_ref[0, pl.ds(lev, 1), :], pltpu.roll(u, 1, 0))
        u_next = jnp.where(last_row, wbot_ref[0, pl.ds(lev, 1), :], pltpu.roll(u, rows - 1, 0))
        v_prev = jnp.where(first_lane, to_first(wleft_ref[1], lev), pltpu.roll(v, 1, 1))
        v_next = jnp.where(last_lane, to_last(wright_ref[1], lev), pltpu.roll(v, cols - 1, 1))
        pu = jnp.maximum(u, 0.0)
        mu = jnp.minimum(u, 0.0)
        pu_prev = jnp.maximum(u_prev, 0.0)
        mu_next = jnp.minimum(u_next, 0.0)
        pv = jnp.maximum(v, 0.0)
        mv = jnp.minimum(v, 0.0)
        pv_prev = jnp.maximum(v_prev, 0.0)
        mv_next = jnp.minimum(v_next, 0.0)
        for b in range(nb):
            q = f_ref[b, lev]
            q_prev = jnp.where(first_row, ftop_ref[b, pl.ds(lev, 1), :], pltpu.roll(q, 1, 0))
            q_next = jnp.where(last_row, fbot_ref[b, pl.ds(lev, 1), :], pltpu.roll(q, rows - 1, 0))
            q_w = jnp.where(first_lane, to_first(fleft_ref[b], lev), pltpu.roll(q, 1, 1))
            q_e = jnp.where(last_lane, to_last(fright_ref[b], lev), pltpu.roll(q, cols - 1, 1))
            fxp = pu * q + mu_next * q_next
            fxm = pu_prev * q_prev + mu * q
            fyp = pv * q + mv_next * q_e
            fym = pv_prev * q_w + mv * q
            o_ref[b, lev] = q - (fxp - fxm) - (fyp - fym)


def advect_step(f, w, ftop, fbot, wtop, wbot, fleft, fright, wleft, wright):
    nsp, nlev, rows, cols = f.shape
    main = pl.BlockSpec((SB, nlev, rows, cols), lambda i: (i, 0, 0, 0))
    rowspec = pl.BlockSpec((SB, nlev, cols), lambda i: (i, 0, 0))
    colspec = pl.BlockSpec((SB, rows, cols), lambda i: (i, 0, 0))

    def whole(a):
        return pl.BlockSpec(a.shape, lambda i: (0,) * a.ndim)

    nbytes = 4 * (2 * f.size + w.size)
    return pl.pallas_call(
        step_kernel,
        grid=(nsp // SB,),
        in_specs=[main, whole(w), rowspec, rowspec, whole(wtop), whole(wbot),
                  colspec, colspec, whole(wleft), whole(wright)],
        out_specs=main,
        out_shape=jax.ShapeDtypeStruct(f.shape, f.dtype),
        cost_estimate=pl.CostEstimate(flops=20 * f.size, bytes_accessed=nbytes, transcendentals=0),
    )(f, w, ftop, fbot, wtop, wbot, fleft, fright, wleft, wright)


def exchange(first, last, axes):
    n = lax.axis_size(axes)
    before = lax.ppermute(last, axes, shift_pairs(n, 1))
    after = lax.ppermute(first, axes, shift_pairs(n, -1))
    return before, after


def advection(tracers, wind_courant):
    cols_axes = ("mp", "gy")
    qrf, qrl, qcf, qcl = edges(tracers)
    wrf, wrl, wcf, wcl = edges(wind_courant)
    qtop, qbot = exchange(qrf, qrl, "gx")
    wtop, wbot = exchange(wrf, wrl, "gx")
    qleft, qright = exchange(qcf, qcl, cols_axes)
    wleft, wright = exchange(wcf, wcl, cols_axes)
    mid = advect_step(tracers, wind_courant, qtop, qbot, wtop, wbot, qleft, qright, wleft, wright)
    srf, srl, scf, scl = edges(mid)
    stop, sbot = exchange(srf, srl, "gx")
    sleft, sright = exchange(scf, scl, cols_axes)
    return advect_step(mid, wind_courant, stop, sbot, wtop, wbot, sleft, sright, wleft, wright)


def padded_2(block, sides, width):
    for axis, dim in sides:
        count = lax.axis_size(axis)
        forward = [(i, i + 1) for i in range(count - 1)]
        backward = [(target, source) for source, target in forward]
        low = lax.ppermute(
            lax.slice_in_dim(block, block.shape[dim] - width, None, axis=dim), axis, forward
        )
        high = lax.ppermute(lax.slice_in_dim(block, 0, width, axis=dim), axis, backward)
        block = jnp.concatenate([low, block, high], axis=dim)
    return block


def harmonic(first_cond, second_cond):
    summed = first_cond + second_cond
    return 2.0 * first_cond * second_cond / jnp.where(summed > 0.0, summed, 1.0)


def sweep(padded, saturated, exponent, capacity, previous, surface, outside):
    conductance = saturated * jnp.exp(exponent * jnp.minimum(padded, 0.0))
    center = conductance[:, 1:-1, 1:-1]
    iterate = padded[:, 1:-1, 1:-1]
    east_face = harmonic(center, conductance[:, 2:, 1:-1])
    west_face = harmonic(center, conductance[:, :-2, 1:-1])
    north_face = harmonic(center, conductance[:, 1:-1, 2:])
    south_face = harmonic(center, conductance[:, 1:-1, :-2])
    lateral = (
        east_face * padded[:, 2:, 1:-1]
        + west_face * padded[:, :-2, 1:-1]
        + north_face * padded[:, 1:-1, 2:]
        + south_face * padded[:, 1:-1, :-2]
    )
    vertical = harmonic(center[:-1], center[1:])
    blank_layer = jnp.zeros_like(center[:1])
    below_face = jnp.concatenate([vertical, blank_layer], axis=0)
    above_face = jnp.concatenate([blank_layer, vertical], axis=0)
    inflow = jnp.concatenate([surface[None], jnp.zeros_like(center[1:])], axis=0)
    drainage = jnp.concatenate([jnp.zeros_like(center[:-1]), center[-1:]], axis=0)
    denominator = (
        capacity
        + east_face
        + west_face
        + north_face
        + south_face
        + above_face
        + below_face
        + outside
    )
    numerator = (
        capacity * previous
        + lateral
        + above_face * jnp.concatenate([blank_layer, iterate[:-1]], axis=0)
        + below_face * jnp.concatenate([iterate[1:], blank_layer], axis=0)
        + above_face
        - below_face
        + inflow
        - drainage
    )
    return numerator / denominator


def lookup(soil_kinds, values_table):
    matches = soil_kinds[None] == jnp.arange(values_table.shape[0], dtype=jnp.int32)[:, None, None]
    return jnp.sum(jnp.where(matches, values_table[:, None, None], jnp.float32(0.0)), axis=0)


def forcing_fields(advected):
    precip = jax.nn.softplus(advected[3, 0])
    evaporation = jax.nn.softplus(-advected[1, 0])
    radiation = jax.nn.sigmoid(advected[0, 0]) * jnp.exp(-jax.nn.softplus(advected[2, 0]))
    return jnp.stack([precip, evaporation, radiation], axis=0)


def on_device(
    tracers,
    wind_courant,
    pressure_head,
    storage,
    soil_type,
    land_mask,
    conductivity_table,
    exponent_table,
):
    advected = advection(tracers, wind_courant)
    received = lax.all_to_all(
        forcing_fields(advected), "gy", split_axis=1, concat_axis=2, tiled=True
    )
    surface = land_mask.astype(jnp.float32) * (received[0] - received[1] * received[2])
    saturated = lookup(soil_type, conductivity_table)
    exponent = lookup(soil_type, exponent_table)
    layers = pressure_head.shape[0]
    padded_head = padded_2(
        jnp.concatenate([pressure_head, saturated[None], exponent[None]], axis=0),
        ((("gx", "gy"), 1), ("mp", 2)),
        1,
    )
    saturated_padded = padded_head[layers]
    exponent_padded = padded_head[layers + 1]
    iterate = sweep(
        padded_head[:layers],
        saturated_padded,
        exponent_padded,
        storage,
        pressure_head,
        surface,
        0.0,
    )
    for repeat in range(SWEEPS - 1):
        padded_next = padded_2(iterate, ((("gx", "gy"), 1), ("mp", 2)), 1)
        iterate = sweep(
            padded_next, saturated_padded, exponent_padded, storage, pressure_head, surface, 0.0
        )
    return (advected, iterate)


def solution(mesh):
    placed = (
        P(None, None, "gx", ("mp", "gy")),
        P(None, None, "gx", ("mp", "gy")),
        P(None, ("gx", "gy"), "mp"),
        P(None, ("gx", "gy"), "mp"),
        P(("gx", "gy"), "mp"),
        P(("gx", "gy"), "mp"),
        P(),
        P(),
    )
    return jax.shard_map(
        on_device,
        mesh=mesh,
        in_specs=placed,
        out_specs=(P(None, None, "gx", ("mp", "gy")), P(None, ("gx", "gy"), "mp")),
        check_vma=False,
    )
```

profile of v0, /device:TPU:8, one launch (start us, length us, event | category | flops | bytes accessed | tf_op | source)
XLA Modules:
  0.0 173.3 jit_solution(439807235116130602)
XLA Ops:
  0.7 2.3 %shard_map.96 = (f32[2,60,128]{2,1,0:T(8,128)}, f32[2,60,128]{2,1,0:T(8,128)}, f32[2,16,128]{2,1,0:T(8,128)}, f32[2,16,128]{2,1,0:T(8,128)}) custom-call(f32[2,60,16,128]{3,2,1,0:T(8,128)} %w_ref.3), custom_call_target="tpu_custom_call" | custom-call | flops 983040 | bytes 983040 | tf_op jit(solution)/shard_map/pallas_call | solution.py:44
  3.0 3.5 %collective-permute-start.2 = (f32[2,60,128]{2,1,0:T(8,128)}, f32[2,60,128]{2,1,0:T(8,128)S(1)}, u32[]{:S(2)}, u32[]{:S(2)}) collective-permute-start(f32[2,60,128]{2,1,0:T(8,128)} %get-tuple-element.16), channel_id=1, source_target_pairs={{0,2},{2,4},{4,6},{6,8},{8,10},{10,12},{12,14},{14,16},{16,18},{18... | collective-permute-start | bytes 184328 | tf_op jit(solution)/shard_map/ppermute | solution.py:122
  6.6 7.4 %shard_map.95 = (f32[16,60,128]{2,1,0:T(8,128)}, f32[16,60,128]{2,1,0:T(8,128)}, f32[16,16,128]{2,1,0:T(8,128)}, f32[16,16,128]{2,1,0:T(8,128)}) custom-call(f32[16,60,16,128]{3,2,1,0:T(8,128)} %f_ref.5), custom_call_target="tpu_custom_call" | custom-call | flops 7864320 | bytes 7864320 | tf_op jit(solution)/shard_map/pallas_call | solution.py:44
  14.0 3.4 %collective-permute-start = (f32[16,60,128]{2,1,0:T(8,128)}, f32[16,60,128]{2,1,0:T(8,128)S(1)}, u32[]{:S(2)}, u32[]{:S(2)}) collective-permute-start(f32[16,60,128]{2,1,0:T(8,128)} %get-tuple-element.14), channel_id=1, source_target_pairs={{0,2},{2,4},{4,6},{6,8},{8,10},{10,12},{12,14},{14,16},{16,18},{18... | collective-permute-start | bytes 1474568 | tf_op jit(solution)/shard_map/ppermute | solution.py:122
  17.4 6.7 %collective-permute-start.1 = (f32[16,60,128]{2,1,0:T(8,128)}, f32[16,60,128]{2,1,0:T(8,128)S(1)}, u32[]{:S(2)}, u32[]{:S(2)}) collective-permute-start(f32[16,60,128]{2,1,0:T(8,128)} %get-tuple-element.15), channel_id=1, source_target_pairs={{2,0},{4,2},{6,4},{8,6},{10,8},{12,10},{14,12},{16,14},{18,16},{20... | collective-permute-start | bytes 1474568 | tf_op jit(solution)/shard_map/ppermute | solution.py:123
  24.1 0.1 select_reduce_fusion.1
  24.2 1.9 %collective-permute-start.12 = (f32[10,1,256]{2,1,0:T(1,128)S(1)}, f32[10,1,256]{2,1,0:T(1,128)S(1)}, u32[]{:S(2)}, u32[]{:S(2)}) collective-permute-start(f32[10,1,256]{2,1,0:T(1,128)S(1)} %get-tuple-element.41), channel_id=1, source_target_pairs={{0,1},{1,2},{2,3},{3,4},{4,5},{5,6},{6,7},{7,8},{8,9},{9,10},{10,1... | collective-permute-start | bytes 30728 | tf_op jit(solution)/shard_map/ppermute | solution.py:147
  26.1 7.9 %collective-permute-start.13 = (f32[10,1,256]{2,1,0:T(1,128)S(1)}, f32[10,1,256]{2,1,0:T(1,128)S(1)}, u32[]{:S(2)}, u32[]{:S(2)}) collective-permute-start(f32[10,1,256]{2,1,0:T(1,128)S(1)} %get-tuple-element.42), channel_id=1, source_target_pairs={{1,0},{2,1},{3,2},{4,3},{5,4},{6,5},{7,6},{8,7},{9,8},{10,9},{11,1... | collective-permute-start | bytes 30728 | tf_op jit(solution)/shard_map/ppermute | solution.py:150
  34.0 1.3 collective-permute-start.6
  35.3 0.0 collective-permute-done.13
  35.4 1.3 collective-permute-start.7
  36.7 2.9 %collective-permute-start.3 = (f32[2,60,128]{2,1,0:T(8,128)S(1)}, f32[2,60,128]{2,1,0:T(8,128)S(1)}, u32[]{:S(2)}, u32[]{:S(2)}) collective-permute-start(f32[2,60,128]{2,1,0:T(8,128)S(1)} %copy-done.18), channel_id=1, source_target_pairs={{2,0},{4,2},{6,4},{8,6},{10,8},{12,10},{14,12},{16,14},{18,16},{20... | collective-permute-start | bytes 184328 | tf_op jit(solution)/shard_map/ppermute | solution.py:123
  39.7 1.3 collective-permute-done.7.wright_ref
  41.0 6.3 %collective-permute-start.4 = (f32[16,16,128]{2,1,0:T(8,128)}, f32[16,16,128]{2,1,0:T(8,128)S(1)}, u32[]{:S(2)}, u32[]{:S(2)}) collective-permute-start(f32[16,16,128]{2,1,0:T(8,128)} %get-tuple-element.18), channel_id=1, source_target_pairs={{0,1},{1,64},{64,65},{2,3},{3,66},{66,67},{4,5},{5,68},{68,69},{6,... | collective-permute-start | bytes 393224 | tf_op jit(solution)/shard_map/ppermute | solution.py:122
  47.3 0.0 copy-start.6
  47.3 1.3 collective-permute-start.5
  48.6 0.1 fusion.70
  48.7 8.6 %collective-permute-start.14 = (f32[10,10,1]{2,1,0:T(8,128)S(1)}, f32[10,10,1]{2,1,0:T(8,128)S(1)}, u32[]{:S(2)}, u32[]{:S(2)}) collective-permute-start(f32[10,10,1]{2,1,0:T(8,128)S(1)} %get-tuple-element.35), channel_id=1, source_target_pairs={{0,64},{1,65},{2,66},{3,67},{4,68},{5,69},{6,70},{7,71},{8,72},{9,... | collective-permute-start | bytes 1208 | tf_op jit(solution)/shard_map/ppermute | solution.py:147
  57.3 1.3 collective-permute-start.15
  58.7 0.6 copy-done.9
  59.2 0.2 copy-done.2
  59.5 0.8 copy-done.3
  60.3 15.7 %shard_map.97.f_ref = f32[16,60,16,128]{3,2,1,0:T(8,128)} custom-call(f32[16,60,16,128]{3,2,1,0:T(8,128)} %f_ref.5, f32[2,60,16,128]{3,2,1,0:T(8,128)} %w_ref.3, f32[16,60,128]{2,1,0:T(8,128)} %copy-done.2, f32[16,60,128]{2,1,0:T(8,128)} %copy-done.3, f32[2,60,128]{2,1,0:T(8,128)} %copy-done.6, f32[2,60,128]{2,1,0:T(8,128)} %copy-done.7, ...), custom_call_target="tpu_custom_call" | custom-call | flops 39321600 | bytes 16711680 | tf_op jit(solution)/shard_map/pallas_call | solution.py:109
  76.0 7.4 %shard_map.98 = (f32[16,60,128]{2,1,0:T(8,128)}, f32[16,60,128]{2,1,0:T(8,128)}, f32[16,16,128]{2,1,0:T(8,128)}, f32[16,16,128]{2,1,0:T(8,128)}) custom-call(f32[16,60,16,128]{3,2,1,0:T(8,128)} %shard_map.97.f_ref), custom_call_target="tpu_custom_call" | custom-call | flops 7864320 | bytes 7864320 | tf_op jit(solution)/shard_map/pallas_call | solution.py:44
  83.4 1.9 %collective-permute-start.8 = (f32[16,60,128]{2,1,0:T(8,128)}, f32[16,60,128]{2,1,0:T(8,128)S(1)}, u32[]{:S(2)}, u32[]{:S(2)}) collective-permute-start(f32[16,60,128]{2,1,0:T(8,128)} %get-tuple-element.22), channel_id=1, source_target_pairs={{0,2},{2,4},{4,6},{6,8},{8,10},{10,12},{12,14},{14,16},{16,18},{18... | collective-permute-start | bytes 1474568 | tf_op jit(solution)/shard_map/ppermute | solution.py:122
  85.3 8.1 %collective-permute-start.9 = (f32[16,60,128]{2,1,0:T(8,128)}, f32[16,60,128]{2,1,0:T(8,128)S(1)}, u32[]{:S(2)}, u32[]{:S(2)}) collective-permute-start(f32[16,60,128]{2,1,0:T(8,128)} %get-tuple-element.23), channel_id=1, source_target_pairs={{2,0},{4,2},{6,4},{8,6},{10,8},{12,10},{14,12},{16,14},{18,16},{20... | collective-permute-start | bytes 1474568 | tf_op jit(solution)/shard_map/ppermute | solution.py:123
  93.5 0.1 maximum_bitcast_fusion.1
  93.6 0.2 fusion.3
  93.8 0.1 slice.312
  93.9 1.3 collective-permute-start.10
  95.2 1.3 collective-permute-start.11
  96.5 0.1 fusion.58
  96.6 6.4 %collective-permute-done.11.fright_ref = f32[16,16,128]{2,1,0:T(8,128)S(1)} collective-permute-done((f32[16,16,128]{2,1,0:T(8,128)}, f32[16,16,128]{2,1,0:T(8,128)S(1)}, u32[]{:S(2)}, u32[]{:S(2)}) %collective-permute-start.11) | collective-permute-done | bytes 131104 | tf_op jit(solution)/shard_map/ppermute | solution.py:123
  103.0 0.2 collective-permute-done.8.ftop_ref
  103.2 1.2 collective-permute-done.9.fbot_ref
  104.5 0.8 copy-done.5
  105.3 15.6 %shard_map.99 = f32[16,60,16,128]{3,2,1,0:T(8,128)} custom-call(f32[16,60,16,128]{3,2,1,0:T(8,128)} %shard_map.97.f_ref, f32[2,60,16,128]{3,2,1,0:T(8,128)} %w_ref.3, f32[16,60,128]{2,1,0:T(8,128)} %copy-done.4, f32[16,60,128]{2,1,0:T(8,128)} %copy-done.5, f32[2,60,128]{2,1,0:T(8,128)} %copy-done.6, f32[2,60,128]{2,1,0:T(8,128)} %copy-done.7, ...), custom_call_target="tpu_custom_call" | custom-call | flops 39321600 | bytes 16711680 | tf_op jit(solution)/shard_map/pallas_call | solution.py:109
  120.9 0.8 compare_select_fusion.17
  121.7 7.7 %all_to_all.15 = f32[3,16,128]{2,0,1:T(4,128)S(1)} all-to-all(f32[3,16,128]{2,0,1:T(4,128)S(1)} %copy.12), channel_id=1, replica_groups=mesh['mp'=2,'gx'=32,'gy'=2] {'gy'}, dimensions={1} | all-to-all | bytes 49152 | tf_op jit(solution)/shard_map/all_to_all | solution.py:226
  129.4 0.2 fusion.12
  129.7 2.1 %collective-permute-start.16 = (f32[8,1,256]{2,1,0:T(1,128)S(1)}, f32[8,1,256]{2,1,0:T(1,128)S(1)}, u32[]{:S(2)}, u32[]{:S(2)}) collective-permute-start(f32[8,1,256]{2,1,0:T(1,128)S(1)} %get-tuple-element.49), channel_id=1, source_target_pairs={{0,1},{1,2},{2,3},{3,4},{4,5},{5,6},{6,7},{7,8},{8,9},{9,10},{10,1... | collective-permute-start | bytes 24584 | tf_op jit(solution)/shard_map/ppermute | solution.py:147
  131.8 7.7 %collective-permute-start.17 = (f32[8,1,256]{2,1,0:T(1,128)S(1)}, f32[8,1,256]{2,1,0:T(1,128)S(1)}, u32[]{:S(2)}, u32[]{:S(2)}) collective-permute-start(f32[8,1,256]{2,1,0:T(1,128)S(1)} %get-tuple-element.50), channel_id=1, source_target_pairs={{1,0},{2,1},{3,2},{4,3},{5,4},{6,5},{7,6},{8,7},{9,8},{10,9},{11,1... | collective-permute-start | bytes 24584 | tf_op jit(solution)/shard_map/ppermute | solution.py:150
  139.5 1.3 collective-permute-done.17
  140.9 0.1 fusion.72
  140.9 2.3 %collective-permute-start.18 = (f32[8,10,1]{2,1,0:T(8,128)S(1)}, f32[8,10,1]{2,1,0:T(8,128)S(1)}, u32[]{:S(2)}, u32[]{:S(2)}) collective-permute-start(f32[8,10,1]{2,1,0:T(8,128)S(1)} %get-tuple-element.39), channel_id=1, source_target_pairs={{0,64},{1,65},{2,66},{3,67},{4,68},{5,69},{6,70},{7,71},{8,72},{9,... | collective-permute-start | bytes 968 | tf_op jit(solution)/shard_map/ppermute | solution.py:147
  143.2 1.3 collective-permute-start.19
  144.5 0.6 collective-permute-done.18
  145.1 5.8 %collective-permute-done.19 = f32[8,10,1]{2,1,0:T(8,128)S(1)} collective-permute-done((f32[8,10,1]{2,1,0:T(8,128)S(1)}, f32[8,10,1]{2,1,0:T(8,128)S(1)}, u32[]{:S(2)}, u32[]{:S(2)}) %collective-permute-start.19) | collective-permute-done | bytes 352 | tf_op jit(solution)/shard_map/ppermute | solution.py:150
  150.9 0.2 fusion.6
  151.1 0.1 fusion.59
  151.2 0.1 slice.326
  151.3 0.2 fusion.15
  151.5 1.9 %collective-permute-start.20 = (f32[8,1,256]{2,1,0:T(1,128)S(1)}, f32[8,1,256]{2,1,0:T(1,128)S(1)}, u32[]{:S(2)}, u32[]{:S(2)}) collective-permute-start(f32[8,1,256]{2,1,0:T(1,128)S(1)} %get-tuple-element.45), channel_id=1, source_target_pairs={{0,1},{1,2},{2,3},{3,4},{4,5},{5,6},{6,7},{7,8},{8,9},{9,10},{10,1... | collective-permute-start | bytes 24584 | tf_op jit(solution)/shard_map/ppermute | solution.py:147
  153.5 7.9 %collective-permute-start.21 = (f32[8,1,256]{2,1,0:T(1,128)S(1)}, f32[8,1,256]{2,1,0:T(1,128)S(1)}, u32[]{:S(2)}, u32[]{:S(2)}) collective-permute-start(f32[8,1,256]{2,1,0:T(1,128)S(1)} %get-tuple-element.46), channel_id=1, source_target_pairs={{1,0},{2,1},{3,2},{4,3},{5,4},{6,5},{7,6},{8,7},{9,8},{10,9},{11,1... | collective-permute-start | bytes 24584 | tf_op jit(solution)/shard_map/ppermute | solution.py:150
  161.3 1.3 collective-permute-done.21
  162.7 0.1 fusion.71
  162.8 1.6 collective-permute-start.22
  164.4 1.3 collective-permute-start.23
  165.7 0.6 collective-permute-done.22
  166.2 5.8 %collective-permute-done.23 = f32[8,10,1]{2,1,0:T(8,128)S(1)} collective-permute-done((f32[8,10,1]{2,1,0:T(8,128)S(1)}, f32[8,10,1]{2,1,0:T(8,128)S(1)}, u32[]{:S(2)}, u32[]{:S(2)}) %collective-permute-start.23) | collective-permute-done | bytes 352 | tf_op jit(solution)/shard_map/ppermute | solution.py:150
  172.0 0.2 fusion.9
  172.2 0.1 fusion.60
  172.3 0.1 slice.340
  172.4 0.9 fusion.18
  (63 shorter events, 0.3 us)
Async XLA Ops:
  0.6 23.4 %copy-start.14 = (s32[8,256]{1,0:T(8,128)S(1)}, s32[8,256]{1,0:T(8,128)}, u32[]{:S(2)}) copy-start(s32[8,256]{1,0:T(8,128)} %param.12) | copy-start | bytes 24580
  0.6 23.4 %copy-start.16 = (f32[12]{0:T(128)S(1)}, f32[12]{0:T(128)}, u32[]{:S(2)}) copy-start(f32[12]{0:T(128)} %param.14) | copy-start | bytes 148
  0.7 23.4 %copy-start.17 = (f32[12]{0:T(128)S(1)}, f32[12]{0:T(128)}, u32[]{:S(2)}) copy-start(f32[12]{0:T(128)} %param.15) | copy-start | bytes 148
  0.7 23.5 %copy-start = (f32[8,8,256]{2,1,0:T(8,128)S(1)}, f32[8,8,256]{2,1,0:T(8,128)}, u32[]{:S(2)}) copy-start(f32[8,8,256]{2,1,0:T(8,128)} %param.10) | copy-start | bytes 196612
  3.0 31.0 %copy-start.20 = (f32[2,16,128]{2,1,0:T(8,128)S(1)}, f32[2,16,128]{2,1,0:T(8,128)}, u32[]{:S(2)}) copy-start(f32[2,16,128]{2,1,0:T(8,128)} %get-tuple-element.20) | copy-start | bytes 49156
  3.0 32.4 %copy-start.19 = (f32[2,16,128]{2,1,0:T(8,128)S(1)}, f32[2,16,128]{2,1,0:T(8,128)}, u32[]{:S(2)}) copy-start(f32[2,16,128]{2,1,0:T(8,128)} %get-tuple-element.21) | copy-start | bytes 49156
  3.0 33.7 %copy-start.18 = (f32[2,60,128]{2,1,0:T(8,128)S(1)}, f32[2,60,128]{2,1,0:T(8,128)}, u32[]{:S(2)}) copy-start(f32[2,60,128]{2,1,0:T(8,128)} %get-tuple-element.17) | copy-start | bytes 184324
  3.0 44.2 %collective-permute-start.2 = (f32[2,60,128]{2,1,0:T(8,128)}, f32[2,60,128]{2,1,0:T(8,128)S(1)}, u32[]{:S(2)}, u32[]{:S(2)}) collective-permute-start(f32[2,60,128]{2,1,0:T(8,128)} %get-tuple-element.16), channel_id=1, source_target_pairs={{0,2},{2,4},{4,6},{6,8},{8,10},{10,12},{12,14},{14,16},{16,18},{18... | collective-permute-start | bytes 184328 | tf_op jit(solution)/shard_map/ppermute | solution.py:122
  14.0 44.6 %collective-permute-start = (f32[16,60,128]{2,1,0:T(8,128)}, f32[16,60,128]{2,1,0:T(8,128)S(1)}, u32[]{:S(2)}, u32[]{:S(2)}) collective-permute-start(f32[16,60,128]{2,1,0:T(8,128)} %get-tuple-element.14), channel_id=1, source_target_pairs={{0,2},{2,4},{4,6},{6,8},{8,10},{10,12},{12,14},{14,16},{16,18},{18... | collective-permute-start | bytes 1474568 | tf_op jit(solution)/shard_map/ppermute | solution.py:122
  17.4 41.3 %collective-permute-start.1 = (f32[16,60,128]{2,1,0:T(8,128)}, f32[16,60,128]{2,1,0:T(8,128)S(1)}, u32[]{:S(2)}, u32[]{:S(2)}) collective-permute-start(f32[16,60,128]{2,1,0:T(8,128)} %get-tuple-element.15), channel_id=1, source_target_pairs={{2,0},{4,2},{6,4},{8,6},{10,8},{12,10},{14,12},{16,14},{18,16},{20... | collective-permute-start | bytes 1474568 | tf_op jit(solution)/shard_map/ppermute | solution.py:123
  24.2 9.8 %collective-permute-start.12 = (f32[10,1,256]{2,1,0:T(1,128)S(1)}, f32[10,1,256]{2,1,0:T(1,128)S(1)}, u32[]{:S(2)}, u32[]{:S(2)}) collective-permute-start(f32[10,1,256]{2,1,0:T(1,128)S(1)} %get-tuple-element.41), channel_id=1, source_target_pairs={{0,1},{1,2},{2,3},{3,4},{4,5},{5,6},{6,7},{7,8},{8,9},{9,10},{10,1... | collective-permute-start | bytes 30728 | tf_op jit(solution)/shard_map/ppermute | solution.py:147
  26.1 9.2 %collective-permute-start.13 = (f32[10,1,256]{2,1,0:T(1,128)S(1)}, f32[10,1,256]{2,1,0:T(1,128)S(1)}, u32[]{:S(2)}, u32[]{:S(2)}) collective-permute-start(f32[10,1,256]{2,1,0:T(1,128)S(1)} %get-tuple-element.42), channel_id=1, source_target_pairs={{1,0},{2,1},{3,2},{4,3},{5,4},{6,5},{7,6},{8,7},{9,8},{10,9},{11,1... | collective-permute-start | bytes 30728 | tf_op jit(solution)/shard_map/ppermute | solution.py:150
  34.0 2.7 %collective-permute-start.6 = (f32[2,16,128]{2,1,0:T(8,128)S(1)}, f32[2,16,128]{2,1,0:T(8,128)S(1)}, u32[]{:S(2)}, u32[]{:S(2)}) collective-permute-start(f32[2,16,128]{2,1,0:T(8,128)S(1)} %copy-done.20), channel_id=1, source_target_pairs={{0,1},{1,64},{64,65},{2,3},{3,66},{66,67},{4,5},{5,68},{68,69},{6,... | collective-permute-start | bytes 49160 | tf_op jit(solution)/shard_map/ppermute | solution.py:122
  35.4 5.6 %collective-permute-start.7 = (f32[2,16,128]{2,1,0:T(8,128)S(1)}, f32[2,16,128]{2,1,0:T(8,128)S(1)}, u32[]{:S(2)}, u32[]{:S(2)}) collective-permute-start(f32[2,16,128]{2,1,0:T(8,128)S(1)} %copy-done.19), channel_id=1, source_target_pairs={{1,0},{64,1},{65,64},{3,2},{66,3},{67,66},{5,4},{68,5},{69,68},{7,... | collective-permute-start | bytes 49160 | tf_op jit(solution)/shard_map/ppermute | solution.py:123
  36.7 21.9 %copy-start.12 = (f32[2,16,128]{2,1,0:T(8,128)}, f32[2,16,128]{2,1,0:T(8,128)S(1)}, u32[]{:S(2)}) copy-start(f32[2,16,128]{2,1,0:T(8,128)S(1)} %collective-permute-done.6.wleft_ref) | copy-start | bytes 49156
  36.7 11.9 %collective-permute-start.3 = (f32[2,60,128]{2,1,0:T(8,128)S(1)}, f32[2,60,128]{2,1,0:T(8,128)S(1)}, u32[]{:S(2)}, u32[]{:S(2)}) collective-permute-start(f32[2,60,128]{2,1,0:T(8,128)S(1)} %copy-done.18), channel_id=1, source_target_pairs={{2,0},{4,2},{6,4},{8,6},{10,8},{12,10},{14,12},{16,14},{18,16},{20... | collective-permute-start | bytes 184328 | tf_op jit(solution)/shard_map/ppermute | solution.py:123
  41.0 17.7 %copy-start.13 = (f32[2,16,128]{2,1,0:T(8,128)}, f32[2,16,128]{2,1,0:T(8,128)S(1)}, u32[]{:S(2)}) copy-start(f32[2,16,128]{2,1,0:T(8,128)S(1)} %collective-permute-done.7.wright_ref) | copy-start | bytes 49156
  41.0 16.3 %collective-permute-start.4 = (f32[16,16,128]{2,1,0:T(8,128)}, f32[16,16,128]{2,1,0:T(8,128)S(1)}, u32[]{:S(2)}, u32[]{:S(2)}) collective-permute-start(f32[16,16,128]{2,1,0:T(8,128)} %get-tuple-element.18), channel_id=1, source_target_pairs={{0,1},{1,64},{64,65},{2,3},{3,66},{66,67},{4,5},{5,68},{68,69},{6,... | collective-permute-start | bytes 393224 | tf_op jit(solution)/shard_map/ppermute | solution.py:122
  47.3 11.4 %copy-start.6 = (f32[2,60,128]{2,1,0:T(8,128)}, f32[2,60,128]{2,1,0:T(8,128)S(1)}, u32[]{:S(2)}) copy-start(f32[2,60,128]{2,1,0:T(8,128)S(1)} %collective-permute-done.2.wtop_ref) | copy-start | bytes 184324
  47.3 11.3 %collective-permute-start.5 = (f32[16,16,128]{2,1,0:T(8,128)}, f32[16,16,128]{2,1,0:T(8,128)S(1)}, u32[]{:S(2)}, u32[]{:S(2)}) collective-permute-start(f32[16,16,128]{2,1,0:T(8,128)} %get-tuple-element.19), channel_id=1, source_target_pairs={{1,0},{64,1},{65,64},{3,2},{66,3},{67,66},{5,4},{68,5},{69,68},{7,... | collective-permute-start | bytes 393224 | tf_op jit(solution)/shard_map/ppermute | solution.py:123
  48.7 10.0 %copy-start.7 = (f32[2,60,128]{2,1,0:T(8,128)}, f32[2,60,128]{2,1,0:T(8,128)S(1)}, u32[]{:S(2)}) copy-start(f32[2,60,128]{2,1,0:T(8,128)S(1)} %collective-permute-done.3.wbot_ref) | copy-start | bytes 184324
  48.7 44.8 %collective-permute-start.14 = (f32[10,10,1]{2,1,0:T(8,128)S(1)}, f32[10,10,1]{2,1,0:T(8,128)S(1)}, u32[]{:S(2)}, u32[]{:S(2)}) collective-permute-start(f32[10,10,1]{2,1,0:T(8,128)S(1)} %get-tuple-element.35), channel_id=1, source_target_pairs={{0,64},{1,65},{2,66},{3,67},{4,68},{5,69},{6,70},{7,71},{8,72},{9,... | collective-permute-start | bytes 1208 | tf_op jit(solution)/shard_map/ppermute | solution.py:147
  57.3 1.4 copy-start.8
  57.3 36.2 %collective-permute-start.15 = (f32[10,10,1]{2,1,0:T(8,128)S(1)}, f32[10,10,1]{2,1,0:T(8,128)S(1)}, u32[]{:S(2)}, u32[]{:S(2)}) collective-permute-start(f32[10,10,1]{2,1,0:T(8,128)S(1)} %get-tuple-element.36), channel_id=1, source_target_pairs={{64,0},{65,1},{66,2},{67,3},{68,4},{69,5},{70,6},{71,7},{72,8},{73... | collective-permute-start | bytes 1208 | tf_op jit(solution)/shard_map/ppermute | solution.py:150
  58.6 0.7 copy-start.9
  58.6 0.9 copy-start.2
  59.5 0.8 copy-start.3
  83.4 19.8 %collective-permute-start.8 = (f32[16,60,128]{2,1,0:T(8,128)}, f32[16,60,128]{2,1,0:T(8,128)S(1)}, u32[]{:S(2)}, u32[]{:S(2)}) collective-permute-start(f32[16,60,128]{2,1,0:T(8,128)} %get-tuple-element.22), channel_id=1, source_target_pairs={{0,2},{2,4},{4,6},{6,8},{8,10},{10,12},{12,14},{14,16},{16,18},{18... | collective-permute-start | bytes 1474568 | tf_op jit(solution)/shard_map/ppermute | solution.py:122
  85.3 19.1 %collective-permute-start.9 = (f32[16,60,128]{2,1,0:T(8,128)}, f32[16,60,128]{2,1,0:T(8,128)S(1)}, u32[]{:S(2)}, u32[]{:S(2)}) collective-permute-start(f32[16,60,128]{2,1,0:T(8,128)} %get-tuple-element.23), channel_id=1, source_target_pairs={{2,0},{4,2},{6,4},{8,6},{10,8},{12,10},{14,12},{16,14},{18,16},{20... | collective-permute-start | bytes 1474568 | tf_op jit(solution)/shard_map/ppermute | solution.py:123
  93.9 2.7 %collective-permute-start.10 = (f32[16,16,128]{2,1,0:T(8,128)}, f32[16,16,128]{2,1,0:T(8,128)S(1)}, u32[]{:S(2)}, u32[]{:S(2)}) collective-permute-start(f32[16,16,128]{2,1,0:T(8,128)} %get-tuple-element.24), channel_id=1, source_target_pairs={{0,1},{1,64},{64,65},{2,3},{3,66},{66,67},{4,5},{5,68},{68,69},{6,... | collective-permute-start | bytes 393224 | tf_op jit(solution)/shard_map/ppermute | solution.py:122
  95.2 7.8 %collective-permute-start.11 = (f32[16,16,128]{2,1,0:T(8,128)}, f32[16,16,128]{2,1,0:T(8,128)S(1)}, u32[]{:S(2)}, u32[]{:S(2)}) collective-permute-start(f32[16,16,128]{2,1,0:T(8,128)} %get-tuple-element.25), channel_id=1, source_target_pairs={{1,0},{64,1},{65,64},{3,2},{66,3},{67,66},{5,4},{68,5},{69,68},{7,... | collective-permute-start | bytes 393224 | tf_op jit(solution)/shard_map/ppermute | solution.py:123
  96.6 32.8 %copy-start.15 = (s32[8,256]{1,0:T(8,128)S(1)}, s32[8,256]{1,0:T(8,128)}, u32[]{:S(2)}) copy-start(s32[8,256]{1,0:T(8,128)} %param.13) | copy-start | bytes 24580
  96.6 32.8 %copy-start.1 = (f32[8,8,256]{2,1,0:T(8,128)S(1)}, f32[8,8,256]{2,1,0:T(8,128)}, u32[]{:S(2)}) copy-start(f32[8,8,256]{2,1,0:T(8,128)} %param.11) | copy-start | bytes 196612
  96.6 7.9 %copy-start.10 = (f32[16,16,128]{2,1,0:T(8,128)}, f32[16,16,128]{2,1,0:T(8,128)S(1)}, u32[]{:S(2)}) copy-start(f32[16,16,128]{2,1,0:T(8,128)S(1)} %collective-permute-done.10.fleft_ref) | copy-start | bytes 393220
  103.0 1.5 copy-start.11
  103.2 1.2 copy-start.4
  104.5 0.8 copy-start.5
  129.7 9.8 %collective-permute-start.16 = (f32[8,1,256]{2,1,0:T(1,128)S(1)}, f32[8,1,256]{2,1,0:T(1,128)S(1)}, u32[]{:S(2)}, u32[]{:S(2)}) collective-permute-start(f32[8,1,256]{2,1,0:T(1,128)S(1)} %get-tuple-element.49), channel_id=1, source_target_pairs={{0,1},{1,2},{2,3},{3,4},{4,5},{5,6},{6,7},{7,8},{8,9},{9,10},{10,1... | collective-permute-start | bytes 24584 | tf_op jit(solution)/shard_map/ppermute | solution.py:147
  131.8 9.1 %collective-permute-start.17 = (f32[8,1,256]{2,1,0:T(1,128)S(1)}, f32[8,1,256]{2,1,0:T(1,128)S(1)}, u32[]{:S(2)}, u32[]{:S(2)}) collective-permute-start(f32[8,1,256]{2,1,0:T(1,128)S(1)} %get-tuple-element.50), channel_id=1, source_target_pairs={{1,0},{2,1},{3,2},{4,3},{5,4},{6,5},{7,6},{8,7},{9,8},{10,9},{11,1... | collective-permute-start | bytes 24584 | tf_op jit(solution)/shard_map/ppermute | solution.py:150
  140.9 4.2 %collective-permute-start.18 = (f32[8,10,1]{2,1,0:T(8,128)S(1)}, f32[8,10,1]{2,1,0:T(8,128)S(1)}, u32[]{:S(2)}, u32[]{:S(2)}) collective-permute-start(f32[8,10,1]{2,1,0:T(8,128)S(1)} %get-tuple-element.39), channel_id=1, source_target_pairs={{0,64},{1,65},{2,66},{3,67},{4,68},{5,69},{6,70},{7,71},{8,72},{9,... | collective-permute-start | bytes 968 | tf_op jit(solution)/shard_map/ppermute | solution.py:147
  143.2 7.7 %collective-permute-start.19 = (f32[8,10,1]{2,1,0:T(8,128)S(1)}, f32[8,10,1]{2,1,0:T(8,128)S(1)}, u32[]{:S(2)}, u32[]{:S(2)}) collective-permute-start(f32[8,10,1]{2,1,0:T(8,128)S(1)} %get-tuple-element.40), channel_id=1, source_target_pairs={{64,0},{65,1},{66,2},{67,3},{68,4},{69,5},{70,6},{71,7},{72,8},{73... | collective-permute-start | bytes 968 | tf_op jit(solution)/shard_map/ppermute | solution.py:150
  151.5 9.8 %collective-permute-start.20 = (f32[8,1,256]{2,1,0:T(1,128)S(1)}, f32[8,1,256]{2,1,0:T(1,128)S(1)}, u32[]{:S(2)}, u32[]{:S(2)}) collective-permute-start(f32[8,1,256]{2,1,0:T(1,128)S(1)} %get-tuple-element.45), channel_id=1, source_target_pairs={{0,1},{1,2},{2,3},{3,4},{4,5},{5,6},{6,7},{7,8},{8,9},{9,10},{10,1... | collective-permute-start | bytes 24584 | tf_op jit(solution)/shard_map/ppermute | solution.py:147
  153.5 9.2 %collective-permute-start.21 = (f32[8,1,256]{2,1,0:T(1,128)S(1)}, f32[8,1,256]{2,1,0:T(1,128)S(1)}, u32[]{:S(2)}, u32[]{:S(2)}) collective-permute-start(f32[8,1,256]{2,1,0:T(1,128)S(1)} %get-tuple-element.46), channel_id=1, source_target_pairs={{1,0},{2,1},{3,2},{4,3},{5,4},{6,5},{7,6},{8,7},{9,8},{10,9},{11,1... | collective-permute-start | bytes 24584 | tf_op jit(solution)/shard_map/ppermute | solution.py:150
  162.8 3.5 %collective-permute-start.22 = (f32[8,10,1]{2,1,0:T(8,128)S(1)}, f32[8,10,1]{2,1,0:T(8,128)S(1)}, u32[]{:S(2)}, u32[]{:S(2)}) collective-permute-start(f32[8,10,1]{2,1,0:T(8,128)S(1)} %get-tuple-element.37), channel_id=1, source_target_pairs={{0,64},{1,65},{2,66},{3,67},{4,68},{5,69},{6,70},{7,71},{8,72},{9,... | collective-permute-start | bytes 968 | tf_op jit(solution)/shard_map/ppermute | solution.py:147
  164.4 7.7 %collective-permute-start.23 = (f32[8,10,1]{2,1,0:T(8,128)S(1)}, f32[8,10,1]{2,1,0:T(8,128)S(1)}, u32[]{:S(2)}, u32[]{:S(2)}) collective-permute-start(f32[8,10,1]{2,1,0:T(8,128)S(1)} %get-tuple-element.38), channel_id=1, source_target_pairs={{64,0},{65,1},{66,2},{67,3},{68,4},{69,5},{70,6},{71,7},{72,8},{73... | collective-permute-start | bytes 968 | tf_op jit(solution)/shard_map/ppermute | solution.py:150
where the time goes:
time: 175 us; the launch traced here: 173 us
  starting transfers between devices  84.9 us (49%)
  Pallas kernels  48.5 us (28%)
  waiting for transfers between devices  24.6 us (14%)
  blocking collectives  7.7 us (4%)
  other arithmetic  3.32 us (2%)
  local copies, waits for them, and re-layouts  3.01 us (2%)
    pallas_call x2, Pallas kernels, advect_step(): pl.pallas_call(step_kernel, grid=(nsp // SB,), in_specs=[main, whole(w),...  31.3 us
    ppermute x6, starting transfers between devices, padded_2(): lax.ppermute(lax.slice_in_dim(block, 0, width, axis=dim), axis, backward)  27.3 us
    ppermute x6, starting transfers between devices, exchange(): after = lax.ppermute(first, axes, shift_pairs(n, -1))  21.6 us
    ppermute x6, starting transfers between devices, padded_2(): lax.ppermute(lax.slice_in_dim(block, block.shape[dim] - width, None, axis...  18.3 us
    ppermute x6, starting transfers between devices, exchange(): before = lax.ppermute(last, axes, shift_pairs(n, 1))  17.7 us
    pallas_call x3, Pallas kernels, edges(): pl.pallas_call(edge_kernel, grid=(n // nb,), in_specs=[pl.BlockSpec((nb,...  17.2 us
    ppermute x6, waiting for transfers between devices, padded_2(): lax.ppermute(lax.slice_in_dim(block, 0, width, axis=dim), axis, backward)  14.3 us
    ppermute x6, waiting for transfers between devices, exchange(): after = lax.ppermute(first, axes, shift_pairs(n, -1))  8.91 us
  transfers between devices with their start and end apart: 24, of which 10 were waited for; matrix products, arithmetic and copies ran while one was open for 0% of the time, Pallas kernels for 18%

commit v1 on v0

--- a/solution.py
+++ b/solution.py
@@ -17,38 +17,64 @@
     return [(i + 1, i) for i in range(count - 1)]
 
 
-def edge_kernel(f_ref, rf_ref, rl_ref, cf_ref, cl_ref):
-    nb, nlev, rows, cols = f_ref.shape
+def edge_body(f_ref, b, rf_ref, rl_ref, cf_ref, cl_ref):
+    nlev, rows, cols = f_ref.shape[1:]
     lane = lax.broadcasted_iota(jnp.int32, (rows, cols), 1)
-    for b in range(nb):
-        acc_f = jnp.zeros((rows, cols), jnp.float32)
-        acc_l = jnp.zeros((rows, cols), jnp.float32)
-        for lev in range(nlev):
-            q = f_ref[b, lev]
-            rf_ref[b, pl.ds(lev, 1), :] = q[0:1, :]
-            rl_ref[b, pl.ds(lev, 1), :] = q[rows - 1:rows, :]
-            at_lev = lane == lev
-            acc_f = jnp.where(at_lev, pltpu.roll(q, lev, 1) if lev else q, acc_f)
-            acc_l = jnp.where(at_lev, pltpu.roll(q, (lev + 1) % cols, 1), acc_l)
-        cf_ref[b] = acc_f
-        cl_ref[b] = acc_l
-
-
-def edges(f):
+    acc_f = jnp.zeros((rows, cols), jnp.float32)
+    acc_l = jnp.zeros((rows, cols), jnp.float32)
+    for lev in range(nlev):
+        q = f_ref[b, lev]
+        rf_ref[b, pl.ds(lev, 1), :] = q[0:1, :]
+        rl_ref[b, pl.ds(lev, 1), :] = q[rows - 1:rows, :]
+        at_lev = lane == lev
+        acc_f = jnp.where(at_lev, pltpu.roll(q, lev, 1) if lev else q, acc_f)
+        acc_l = jnp.where(at_lev, pltpu.roll(q, (lev + 1) % cols, 1), acc_l)
+    cf_ref[b] = acc_f
+    cl_ref[b] = acc_l
+
+
+def edge_kernel(nmain, f_ref, *refs):
+    if len(refs) == 5:
+        w_ref, outs = refs[0], refs[1:]
+    else:
+        w_ref, outs = None, refs
+    i = pl.program_id(0)
+
+    @pl.when(i < nmain)
+    def _():
+        for b in range(f_ref.shape[0]):
+            edge_body(f_ref, b, *outs)
+
+    if w_ref is not None:
+        @pl.when(i == nmain)
+        def _():
+            for b in range(w_ref.shape[0]):
+                edge_body(w_ref, b, *outs)
+
+
+def edges(f, w=None):
     n, nlev, rows, cols = f.shape
-    nb = EB if n % EB == 0 else 1
-    row_shape = jax.ShapeDtypeStruct((n, nlev, cols), f.dtype)
-    col_shape = jax.ShapeDtypeStruct((n, rows, cols), f.dtype)
+    nb = 2
+    nmain = n // nb
+    total = n + (0 if w is None else w.shape[0])
+    row_shape = jax.ShapeDtypeStruct((total, nlev, cols), f.dtype)
+    col_shape = jax.ShapeDtypeStruct((total, rows, cols), f.dtype)
     rspec = pl.BlockSpec((nb, nlev, cols), lambda i: (i, 0, 0))
     cspec = pl.BlockSpec((nb, rows, cols), lambda i: (i, 0, 0))
+    in_specs = [pl.BlockSpec((nb, nlev, rows, cols), lambda i: (jnp.minimum(i, nmain - 1), 0, 0, 0))]
+    args = [f]
+    if w is not None:
+        in_specs.append(pl.BlockSpec(w.shape, lambda i: (0, 0, 0, 0)))
+        args.append(w)
     return pl.pallas_call(
-        edge_kernel,
-        grid=(n // nb,),
-        in_specs=[pl.BlockSpec((nb, nlev, rows, cols), lambda i: (i, 0, 0, 0))],
+        functools.partial(edge_kernel, nmain),
+        grid=(total // nb,),
+        in_specs=in_specs,
         out_specs=[rspec, rspec, cspec, cspec],
         out_shape=[row_shape, row_shape, col_shape, col_shape],
-        cost_estimate=pl.CostEstimate(flops=4 * f.size, bytes_accessed=4 * f.size, transcendentals=0),
-    )(f)
+        cost_estimate=pl.CostEstimate(flops=4 * total * nlev * rows * cols,
+                                      bytes_accessed=4 * total * nlev * rows * cols, transcendentals=0),
+    )(*args)
 
 
 def step_kernel(f_ref, w_ref, ftop_ref, fbot_ref, wtop_ref, wbot_ref,
@@ -101,16 +127,15 @@
     main = pl.BlockSpec((SB, nlev, rows, cols), lambda i: (i, 0, 0, 0))
     rowspec = pl.BlockSpec((SB, nlev, cols), lambda i: (i, 0, 0))
     colspec = pl.BlockSpec((SB, rows, cols), lambda i: (i, 0, 0))
-
-    def whole(a):
-        return pl.BlockSpec(a.shape, lambda i: (0,) * a.ndim)
-
+    wblock = nsp // 2
+    wrowspec = pl.BlockSpec((2, nlev, cols), lambda i: (wblock, 0, 0))
+    wcolspec = pl.BlockSpec((2, rows, cols), lambda i: (wblock, 0, 0))
     nbytes = 4 * (2 * f.size + w.size)
     return pl.pallas_call(
         step_kernel,
         grid=(nsp // SB,),
-        in_specs=[main, whole(w), rowspec, rowspec, whole(wtop), whole(wbot),
-                  colspec, colspec, whole(wleft), whole(wright)],
+        in_specs=[main, pl.BlockSpec(w.shape, lambda i: (0, 0, 0, 0)), rowspec, rowspec, wrowspec, wrowspec,
+                  colspec, colspec, wcolspec, wcolspec],
         out_specs=main,
         out_shape=jax.ShapeDtypeStruct(f.shape, f.dtype),
         cost_estimate=pl.CostEstimate(flops=20 * f.size, bytes_accessed=nbytes, transcendentals=0),
@@ -126,30 +151,29 @@
 
 def advection(tracers, wind_courant):
     cols_axes = ("mp", "gy")
-    qrf, qrl, qcf, qcl = edges(tracers)
-    wrf, wrl, wcf, wcl = edges(wind_courant)
-    qtop, qbot = exchange(qrf, qrl, "gx")
-    wtop, wbot = exchange(wrf, wrl, "gx")
-    qleft, qright = exchange(qcf, qcl, cols_axes)
-    wleft, wright = exchange(wcf, wcl, cols_axes)
-    mid = advect_step(tracers, wind_courant, qtop, qbot, wtop, wbot, qleft, qright, wleft, wright)
+    rf, rl, cf, cl = edges(tracers, wind_courant)
+    top, bot = exchange(rf, rl, "gx")
+    left, right = exchange(cf, cl, cols_axes)
+    mid = advect_step(tracers, wind_courant, top, bot, top, bot, left, right, left, right)
     srf, srl, scf, scl = edges(mid)
     stop, sbot = exchange(srf, srl, "gx")
     sleft, sright = exchange(scf, scl, cols_axes)
-    return advect_step(mid, wind_courant, stop, sbot, wtop, wbot, sleft, sright, wleft, wright)
+    return advect_step(mid, wind_courant, stop, sbot, top, bot, sleft, sright, left, right)
 
 
 def padded_2(block, sides, width):
-    for axis, dim in sides:
-        count = lax.axis_size(axis)
-        forward = [(i, i + 1) for i in range(count - 1)]
-        backward = [(target, source) for source, target in forward]
-        low = lax.ppermute(
-            lax.slice_in_dim(block, block.shape[dim] - width, None, axis=dim), axis, forward
-        )
-        high = lax.ppermute(lax.slice_in_dim(block, 0, width, axis=dim), axis, backward)
-        block = jnp.concatenate([low, block, high], axis=dim)
-    return block
+    (row_axes, row_dim), (col_axes, col_dim) = sides
+    rows, cols = block.shape[row_dim], block.shape[col_dim]
+    top, bot = exchange(lax.slice_in_dim(block, 0, 1, axis=row_dim),
+                        lax.slice_in_dim(block, rows - 1, rows, axis=row_dim), row_axes)
+    left, right = exchange(lax.slice_in_dim(block, 0, 1, axis=col_dim),
+                           lax.slice_in_dim(block, cols - 1, cols, axis=col_dim), col_axes)
+    mid = jnp.concatenate([top, block, bot], axis=row_dim)
+    spec = [(0, 0)] * block.ndim
+    spec[row_dim] = (1, 1)
+    left = jnp.pad(left, spec)
+    right = jnp.pad(right, spec)
+    return jnp.concatenate([left, mid, right], axis=col_dim)
 
 
 def harmonic(first_cond, second_cond):

time: 175 us -> 150 us (0.86)
  the two profiles are of different devices: /device:TPU:8 before, /device:TPU:31 now
where the time goes in v1:
time: 150 us; the launch traced here: 149 us
  starting transfers between devices  55.7 us (37%)
  Pallas kernels  50.3 us (34%)
  waiting for transfers between devices  30.5 us (20%)
  blocking collectives  4.65 us (3%)
  other arithmetic  3.25 us (2%)
  local copies, waits for them, and re-layouts  3.12 us (2%)
    ppermute x10, starting transfers between devices, exchange(): after = lax.ppermute(first, axes, shift_pairs(n, -1))  34.2 us
    pallas_call x2, Pallas kernels, advect_step(): pl.pallas_call(step_kernel, grid=(nsp // SB,), in_specs=[main, pl.BlockSp...  31.3 us
    ppermute x10, starting transfers between devices, exchange(): before = lax.ppermute(last, axes, shift_pairs(n, 1))  21.6 us
    pallas_call x2, Pallas kernels, edges(): pl.pallas_call(functools.partial(edge_kernel, nmain), grid=(total // nb,)...  19 us
    ppermute x10, waiting for transfers between devices, exchange(): after = lax.ppermute(first, axes, shift_pairs(n, -1))  15.9 us
    ppermute x10, waiting for transfers between devices, exchange(): before = lax.ppermute(last, axes, shift_pairs(n, 1))  14.6 us
    all_to_all x1, blocking collectives, on_device(): lax.all_to_all(forcing_fields(advected), 'gy', split_axis=1, concat_axis=...  4.65 us
  transfers between devices with their start and end apart: 20, of which 6 were waited for; matrix products, arithmetic and copies ran while one was open for 1% of the time, Pallas kernels for 17%

profile of v1, /device:TPU:31, one launch (start us, length us, event | category | flops | bytes accessed | tf_op | source)
XLA Modules:
  0.0 148.8 jit_solution(9606922126536442720)
XLA Ops:
  0.7 10.0 %shard_map.95 = (f32[18,60,128]{2,1,0:T(8,128)}, f32[18,60,128]{2,1,0:T(8,128)}, f32[18,16,128]{2,1,0:T(8,128)}, f32[18,16,128]{2,1,0:T(8,128)}) custom-call(f32[16,60,16,128]{3,2,1,0:T(8,128)} %f_ref.3, f32[2,60,16,128]{3,2,1,0:T(8,128)} %w_ref.3), custom_call_target="tpu_custom_call" | custom-call | flops 8847360 | bytes 8847360 | tf_op jit(solution)/shard_map/pallas_call | solution.py:69
  10.7 3.4 %collective-permute-start = (f32[18,60,128]{2,1,0:T(8,128)}, f32[18,60,128]{2,1,0:T(8,128)S(1)}, u32[]{:S(2)}, u32[]{:S(2)}) collective-permute-start(f32[18,60,128]{2,1,0:T(8,128)} %get-tuple-element.10), channel_id=1, source_target_pairs={{0,2},{2,4},{4,6},{6,8},{8,10},{10,12},{12,14},{14,16},{16,18},{18... | collective-permute-start | bytes 1658888 | tf_op jit(solution)/shard_map/ppermute | solution.py:147
  14.1 1.9 %collective-permute-start.1 = (f32[18,60,128]{2,1,0:T(8,128)}, f32[18,60,128]{2,1,0:T(8,128)S(1)}, u32[]{:S(2)}, u32[]{:S(2)}) collective-permute-start(f32[18,60,128]{2,1,0:T(8,128)} %get-tuple-element.11), channel_id=1, source_target_pairs={{2,0},{4,2},{6,4},{8,6},{10,8},{12,10},{14,12},{16,14},{18,16},{20... | collective-permute-start | bytes 1658888 | tf_op jit(solution)/shard_map/ppermute | solution.py:148
  16.0 1.3 collective-permute-start.2
  17.4 0.1 select_reduce_fusion.1
  17.5 0.1 fusion.70
  17.6 1.3 collective-permute-start.8
  18.9 6.5 %collective-permute-start.11 = (f32[10,8,1]{2,1,0:T(8,128)S(1)}, f32[10,8,1]{2,1,0:T(8,128)S(1)}, u32[]{:S(2)}, u32[]{:S(2)}) collective-permute-start(f32[10,8,1]{2,1,0:T(8,128)S(1)} %get-tuple-element.30), channel_id=1, source_target_pairs={{64,0},{65,1},{66,2},{67,3},{68,4},{69,5},{70,6},{71,7},{72,8},{73... | collective-permute-start | bytes 968 | tf_op jit(solution)/shard_map/ppermute | solution.py:148
  25.4 12.0 %collective-permute-done.8 = f32[10,8,1]{2,1,0:T(8,128)S(1)} collective-permute-done((f32[10,8,1]{2,1,0:T(8,128)S(1)}, f32[10,8,1]{2,1,0:T(8,128)S(1)}, u32[]{:S(2)}, u32[]{:S(2)}) %collective-permute-start.8) | collective-permute-done | bytes 352 | tf_op jit(solution)/shard_map/ppermute | solution.py:147
  37.4 1.3 collective-permute-start.3
  38.7 2.5 %collective-permute-start.10 = (f32[10,1,256]{2,1,0:T(1,128)S(1)}, f32[10,1,256]{2,1,0:T(1,128)S(1)}, u32[]{:S(2)}, u32[]{:S(2)}) collective-permute-start(f32[10,1,256]{2,1,0:T(1,128)S(1)} %get-tuple-element.28), channel_id=1, source_target_pairs={{1,0},{2,1},{3,2},{4,3},{5,4},{6,5},{7,6},{8,7},{9,8},{10,9},{11,1... | collective-permute-start | bytes 30728 | tf_op jit(solution)/shard_map/ppermute | solution.py:148
  41.2 5.2 %collective-permute-start.9 = (f32[10,1,256]{2,1,0:T(1,128)S(1)}, f32[10,1,256]{2,1,0:T(1,128)S(1)}, u32[]{:S(2)}, u32[]{:S(2)}) collective-permute-start(f32[10,1,256]{2,1,0:T(1,128)S(1)} %get-tuple-element.27), channel_id=1, source_target_pairs={{0,1},{1,2},{2,3},{3,4},{4,5},{5,6},{6,7},{7,8},{8,9},{9,10},{10,1... | collective-permute-start | bytes 30728 | tf_op jit(solution)/shard_map/ppermute | solution.py:147
  46.5 0.0 collective-permute-done.ftop_ref.wtop_ref
  46.6 0.0 collective-permute-done.1.fbot_ref.wbot_ref
  46.6 0.6 copy-done.4
  47.2 0.3 copy-done
  47.4 0.8 copy-done.1
  48.3 15.7 %shard_map.96.f_ref = f32[16,60,16,128]{3,2,1,0:T(8,128)} custom-call(f32[16,60,16,128]{3,2,1,0:T(8,128)} %f_ref.3, f32[2,60,16,128]{3,2,1,0:T(8,128)} %w_ref.3, f32[18,60,128]{2,1,0:T(8,128)} %copy-done, f32[18,60,128]{2,1,0:T(8,128)} %copy-done.1, f32[18,60,128]{2,1,0:T(8,128)} %copy-done, f32[18,60,128]{2,1,0:T(8,128)} %copy-done.1, ...), custom_call_target="tpu_custom_call" | custom-call | flops 39321600 | bytes 16711680 | tf_op jit(solution)/shard_map/pallas_call | solution.py:134
  63.9 9.0 %shard_map.97 = (f32[16,60,128]{2,1,0:T(8,128)}, f32[16,60,128]{2,1,0:T(8,128)}, f32[16,16,128]{2,1,0:T(8,128)}, f32[16,16,128]{2,1,0:T(8,128)}) custom-call(f32[16,60,16,128]{3,2,1,0:T(8,128)} %shard_map.96.f_ref), custom_call_target="tpu_custom_call" | custom-call | flops 7864320 | bytes 7864320 | tf_op jit(solution)/shard_map/pallas_call | solution.py:69
  72.9 1.9 %collective-permute-start.4 = (f32[16,60,128]{2,1,0:T(8,128)}, f32[16,60,128]{2,1,0:T(8,128)S(1)}, u32[]{:S(2)}, u32[]{:S(2)}) collective-permute-start(f32[16,60,128]{2,1,0:T(8,128)} %get-tuple-element.14), channel_id=1, source_target_pairs={{0,2},{2,4},{4,6},{6,8},{8,10},{10,12},{12,14},{14,16},{16,18},{18... | collective-permute-start | bytes 1474568 | tf_op jit(solution)/shard_map/ppermute | solution.py:147
  74.8 3.4 %collective-permute-start.5 = (f32[16,60,128]{2,1,0:T(8,128)}, f32[16,60,128]{2,1,0:T(8,128)S(1)}, u32[]{:S(2)}, u32[]{:S(2)}) collective-permute-start(f32[16,60,128]{2,1,0:T(8,128)} %get-tuple-element.15), channel_id=1, source_target_pairs={{2,0},{4,2},{6,4},{8,6},{10,8},{12,10},{14,12},{16,14},{18,16},{20... | collective-permute-start | bytes 1474568 | tf_op jit(solution)/shard_map/ppermute | solution.py:148
  78.2 0.0 collective-permute-done.10
  78.2 0.0 collective-permute-done.9
  78.2 0.1 maximum_bitcast_fusion.1
  78.3 0.2 fusion.3
  78.5 0.1 slice.312
  78.6 1.3 collective-permute-start.6
  79.9 3.0 %collective-permute-start.7 = (f32[16,16,128]{2,1,0:T(8,128)}, f32[16,16,128]{2,1,0:T(8,128)S(1)}, u32[]{:S(2)}, u32[]{:S(2)}) collective-permute-start(f32[16,16,128]{2,1,0:T(8,128)} %get-tuple-element.17), channel_id=1, source_target_pairs={{1,0},{64,1},{65,64},{3,2},{66,3},{67,66},{5,4},{68,5},{69,68},{7,... | collective-permute-start | bytes 393224 | tf_op jit(solution)/shard_map/ppermute | solution.py:148
  82.9 0.1 fusion.58
  83.1 0.0 copy-start.11
  83.1 0.0 copy-start.5
  83.1 0.0 collective-permute-done.6.fleft_ref
  83.1 1.0 collective-permute-done.7.fright_ref
  84.1 2.5 %collective-permute-done.4.ftop_ref = f32[16,60,128]{2,1,0:T(8,128)S(1)} collective-permute-done((f32[16,60,128]{2,1,0:T(8,128)}, f32[16,60,128]{2,1,0:T(8,128)S(1)}, u32[]{:S(2)}, u32[]{:S(2)}) %collective-permute-start.4) | collective-permute-done | bytes 491552 | tf_op jit(solution)/shard_map/ppermute | solution.py:147
  86.6 5.5 %collective-permute-done.5.fbot_ref = f32[16,60,128]{2,1,0:T(8,128)S(1)} collective-permute-done((f32[16,60,128]{2,1,0:T(8,128)}, f32[16,60,128]{2,1,0:T(8,128)S(1)}, u32[]{:S(2)}, u32[]{:S(2)}) %collective-permute-start.5) | collective-permute-done | bytes 491552 | tf_op jit(solution)/shard_map/ppermute | solution.py:148
  92.2 0.8 copy-done.7
  93.0 15.6 %shard_map.98 = f32[16,60,16,128]{3,2,1,0:T(8,128)} custom-call(f32[16,60,16,128]{3,2,1,0:T(8,128)} %shard_map.96.f_ref, f32[2,60,16,128]{3,2,1,0:T(8,128)} %w_ref.3, f32[16,60,128]{2,1,0:T(8,128)} %copy-done.6, f32[16,60,128]{2,1,0:T(8,128)} %copy-done.7, f32[18,60,128]{2,1,0:T(8,128)} %copy-done, f32[18,60,128]{2,1,0:T(8,128)} %copy-done.1, ...), custom_call_target="tpu_custom_call" | custom-call | flops 39321600 | bytes 16711680 | tf_op jit(solution)/shard_map/pallas_call | solution.py:134
  108.6 0.8 compare_select_fusion.17
  109.4 4.7 %all_to_all.15 = f32[3,16,128]{2,0,1:T(4,128)S(1)} all-to-all(f32[3,16,128]{2,0,1:T(4,128)S(1)} %copy.12), channel_id=1, replica_groups=mesh['mp'=2,'gx'=32,'gy'=2] {'gy'}, dimensions={1} | all-to-all | bytes 49152 | tf_op jit(solution)/shard_map/all_to_all | solution.py:250
  114.1 0.2 fusion.12
  114.3 0.1 fusion.75
  114.4 1.3 collective-permute-start.12
  115.7 5.5 %collective-permute-start.15 = (f32[8,8,1]{2,1,0:T(8,128)S(1)}, f32[8,8,1]{2,1,0:T(8,128)S(1)}, u32[]{:S(2)}, u32[]{:S(2)}) collective-permute-start(f32[8,8,1]{2,1,0:T(8,128)S(1)} %get-tuple-element.40), channel_id=1, source_target_pairs={{64,0},{65,1},{66,2},{67,3},{68,4},{69,5},{70,6},{71,7},{72,8},{73... | collective-permute-start | bytes 776 | tf_op jit(solution)/shard_map/ppermute | solution.py:148
  121.2 2.1 %collective-permute-start.13 = (f32[8,1,256]{2,1,0:T(1,128)S(1)}, f32[8,1,256]{2,1,0:T(1,128)S(1)}, u32[]{:S(2)}, u32[]{:S(2)}) collective-permute-start(f32[8,1,256]{2,1,0:T(1,128)S(1)} %get-tuple-element.41), channel_id=1, source_target_pairs={{0,1},{1,2},{2,3},{3,4},{4,5},{5,6},{6,7},{7,8},{8,9},{9,10},{10,1... | collective-permute-start | bytes 24584 | tf_op jit(solution)/shard_map/ppermute | solution.py:147
  123.3 2.7 %collective-permute-start.14 = (f32[8,1,256]{2,1,0:T(1,128)S(1)}, f32[8,1,256]{2,1,0:T(1,128)S(1)}, u32[]{:S(2)}, u32[]{:S(2)}) collective-permute-start(f32[8,1,256]{2,1,0:T(1,128)S(1)} %get-tuple-element.42), channel_id=1, source_target_pairs={{1,0},{2,1},{3,2},{4,3},{5,4},{6,5},{7,6},{8,7},{9,8},{10,9},{11,1... | collective-permute-start | bytes 24584 | tf_op jit(solution)/shard_map/ppermute | solution.py:148
  126.0 0.0 collective-permute-done.15
  126.1 0.0 collective-permute-done.13
  126.1 4.3 %collective-permute-done.14 = f32[8,1,256]{2,1,0:T(1,128)S(1)} collective-permute-done((f32[8,1,256]{2,1,0:T(1,128)S(1)}, f32[8,1,256]{2,1,0:T(1,128)S(1)}, u32[]{:S(2)}, u32[]{:S(2)}) %collective-permute-start.14) | collective-permute-done | bytes 8224 | tf_op jit(solution)/shard_map/ppermute | solution.py:148
  130.4 0.2 fusion.6
  130.6 0.1 fusion.59
  130.7 0.1 slice.326
  130.8 0.2 fusion.15
  131.0 0.1 fusion.72
  131.1 1.3 collective-permute-start.16
  132.4 5.5 %collective-permute-start.19 = (f32[8,8,1]{2,1,0:T(8,128)S(1)}, f32[8,8,1]{2,1,0:T(8,128)S(1)}, u32[]{:S(2)}, u32[]{:S(2)}) collective-permute-start(f32[8,8,1]{2,1,0:T(8,128)S(1)} %get-tuple-element.34), channel_id=1, source_target_pairs={{64,0},{65,1},{66,2},{67,3},{68,4},{69,5},{70,6},{71,7},{72,8},{73... | collective-permute-start | bytes 776 | tf_op jit(solution)/shard_map/ppermute | solution.py:148
  137.9 2.5 %collective-permute-start.17 = (f32[8,1,256]{2,1,0:T(1,128)S(1)}, f32[8,1,256]{2,1,0:T(1,128)S(1)}, u32[]{:S(2)}, u32[]{:S(2)}) collective-permute-start(f32[8,1,256]{2,1,0:T(1,128)S(1)} %get-tuple-element.35), channel_id=1, source_target_pairs={{0,1},{1,2},{2,3},{3,4},{4,5},{5,6},{6,7},{7,8},{8,9},{9,10},{10,1... | collective-permute-start | bytes 24584 | tf_op jit(solution)/shard_map/ppermute | solution.py:147
  140.4 1.9 %collective-permute-start.18 = (f32[8,1,256]{2,1,0:T(1,128)S(1)}, f32[8,1,256]{2,1,0:T(1,128)S(1)}, u32[]{:S(2)}, u32[]{:S(2)}) collective-permute-start(f32[8,1,256]{2,1,0:T(1,128)S(1)} %get-tuple-element.36), channel_id=1, source_target_pairs={{1,0},{2,1},{3,2},{4,3},{5,4},{6,5},{7,6},{8,7},{9,8},{10,9},{11,1... | collective-permute-start | bytes 24584 | tf_op jit(solution)/shard_map/ppermute | solution.py:148
  142.4 0.0 collective-permute-done.16
  142.4 0.0 collective-permute-done.19
  142.4 5.1 %collective-permute-done.18 = f32[8,1,256]{2,1,0:T(1,128)S(1)} collective-permute-done((f32[8,1,256]{2,1,0:T(1,128)S(1)}, f32[8,1,256]{2,1,0:T(1,128)S(1)}, u32[]{:S(2)}, u32[]{:S(2)}) %collective-permute-start.18) | collective-permute-done | bytes 8224 | tf_op jit(solution)/shard_map/ppermute | solution.py:148
  147.5 0.2 fusion.9
  147.7 0.1 fusion.60
  147.8 0.1 slice.340
  147.9 0.9 fusion.18
  (44 shorter events, 0.2 us)
Async XLA Ops:
  0.6 16.7 %copy-start.10 = (s32[8,256]{1,0:T(8,128)S(1)}, s32[8,256]{1,0:T(8,128)}, u32[]{:S(2)}) copy-start(s32[8,256]{1,0:T(8,128)} %param.12) | copy-start | bytes 24580
  0.6 16.7 %copy-start.12 = (f32[12]{0:T(128)S(1)}, f32[12]{0:T(128)}, u32[]{:S(2)}) copy-start(f32[12]{0:T(128)} %param.14) | copy-start | bytes 148
  0.7 16.7 %copy-start.13 = (f32[12]{0:T(128)S(1)}, f32[12]{0:T(128)}, u32[]{:S(2)}) copy-start(f32[12]{0:T(128)} %param.15) | copy-start | bytes 148
  0.7 16.8 %copy-start.2 = (f32[8,8,256]{2,1,0:T(8,128)S(1)}, f32[8,8,256]{2,1,0:T(8,128)}, u32[]{:S(2)}) copy-start(f32[8,8,256]{2,1,0:T(8,128)} %param.10) | copy-start | bytes 196612
  10.7 35.9 %collective-permute-start = (f32[18,60,128]{2,1,0:T(8,128)}, f32[18,60,128]{2,1,0:T(8,128)S(1)}, u32[]{:S(2)}, u32[]{:S(2)}) collective-permute-start(f32[18,60,128]{2,1,0:T(8,128)} %get-tuple-element.10), channel_id=1, source_target_pairs={{0,2},{2,4},{4,6},{6,8},{8,10},{10,12},{12,14},{14,16},{16,18},{18... | collective-permute-start | bytes 1658888 | tf_op jit(solution)/shard_map/ppermute | solution.py:147
  14.1 32.4 %collective-permute-start.1 = (f32[18,60,128]{2,1,0:T(8,128)}, f32[18,60,128]{2,1,0:T(8,128)S(1)}, u32[]{:S(2)}, u32[]{:S(2)}) collective-permute-start(f32[18,60,128]{2,1,0:T(8,128)} %get-tuple-element.11), channel_id=1, source_target_pairs={{2,0},{4,2},{6,4},{8,6},{10,8},{12,10},{14,12},{16,14},{18,16},{20... | collective-permute-start | bytes 1658888 | tf_op jit(solution)/shard_map/ppermute | solution.py:148
  16.0 25.2 %collective-permute-start.2 = (f32[18,16,128]{2,1,0:T(8,128)}, f32[18,16,128]{2,1,0:T(8,128)S(1)}, u32[]{:S(2)}, u32[]{:S(2)}) collective-permute-start(f32[18,16,128]{2,1,0:T(8,128)} %get-tuple-element.12), channel_id=1, source_target_pairs={{0,1},{1,64},{64,65},{2,3},{3,66},{66,67},{4,5},{5,68},{68,69},{6,... | collective-permute-start | bytes 442376 | tf_op jit(solution)/shard_map/ppermute | solution.py:147
  17.6 19.9 %collective-permute-start.8 = (f32[10,8,1]{2,1,0:T(8,128)S(1)}, f32[10,8,1]{2,1,0:T(8,128)S(1)}, u32[]{:S(2)}, u32[]{:S(2)}) collective-permute-start(f32[10,8,1]{2,1,0:T(8,128)S(1)} %get-tuple-element.29), channel_id=1, source_target_pairs={{0,64},{1,65},{2,66},{3,67},{4,68},{5,69},{6,70},{7,71},{8,72},{9,... | collective-permute-start | bytes 968 | tf_op jit(solution)/shard_map/ppermute | solution.py:147
  18.9 19.9 %collective-permute-start.11 = (f32[10,8,1]{2,1,0:T(8,128)S(1)}, f32[10,8,1]{2,1,0:T(8,128)S(1)}, u32[]{:S(2)}, u32[]{:S(2)}) collective-permute-start(f32[10,8,1]{2,1,0:T(8,128)S(1)} %get-tuple-element.30), channel_id=1, source_target_pairs={{64,0},{65,1},{66,2},{67,3},{68,4},{69,5},{70,6},{71,7},{72,8},{73... | collective-permute-start | bytes 968 | tf_op jit(solution)/shard_map/ppermute | solution.py:148
  37.4 9.1 %collective-permute-start.3 = (f32[18,16,128]{2,1,0:T(8,128)}, f32[18,16,128]{2,1,0:T(8,128)S(1)}, u32[]{:S(2)}, u32[]{:S(2)}) collective-permute-start(f32[18,16,128]{2,1,0:T(8,128)} %get-tuple-element.13), channel_id=1, source_target_pairs={{1,0},{64,1},{65,64},{3,2},{66,3},{67,66},{5,4},{68,5},{69,68},{7,... | collective-permute-start | bytes 442376 | tf_op jit(solution)/shard_map/ppermute | solution.py:148
  38.7 39.5 %collective-permute-start.10 = (f32[10,1,256]{2,1,0:T(1,128)S(1)}, f32[10,1,256]{2,1,0:T(1,128)S(1)}, u32[]{:S(2)}, u32[]{:S(2)}) collective-permute-start(f32[10,1,256]{2,1,0:T(1,128)S(1)} %get-tuple-element.28), channel_id=1, source_target_pairs={{1,0},{2,1},{3,2},{4,3},{5,4},{6,5},{7,6},{8,7},{9,8},{10,9},{11,1... | collective-permute-start | bytes 30728 | tf_op jit(solution)/shard_map/ppermute | solution.py:148
  41.2 5.3 %copy-start.3 = (f32[18,16,128]{2,1,0:T(8,128)}, f32[18,16,128]{2,1,0:T(8,128)S(1)}, u32[]{:S(2)}) copy-start(f32[18,16,128]{2,1,0:T(8,128)S(1)} %collective-permute-done.2.fleft_ref.wleft_ref) | copy-start | bytes 442372
  41.2 37.0 %collective-permute-start.9 = (f32[10,1,256]{2,1,0:T(1,128)S(1)}, f32[10,1,256]{2,1,0:T(1,128)S(1)}, u32[]{:S(2)}, u32[]{:S(2)}) collective-permute-start(f32[10,1,256]{2,1,0:T(1,128)S(1)} %get-tuple-element.27), channel_id=1, source_target_pairs={{0,1},{1,2},{2,3},{3,4},{4,5},{5,6},{6,7},{7,8},{8,9},{9,10},{10,1... | collective-permute-start | bytes 30728 | tf_op jit(solution)/shard_map/ppermute | solution.py:147
  46.5 0.6 copy-start.4
  46.5 0.9 copy-start
  47.4 0.8 copy-start.1
  72.9 13.7 %collective-permute-start.4 = (f32[16,60,128]{2,1,0:T(8,128)}, f32[16,60,128]{2,1,0:T(8,128)S(1)}, u32[]{:S(2)}, u32[]{:S(2)}) collective-permute-start(f32[16,60,128]{2,1,0:T(8,128)} %get-tuple-element.14), channel_id=1, source_target_pairs={{0,2},{2,4},{4,6},{6,8},{8,10},{10,12},{12,14},{14,16},{16,18},{18... | collective-permute-start | bytes 1474568 | tf_op jit(solution)/shard_map/ppermute | solution.py:147
  74.8 17.3 %collective-permute-start.5 = (f32[16,60,128]{2,1,0:T(8,128)}, f32[16,60,128]{2,1,0:T(8,128)S(1)}, u32[]{:S(2)}, u32[]{:S(2)}) collective-permute-start(f32[16,60,128]{2,1,0:T(8,128)} %get-tuple-element.15), channel_id=1, source_target_pairs={{2,0},{4,2},{6,4},{8,6},{10,8},{12,10},{14,12},{16,14},{18,16},{20... | collective-permute-start | bytes 1474568 | tf_op jit(solution)/shard_map/ppermute | solution.py:148
  78.6 4.5 %collective-permute-start.6 = (f32[16,16,128]{2,1,0:T(8,128)}, f32[16,16,128]{2,1,0:T(8,128)S(1)}, u32[]{:S(2)}, u32[]{:S(2)}) collective-permute-start(f32[16,16,128]{2,1,0:T(8,128)} %get-tuple-element.16), channel_id=1, source_target_pairs={{0,1},{1,64},{64,65},{2,3},{3,66},{66,67},{4,5},{5,68},{68,69},{6,... | collective-permute-start | bytes 393224 | tf_op jit(solution)/shard_map/ppermute | solution.py:147
  79.9 4.2 %collective-permute-start.7 = (f32[16,16,128]{2,1,0:T(8,128)}, f32[16,16,128]{2,1,0:T(8,128)S(1)}, u32[]{:S(2)}, u32[]{:S(2)}) collective-permute-start(f32[16,16,128]{2,1,0:T(8,128)} %get-tuple-element.17), channel_id=1, source_target_pairs={{1,0},{64,1},{65,64},{3,2},{66,3},{67,66},{5,4},{68,5},{69,68},{7,... | collective-permute-start | bytes 393224 | tf_op jit(solution)/shard_map/ppermute | solution.py:148
  83.1 31.0 %copy-start.11 = (s32[8,256]{1,0:T(8,128)S(1)}, s32[8,256]{1,0:T(8,128)}, u32[]{:S(2)}) copy-start(s32[8,256]{1,0:T(8,128)} %param.13) | copy-start | bytes 24580
  83.1 31.0 %copy-start.5 = (f32[8,8,256]{2,1,0:T(8,128)S(1)}, f32[8,8,256]{2,1,0:T(8,128)}, u32[]{:S(2)}) copy-start(f32[8,8,256]{2,1,0:T(8,128)} %param.11) | copy-start | bytes 196612
  83.1 9.0 %copy-start.8 = (f32[16,16,128]{2,1,0:T(8,128)}, f32[16,16,128]{2,1,0:T(8,128)S(1)}, u32[]{:S(2)}) copy-start(f32[16,16,128]{2,1,0:T(8,128)S(1)} %collective-permute-done.6.fleft_ref) | copy-start | bytes 393220
  84.1 8.0 %copy-start.9 = (f32[16,16,128]{2,1,0:T(8,128)}, f32[16,16,128]{2,1,0:T(8,128)S(1)}, u32[]{:S(2)}) copy-start(f32[16,16,128]{2,1,0:T(8,128)S(1)} %collective-permute-done.7.fright_ref) | copy-start | bytes 393220
  86.6 5.5 %copy-start.6 = (f32[16,60,128]{2,1,0:T(8,128)}, f32[16,60,128]{2,1,0:T(8,128)S(1)}, u32[]{:S(2)}) copy-start(f32[16,60,128]{2,1,0:T(8,128)S(1)} %collective-permute-done.4.ftop_ref) | copy-start | bytes 1474564
  92.2 0.8 copy-start.7
  114.4 11.6 %collective-permute-start.12 = (f32[8,8,1]{2,1,0:T(8,128)S(1)}, f32[8,8,1]{2,1,0:T(8,128)S(1)}, u32[]{:S(2)}, u32[]{:S(2)}) collective-permute-start(f32[8,8,1]{2,1,0:T(8,128)S(1)} %get-tuple-element.39), channel_id=1, source_target_pairs={{0,64},{1,65},{2,66},{3,67},{4,68},{5,69},{6,70},{7,71},{8,72},{9,... | collective-permute-start | bytes 776 | tf_op jit(solution)/shard_map/ppermute | solution.py:147
  115.7 10.3 %collective-permute-start.15 = (f32[8,8,1]{2,1,0:T(8,128)S(1)}, f32[8,8,1]{2,1,0:T(8,128)S(1)}, u32[]{:S(2)}, u32[]{:S(2)}) collective-permute-start(f32[8,8,1]{2,1,0:T(8,128)S(1)} %get-tuple-element.40), channel_id=1, source_target_pairs={{64,0},{65,1},{66,2},{67,3},{68,4},{69,5},{70,6},{71,7},{72,8},{73... | collective-permute-start | bytes 776 | tf_op jit(solution)/shard_map/ppermute | solution.py:148
  121.2 4.8 %collective-permute-start.13 = (f32[8,1,256]{2,1,0:T(1,128)S(1)}, f32[8,1,256]{2,1,0:T(1,128)S(1)}, u32[]{:S(2)}, u32[]{:S(2)}) collective-permute-start(f32[8,1,256]{2,1,0:T(1,128)S(1)} %get-tuple-element.41), channel_id=1, source_target_pairs={{0,1},{1,2},{2,3},{3,4},{4,5},{5,6},{6,7},{7,8},{8,9},{9,10},{10,1... | collective-permute-start | bytes 24584 | tf_op jit(solution)/shard_map/ppermute | solution.py:147
  123.3 7.1 %collective-permute-start.14 = (f32[8,1,256]{2,1,0:T(1,128)S(1)}, f32[8,1,256]{2,1,0:T(1,128)S(1)}, u32[]{:S(2)}, u32[]{:S(2)}) collective-permute-start(f32[8,1,256]{2,1,0:T(1,128)S(1)} %get-tuple-element.42), channel_id=1, source_target_pairs={{1,0},{2,1},{3,2},{4,3},{5,4},{6,5},{7,6},{8,7},{9,8},{10,9},{11,1... | collective-permute-start | bytes 24584 | tf_op jit(solution)/shard_map/ppermute | solution.py:148
  131.1 11.3 %collective-permute-start.16 = (f32[8,8,1]{2,1,0:T(8,128)S(1)}, f32[8,8,1]{2,1,0:T(8,128)S(1)}, u32[]{:S(2)}, u32[]{:S(2)}) collective-permute-start(f32[8,8,1]{2,1,0:T(8,128)S(1)} %get-tuple-element.33), channel_id=1, source_target_pairs={{0,64},{1,65},{2,66},{3,67},{4,68},{5,69},{6,70},{7,71},{8,72},{9,... | collective-permute-start | bytes 776 | tf_op jit(solution)/shard_map/ppermute | solution.py:147
  132.4 10.0 %collective-permute-start.19 = (f32[8,8,1]{2,1,0:T(8,128)S(1)}, f32[8,8,1]{2,1,0:T(8,128)S(1)}, u32[]{:S(2)}, u32[]{:S(2)}) collective-permute-start(f32[8,8,1]{2,1,0:T(8,128)S(1)} %get-tuple-element.34), channel_id=1, source_target_pairs={{64,0},{65,1},{66,2},{67,3},{68,4},{69,5},{70,6},{71,7},{72,8},{73... | collective-permute-start | bytes 776 | tf_op jit(solution)/shard_map/ppermute | solution.py:148
  137.9 4.5 %collective-permute-start.17 = (f32[8,1,256]{2,1,0:T(1,128)S(1)}, f32[8,1,256]{2,1,0:T(1,128)S(1)}, u32[]{:S(2)}, u32[]{:S(2)}) collective-permute-start(f32[8,1,256]{2,1,0:T(1,128)S(1)} %get-tuple-element.35), channel_id=1, source_target_pairs={{0,1},{1,2},{2,3},{3,4},{4,5},{5,6},{6,7},{7,8},{8,9},{9,10},{10,1... | collective-permute-start | bytes 24584 | tf_op jit(solution)/shard_map/ppermute | solution.py:147
  140.4 7.1 %collective-permute-start.18 = (f32[8,1,256]{2,1,0:T(1,128)S(1)}, f32[8,1,256]{2,1,0:T(1,128)S(1)}, u32[]{:S(2)}, u32[]{:S(2)}) collective-permute-start(f32[8,1,256]{2,1,0:T(1,128)S(1)} %get-tuple-element.36), channel_id=1, source_target_pairs={{1,0},{2,1},{3,2},{4,3},{5,4},{6,5},{7,6},{8,7},{9,8},{10,9},{11,1... | collective-permute-start | bytes 24584 | tf_op jit(solution)/shard_map/ppermute | solution.py:148

commit v2 on v1

--- a/solution.py
+++ b/solution.py
@@ -52,16 +52,17 @@
                 edge_body(w_ref, b, *outs)
 
 
-def edges(f, w=None):
+def edges(f, start, count, w=None):
     n, nlev, rows, cols = f.shape
     nb = 2
-    nmain = n // nb
-    total = n + (0 if w is None else w.shape[0])
+    nmain = count // nb
+    off = start // nb
+    total = count + (0 if w is None else w.shape[0])
     row_shape = jax.ShapeDtypeStruct((total, nlev, cols), f.dtype)
     col_shape = jax.ShapeDtypeStruct((total, rows, cols), f.dtype)
     rspec = pl.BlockSpec((nb, nlev, cols), lambda i: (i, 0, 0))
     cspec = pl.BlockSpec((nb, rows, cols), lambda i: (i, 0, 0))
-    in_specs = [pl.BlockSpec((nb, nlev, rows, cols), lambda i: (jnp.minimum(i, nmain - 1), 0, 0, 0))]
+    in_specs = [pl.BlockSpec((nb, nlev, rows, cols), lambda i: (off + jnp.minimum(i, nmain - 1), 0, 0, 0))]
     args = [f]
     if w is not None:
         in_specs.append(pl.BlockSpec(w.shape, lambda i: (0, 0, 0, 0)))
@@ -77,9 +78,13 @@
     )(*args)
 
 
-def step_kernel(f_ref, w_ref, ftop_ref, fbot_ref, wtop_ref, wbot_ref,
-                fleft_ref, fright_ref, wleft_ref, wright_ref, o_ref):
+def step_kernel(emit, f_ref, w_ref, ftop_ref, fbot_ref, wtop_ref, wbot_ref,
+                fleft_ref, fright_ref, wleft_ref, wright_ref, *refs):
     nb, nlev, rows, cols = f_ref.shape
+    if emit:
+        o_ref, rf_ref, rl_ref, cf_ref, cl_ref = refs
+    else:
+        o_ref = refs[-1]
     row = lax.broadcasted_iota(jnp.int32, (rows, cols), 0)
     lane = lax.broadcasted_iota(jnp.int32, (rows, cols), 1)
     first_row = row == 0
@@ -91,9 +96,11 @@
         return pltpu.roll(x, (cols - lev) % cols, 1) if lev else x
 
     def to_last(x, lev):
-        s = (cols - 1 - lev) % cols
-        return pltpu.roll(x, s, 1) if s else x
-
+        sh = (cols - 1 - lev) % cols
+        return pltpu.roll(x, sh, 1) if sh else x
+
+    acc_f = [jnp.zeros((rows, cols), jnp.float32) for _ in range(nb)]
+    acc_l = [jnp.zeros((rows, cols), jnp.float32) for _ in range(nb)]
     for lev in range(nlev):
         u = w_ref[0, lev]
         v = w_ref[1, lev]
@@ -109,6 +116,7 @@
         mv = jnp.minimum(v, 0.0)
         pv_prev = jnp.maximum(v_prev, 0.0)
         mv_next = jnp.minimum(v_next, 0.0)
+        at_lev = lane == lev
         for b in range(nb):
             q = f_ref[b, lev]
             q_prev = jnp.where(first_row, ftop_ref[b, pl.ds(lev, 1), :], pltpu.roll(q, 1, 0))
@@ -119,27 +127,66 @@
             fxm = pu_prev * q_prev + mu * q
             fyp = pv * q + mv_next * q_e
             fym = pv_prev * q_w + mv * q
-            o_ref[b, lev] = q - (fxp - fxm) - (fyp - fym)
-
-
-def advect_step(f, w, ftop, fbot, wtop, wbot, fleft, fright, wleft, wright):
+            new = q - (fxp - fxm) - (fyp - fym)
+            o_ref[b, lev] = new
+            if emit:
+                rf_ref[b, pl.ds(lev, 1), :] = new[0:1, :]
+                rl_ref[b, pl.ds(lev, 1), :] = new[rows - 1:rows, :]
+                acc_f[b] = jnp.where(at_lev, pltpu.roll(new, lev, 1) if lev else new, acc_f[b])
+                acc_l[b] = jnp.where(at_lev, pltpu.roll(new, (lev + 1) % cols, 1), acc_l[b])
+    if emit:
+        for b in range(nb):
+            cf_ref[b] = acc_f[b]
+            cl_ref[b] = acc_l[b]
+
+
+def advect_step(f, f_off, count, w, ftop, fbot, wtop, wbot, fleft, fright, wleft, wright,
+                emit, into=None, o_off=0, out_total=None):
     nsp, nlev, rows, cols = f.shape
-    main = pl.BlockSpec((SB, nlev, rows, cols), lambda i: (i, 0, 0, 0))
+    fo = f_off // SB
+    oo = o_off // SB
+    src = pl.BlockSpec((SB, nlev, rows, cols), lambda i: (fo + i, 0, 0, 0))
     rowspec = pl.BlockSpec((SB, nlev, cols), lambda i: (i, 0, 0))
     colspec = pl.BlockSpec((SB, rows, cols), lambda i: (i, 0, 0))
-    wblock = nsp // 2
-    wrowspec = pl.BlockSpec((2, nlev, cols), lambda i: (wblock, 0, 0))
-    wcolspec = pl.BlockSpec((2, rows, cols), lambda i: (wblock, 0, 0))
-    nbytes = 4 * (2 * f.size + w.size)
+    wrowspec = pl.BlockSpec((2, nlev, cols), lambda i: (wtop.shape[0] // 2 - 1, 0, 0))
+    wcolspec = pl.BlockSpec((2, rows, cols), lambda i: (wleft.shape[0] // 2 - 1, 0, 0))
+    in_specs = [src, pl.BlockSpec(w.shape, lambda i: (0, 0, 0, 0)), rowspec, rowspec, wrowspec, wrowspec,
+                colspec, colspec, wcolspec, wcolspec]
+    args = [f, w, ftop, fbot, wtop, wbot, fleft, fright, wleft, wright]
+    aliases = {}
+    if emit:
+        out_shape = [jax.ShapeDtypeStruct((count, nlev, rows, cols), f.dtype),
+                     jax.ShapeDtypeStruct((count, nlev, cols), f.dtype),
+                     jax.ShapeDtypeStruct((count, nlev, cols), f.dtype),
+                     jax.ShapeDtypeStruct((count, rows, cols), f.dtype),
+                     jax.ShapeDtypeStruct((count, rows, cols), f.dtype)]
+        out_specs = [pl.BlockSpec((SB, nlev, rows, cols), lambda i: (i, 0, 0, 0)), rowspec, rowspec,
+                     colspec, colspec]
+    else:
+        total = out_total if into is None else into.shape[0]
+        out_shape = jax.ShapeDtypeStruct((total, nlev, rows, cols), f.dtype)
+        out_specs = pl.BlockSpec((SB, nlev, rows, cols), lambda i: (oo + i, 0, 0, 0))
+        if into is not None:
+            in_specs.append(pl.BlockSpec(memory_space=pl.ANY))
+            args.append(into)
+            aliases = {len(args) - 1: 0}
+    nbytes = 4 * (2 * count * nlev * rows * cols + w.size)
+
+    def kernel(*refs):
+        if into is not None:
+            refs = refs[:10] + refs[11:]
+        step_kernel(emit, *refs)
+
     return pl.pallas_call(
-        step_kernel,
-        grid=(nsp // SB,),
-        in_specs=[main, pl.BlockSpec(w.shape, lambda i: (0, 0, 0, 0)), rowspec, rowspec, wrowspec, wrowspec,
-                  colspec, colspec, wcolspec, wcolspec],
-        out_specs=main,
-        out_shape=jax.ShapeDtypeStruct(f.shape, f.dtype),
-        cost_estimate=pl.CostEstimate(flops=20 * f.size, bytes_accessed=nbytes, transcendentals=0),
-    )(f, w, ftop, fbot, wtop, wbot, fleft, fright, wleft, wright)
+        kernel,
+        grid=(count // SB,),
+        in_specs=in_specs,
+        out_specs=out_specs,
+        out_shape=out_shape,
+        input_output_aliases=aliases,
+        cost_estimate=pl.CostEstimate(flops=20 * count * nlev * rows * cols, bytes_accessed=nbytes,
+                                      transcendentals=0),
+    )(*args)
 
 
 def exchange(first, last, axes):
@@ -151,14 +198,29 @@
 
 def advection(tracers, wind_courant):
     cols_axes = ("mp", "gy")
-    rf, rl, cf, cl = edges(tracers, wind_courant)
-    top, bot = exchange(rf, rl, "gx")
-    left, right = exchange(cf, cl, cols_axes)
-    mid = advect_step(tracers, wind_courant, top, bot, top, bot, left, right, left, right)
-    srf, srl, scf, scl = edges(mid)
-    stop, sbot = exchange(srf, srl, "gx")
-    sleft, sright = exchange(scf, scl, cols_axes)
-    return advect_step(mid, wind_courant, stop, sbot, top, bot, sleft, sright, left, right)
+    nsp = tracers.shape[0]
+    half = nsp // 2
+    phase1 = []
+    for c in range(2):
+        rf, rl, cf, cl = edges(tracers, c * half, half, wind_courant if c == 0 else None)
+        top, bot = exchange(rf, rl, "gx")
+        left, right = exchange(cf, cl, cols_axes)
+        phase1.append((top, bot, left, right))
+    wtop, wbot, wleft, wright = phase1[0]
+    phase2 = []
+    for c in range(2):
+        top, bot, left, right = phase1[c]
+        mid, rf, rl, cf, cl = advect_step(tracers, c * half, half, wind_courant, top, bot, wtop, wbot,
+                                          left, right, wleft, wright, True)
+        stop, sbot = exchange(rf, rl, "gx")
+        sleft, sright = exchange(cf, cl, cols_axes)
+        phase2.append((mid, stop, sbot, sleft, sright))
+    out = None
+    for c in range(2):
+        mid, stop, sbot, sleft, sright = phase2[c]
+        out = advect_step(mid, 0, half, wind_courant, stop, sbot, wtop, wbot, sleft, sright, wleft, wright,
+                          False, into=out, o_off=c * half, out_total=nsp)
+    return out
 
 
 def padded_2(block, sides, width):

time: 150 us -> 249 us (1.66)
  the two profiles are of different devices: /device:TPU:31 before, /device:TPU:119 now
where the time goes in v2:
time: 249 us; the launch traced here: 248 us
  Pallas kernels  115 us (46%)
  starting transfers between devices  99.2 us (40%)
  waiting for transfers between devices  19.6 us (8%)
  blocking collectives  6.64 us (3%)
  other arithmetic  3.25 us (1%)
  local copies, waits for them, and re-layouts  2.8 us (1%)
    pallas_call x4, Pallas kernels, advect_step(): pl.pallas_call(kernel, grid=(count // SB,), in_specs=in_specs, out_specs=...  103 us
    ppermute x14, starting transfers between devices, exchange(): before = lax.ppermute(last, axes, shift_pairs(n, 1))  57.6 us
    ppermute x14, starting transfers between devices, exchange(): after = lax.ppermute(first, axes, shift_pairs(n, -1))  41.6 us
    ppermute x14, waiting for transfers between devices, exchange(): after = lax.ppermute(first, axes, shift_pairs(n, -1))  14.4 us
    pallas_call x2, Pallas kernels, edges(): pl.pallas_call(functools.partial(edge_kernel, nmain), grid=(total // nb,)...  11.2 us
    all_to_all x1, blocking collectives, on_device(): lax.all_to_all(forcing_fields(advected), 'gy', split_axis=1, concat_axis=...  6.64 us
    ppermute x14, waiting for transfers between devices, exchange(): before = lax.ppermute(last, axes, shift_pairs(n, 1))  5.26 us
  transfers between devices with their start and end apart: 28, of which 3 were waited for; matrix products, arithmetic and copies ran while one was open for 0% of the time, Pallas kernels for 40%

profile of v2, /device:TPU:119, one launch (start us, length us, event | category | flops | bytes accessed | tf_op | source)
XLA Modules:
  0.0 247.7 jit_solution(9394372543266953419)
XLA Ops:
  0.7 6.1 %shard_map.96 = (f32[10,60,128]{2,1,0:T(8,128)}, f32[10,60,128]{2,1,0:T(8,128)}, f32[10,16,128]{2,1,0:T(8,128)}, f32[10,16,128]{2,1,0:T(8,128)}) custom-call(f32[16,60,16,128]{3,2,1,0:T(8,128)} %refs_0_.5, f32[2,60,16,128]{3,2,1,0:T(8,128)} %refs_1_.7), custom_call_target="tpu_custom_call" | custom-call | flops 4915200 | bytes 4915200 | tf_op jit(solution)/shard_map/pallas_call | solution.py:70
  6.7 1.9 collective-permute-start.2
  8.7 3.4 %collective-permute-start.3 = (f32[10,60,128]{2,1,0:T(8,128)}, f32[10,60,128]{2,1,0:T(8,128)S(1)}, u32[]{:S(2)}, u32[]{:S(2)}) collective-permute-start(f32[10,60,128]{2,1,0:T(8,128)} %get-tuple-element.23), channel_id=1, source_target_pairs={{2,0},{4,2},{6,4},{8,6},{10,8},{12,10},{14,12},{16,14},{18,16},{20... | collective-permute-start | bytes 921608 | tf_op jit(solution)/shard_map/ppermute | solution.py:195
  12.0 1.3 collective-permute-start.6
  13.3 3.8 %collective-permute-start.7 = (f32[10,16,128]{2,1,0:T(8,128)}, f32[10,16,128]{2,1,0:T(8,128)S(1)}, u32[]{:S(2)}, u32[]{:S(2)}) collective-permute-start(f32[10,16,128]{2,1,0:T(8,128)} %get-tuple-element.27), channel_id=1, source_target_pairs={{1,0},{64,1},{65,64},{3,2},{66,3},{67,66},{5,4},{68,5},{69,68},{7,... | collective-permute-start | bytes 245768 | tf_op jit(solution)/shard_map/ppermute | solution.py:195
  17.1 0.1 select_reduce_fusion.1
  17.3 0.1 fusion.70
  17.3 1.3 collective-permute-start.16
  18.7 5.2 %collective-permute-done.16 = f32[10,8,1]{2,1,0:T(8,128)S(1)} collective-permute-done((f32[10,8,1]{2,1,0:T(8,128)S(1)}, f32[10,8,1]{2,1,0:T(8,128)S(1)}, u32[]{:S(2)}, u32[]{:S(2)}) %collective-permute-start.16) | collective-permute-done | bytes 352 | tf_op jit(solution)/shard_map/ppermute | solution.py:194
  23.9 1.3 collective-permute-start.19
  25.2 5.1 %shard_map.95 = (f32[8,60,128]{2,1,0:T(8,128)}, f32[8,60,128]{2,1,0:T(8,128)}, f32[8,16,128]{2,1,0:T(8,128)}, f32[8,16,128]{2,1,0:T(8,128)}) custom-call(f32[16,60,16,128]{3,2,1,0:T(8,128)} %refs_0_.5), custom_call_target="tpu_custom_call" | custom-call | flops 3932160 | bytes 3932160 | tf_op jit(solution)/shard_map/pallas_call | solution.py:70
  30.3 6.0 %collective-permute-start = (f32[8,60,128]{2,1,0:T(8,128)}, f32[8,60,128]{2,1,0:T(8,128)S(1)}, u32[]{:S(2)}, u32[]{:S(2)}) collective-permute-start(f32[8,60,128]{2,1,0:T(8,128)} %get-tuple-element.20), channel_id=1, source_target_pairs={{0,2},{2,4},{4,6},{6,8},{8,10},{10,12},{12,14},{14,16},{16,18},{18... | collective-permute-start | bytes 737288 | tf_op jit(solution)/shard_map/ppermute | solution.py:194
  36.3 1.9 collective-permute-start.1
  38.3 1.3 collective-permute-start.4
  39.6 13.0 %collective-permute-start.17 = (f32[10,1,256]{2,1,0:T(1,128)S(1)}, f32[10,1,256]{2,1,0:T(1,128)S(1)}, u32[]{:S(2)}, u32[]{:S(2)}) collective-permute-start(f32[10,1,256]{2,1,0:T(1,128)S(1)} %get-tuple-element.47), channel_id=1, source_target_pairs={{0,1},{1,2},{2,3},{3,4},{4,5},{5,6},{6,7},{7,8},{8,9},{9,10},{10,1... | collective-permute-start | bytes 30728 | tf_op jit(solution)/shard_map/ppermute | solution.py:194
  52.7 1.9 collective-permute-start.18
  54.7 42.7 %shard_map.98 = (f32[8,60,16,128]{3,2,1,0:T(8,128)}, f32[8,60,128]{2,1,0:T(8,128)}, f32[8,60,128]{2,1,0:T(8,128)}, f32[8,16,128]{2,1,0:T(8,128)}, f32[8,16,128]{2,1,0:T(8,128)}) custom-call(f32[16,60,16,128]{3,2,1,0:T(8,128)} %refs_0_.5, f32[2,60,16,128]{3,2,1,0:T(8,128)} %refs_1_.7, f32[10,60,128]{2,1,0:T(8,128)} %copy-done, f32[10,60,128]{2,1,0:T(8,128)} %copy-done.1, ...), custom_call_target="tpu_custom_call" | custom-call | flops 19660800 | bytes 8847360 | tf_op jit(solution)/shard_map/pallas_call | solution.py:180
  97.4 1.3 collective-permute-start.5
  98.7 8.6 %collective-permute-start.12 = (f32[8,60,128]{2,1,0:T(8,128)}, f32[8,60,128]{2,1,0:T(8,128)S(1)}, u32[]{:S(2)}, u32[]{:S(2)}) collective-permute-start(f32[8,60,128]{2,1,0:T(8,128)} %get-tuple-element.34), channel_id=1, source_target_pairs={{0,2},{2,4},{4,6},{6,8},{8,10},{10,12},{12,14},{14,16},{16,18},{18... | collective-permute-start | bytes 737288 | tf_op jit(solution)/shard_map/ppermute | solution.py:194
  107.3 1.3 collective-permute-start.14
  108.6 0.1 maximum_bitcast_fusion.1
  108.7 1.9 collective-permute-start.13
  110.7 0.0 copy-start.10
  110.7 3.0 %collective-permute-start.15 = (f32[8,16,128]{2,1,0:T(8,128)}, f32[8,16,128]{2,1,0:T(8,128)S(1)}, u32[]{:S(2)}, u32[]{:S(2)}) collective-permute-start(f32[8,16,128]{2,1,0:T(8,128)} %get-tuple-element.37), channel_id=1, source_target_pairs={{1,0},{64,1},{65,64},{3,2},{66,3},{67,66},{5,4},{68,5},{69,68},{7,... | collective-permute-start | bytes 196616 | tf_op jit(solution)/shard_map/ppermute | solution.py:195
  113.8 0.7 copy-done.11
  114.5 42.6 %shard_map.97 = (f32[8,60,16,128]{3,2,1,0:T(8,128)}, f32[8,60,128]{2,1,0:T(8,128)}, f32[8,60,128]{2,1,0:T(8,128)}, f32[8,16,128]{2,1,0:T(8,128)}, f32[8,16,128]{2,1,0:T(8,128)}) custom-call(f32[16,60,16,128]{3,2,1,0:T(8,128)} %refs_0_.5, f32[2,60,16,128]{3,2,1,0:T(8,128)} %refs_1_.7, f32[8,60,128]{2,1,0:T(8,128)} %copy-done.10, f32[8,60,128]{2,1,0:T(8,128)} %copy-done.11, ...), custom_call_target="tpu_custom_call" | custom-call | flops 19660800 | bytes 8847360 | tf_op jit(solution)/shard_map/pallas_call | solution.py:180
  157.0 7.9 %collective-permute-start.8 = (f32[8,60,128]{2,1,0:T(8,128)}, f32[8,60,128]{2,1,0:T(8,128)S(1)}, u32[]{:S(2)}, u32[]{:S(2)}) collective-permute-start(f32[8,60,128]{2,1,0:T(8,128)} %get-tuple-element.29), channel_id=1, source_target_pairs={{0,2},{2,4},{4,6},{6,8},{8,10},{10,12},{12,14},{14,16},{16,18},{18... | collective-permute-start | bytes 737288 | tf_op jit(solution)/shard_map/ppermute | solution.py:194
  164.9 0.0 copy-start.13
  164.9 1.9 collective-permute-start.9
  166.8 0.2 fusion.3
  167.1 1.3 collective-permute-start.10
  168.4 6.4 %collective-permute-start.11 = (f32[8,16,128]{2,1,0:T(8,128)}, f32[8,16,128]{2,1,0:T(8,128)S(1)}, u32[]{:S(2)}, u32[]{:S(2)}) collective-permute-start(f32[8,16,128]{2,1,0:T(8,128)} %get-tuple-element.32), channel_id=1, source_target_pairs={{1,0},{64,1},{65,64},{3,2},{66,3},{67,66},{5,4},{68,5},{69,68},{7,... | collective-permute-start | bytes 196616 | tf_op jit(solution)/shard_map/ppermute | solution.py:195
  174.7 0.1 fusion.58
  174.9 0.1 slice.312
  175.0 0.7 copy-done.7
  175.6 9.1 %shard_map.99.refs_10_ = f32[16,60,16,128]{3,2,1,0:T(8,128)} custom-call(f32[8,60,16,128]{3,2,1,0:T(8,128)} %get-tuple-element.33.refs_0_, f32[2,60,16,128]{3,2,1,0:T(8,128)} %refs_1_.7, f32[8,60,128]{2,1,0:T(8,128)} %copy-done.6, f32[8,60,128]{2,1,0:T(8,128)} %copy-done.7, f32[10,60,128]{2,1,0:T(8,128)} %copy-done, f32[10,60,128]{2,1,0:T(8,128)} %copy-done.1, ...), custom_call_target="tpu_custom_call" | custom-call | flops 19660800 | bytes 8847360 | tf_op jit(solution)/shard_map/pallas_call | solution.py:180
  184.8 0.6 copy-done.16
  185.4 0.0 copy-done.17
  185.4 0.1 copy-done.8
  185.5 0.1 copy-done.9
  185.6 9.1 %shard_map.100 = f32[16,60,16,128]{3,2,1,0:T(8,128)} custom-call(f32[8,60,16,128]{3,2,1,0:T(8,128)} %get-tuple-element.28.refs_0_, f32[2,60,16,128]{3,2,1,0:T(8,128)} %refs_1_.7, f32[8,60,128]{2,1,0:T(8,128)} %copy-done.8, f32[8,60,128]{2,1,0:T(8,128)} %copy-done.9, f32[10,60,128]{2,1,0:T(8,128)} %copy-done, ...), custom_call_target="tpu_custom_call", output_to_operand_aliasing={{}: (10, {})} | custom-call | flops 19660800 | bytes 8847360 | tf_op jit(solution)/shard_map/pallas_call | solution.py:180
  194.7 0.8 compare_select_fusion.17
  195.5 6.6 %all_to_all.15 = f32[3,16,128]{2,0,1:T(4,128)S(1)} all-to-all(f32[3,16,128]{2,0,1:T(4,128)S(1)} %copy.13), channel_id=1, replica_groups=mesh['mp'=2,'gx'=32,'gy'=2] {'gy'}, dimensions={1} | all-to-all | bytes 49152 | tf_op jit(solution)/shard_map/all_to_all | solution.py:312
  202.2 0.2 fusion.12
  202.5 0.1 fusion.75
  202.6 1.3 collective-permute-start.20
  203.9 5.5 %collective-permute-start.23 = (f32[8,8,1]{2,1,0:T(8,128)S(1)}, f32[8,8,1]{2,1,0:T(8,128)S(1)}, u32[]{:S(2)}, u32[]{:S(2)}) collective-permute-start(f32[8,8,1]{2,1,0:T(8,128)S(1)} %get-tuple-element.60), channel_id=1, source_target_pairs={{64,0},{65,1},{66,2},{67,3},{68,4},{69,5},{70,6},{71,7},{72,8},{73... | collective-permute-start | bytes 776 | tf_op jit(solution)/shard_map/ppermute | solution.py:195
  209.4 8.7 %collective-permute-start.21 = (f32[8,1,256]{2,1,0:T(1,128)S(1)}, f32[8,1,256]{2,1,0:T(1,128)S(1)}, u32[]{:S(2)}, u32[]{:S(2)}) collective-permute-start(f32[8,1,256]{2,1,0:T(1,128)S(1)} %get-tuple-element.61), channel_id=1, source_target_pairs={{0,1},{1,2},{2,3},{3,4},{4,5},{5,6},{6,7},{7,8},{8,9},{9,10},{10,1... | collective-permute-start | bytes 24584 | tf_op jit(solution)/shard_map/ppermute | solution.py:194
  218.0 1.9 collective-permute-start.22
  220.0 7.2 %collective-permute-done.22 = f32[8,1,256]{2,1,0:T(1,128)S(1)} collective-permute-done((f32[8,1,256]{2,1,0:T(1,128)S(1)}, f32[8,1,256]{2,1,0:T(1,128)S(1)}, u32[]{:S(2)}, u32[]{:S(2)}) %collective-permute-start.22) | collective-permute-done | bytes 8224 | tf_op jit(solution)/shard_map/ppermute | solution.py:195
  227.2 0.2 fusion.6
  227.4 0.1 fusion.59
  227.5 0.1 slice.326
  227.6 0.2 fusion.15
  227.8 0.1 fusion.72
  227.9 1.3 collective-permute-start.24
  229.2 5.5 %collective-permute-start.27 = (f32[8,8,1]{2,1,0:T(8,128)S(1)}, f32[8,8,1]{2,1,0:T(8,128)S(1)}, u32[]{:S(2)}, u32[]{:S(2)}) collective-permute-start(f32[8,8,1]{2,1,0:T(8,128)S(1)} %get-tuple-element.54), channel_id=1, source_target_pairs={{64,0},{65,1},{66,2},{67,3},{68,4},{69,5},{70,6},{71,7},{72,8},{73... | collective-permute-start | bytes 776 | tf_op jit(solution)/shard_map/ppermute | solution.py:195
  234.7 2.5 %collective-permute-start.25 = (f32[8,1,256]{2,1,0:T(1,128)S(1)}, f32[8,1,256]{2,1,0:T(1,128)S(1)}, u32[]{:S(2)}, u32[]{:S(2)}) collective-permute-start(f32[8,1,256]{2,1,0:T(1,128)S(1)} %get-tuple-element.55), channel_id=1, source_target_pairs={{0,1},{1,2},{2,3},{3,4},{4,5},{5,6},{6,7},{7,8},{8,9},{9,10},{10,1... | collective-permute-start | bytes 24584 | tf_op jit(solution)/shard_map/ppermute | solution.py:194
  237.2 1.9 collective-permute-start.26
  239.3 7.2 %collective-permute-done.26 = f32[8,1,256]{2,1,0:T(1,128)S(1)} collective-permute-done((f32[8,1,256]{2,1,0:T(1,128)S(1)}, f32[8,1,256]{2,1,0:T(1,128)S(1)}, u32[]{:S(2)}, u32[]{:S(2)}) %collective-permute-start.26) | collective-permute-done | bytes 8224 | tf_op jit(solution)/shard_map/ppermute | solution.py:195
  246.4 0.2 fusion.9
  246.6 0.1 fusion.60
  246.8 0.1 slice.340
  246.8 0.9 fusion.18
  (80 shorter events, 0.3 us)
Async XLA Ops:
  0.6 16.5 %copy-start.18 = (s32[8,256]{1,0:T(8,128)S(1)}, s32[8,256]{1,0:T(8,128)}, u32[]{:S(2)}) copy-start(s32[8,256]{1,0:T(8,128)} %param.12) | copy-start | bytes 24580
  0.6 16.5 %copy-start.20 = (f32[12]{0:T(128)S(1)}, f32[12]{0:T(128)}, u32[]{:S(2)}) copy-start(f32[12]{0:T(128)} %param.14) | copy-start | bytes 148
  0.7 16.5 %copy-start.21 = (f32[12]{0:T(128)S(1)}, f32[12]{0:T(128)}, u32[]{:S(2)}) copy-start(f32[12]{0:T(128)} %param.15) | copy-start | bytes 148
  0.7 16.6 %copy-start.2 = (f32[8,8,256]{2,1,0:T(8,128)S(1)}, f32[8,8,256]{2,1,0:T(8,128)}, u32[]{:S(2)}) copy-start(f32[8,8,256]{2,1,0:T(8,128)} %param.10) | copy-start | bytes 196612
  6.7 32.8 %collective-permute-start.2 = (f32[10,60,128]{2,1,0:T(8,128)}, f32[10,60,128]{2,1,0:T(8,128)S(1)}, u32[]{:S(2)}, u32[]{:S(2)}) collective-permute-start(f32[10,60,128]{2,1,0:T(8,128)} %get-tuple-element.22), channel_id=1, source_target_pairs={{0,2},{2,4},{4,6},{6,8},{8,10},{10,12},{12,14},{14,16},{16,18},{18... | collective-permute-start | bytes 921608 | tf_op jit(solution)/shard_map/ppermute | solution.py:194
  8.7 44.0 %collective-permute-start.3 = (f32[10,60,128]{2,1,0:T(8,128)}, f32[10,60,128]{2,1,0:T(8,128)S(1)}, u32[]{:S(2)}, u32[]{:S(2)}) collective-permute-start(f32[10,60,128]{2,1,0:T(8,128)} %get-tuple-element.23), channel_id=1, source_target_pairs={{2,0},{4,2},{6,4},{8,6},{10,8},{12,10},{14,12},{16,14},{18,16},{20... | collective-permute-start | bytes 921608 | tf_op jit(solution)/shard_map/ppermute | solution.py:195
  12.0 24.3 %collective-permute-start.6 = (f32[10,16,128]{2,1,0:T(8,128)}, f32[10,16,128]{2,1,0:T(8,128)S(1)}, u32[]{:S(2)}, u32[]{:S(2)}) collective-permute-start(f32[10,16,128]{2,1,0:T(8,128)} %get-tuple-element.26), channel_id=1, source_target_pairs={{0,1},{1,64},{64,65},{2,3},{3,66},{66,67},{4,5},{5,68},{68,69},{6,... | collective-permute-start | bytes 245768 | tf_op jit(solution)/shard_map/ppermute | solution.py:194
  13.3 24.9 %collective-permute-start.7 = (f32[10,16,128]{2,1,0:T(8,128)}, f32[10,16,128]{2,1,0:T(8,128)S(1)}, u32[]{:S(2)}, u32[]{:S(2)}) collective-permute-start(f32[10,16,128]{2,1,0:T(8,128)} %get-tuple-element.27), channel_id=1, source_target_pairs={{1,0},{64,1},{65,64},{3,2},{66,3},{67,66},{5,4},{68,5},{69,68},{7,... | collective-permute-start | bytes 245768 | tf_op jit(solution)/shard_map/ppermute | solution.py:195
  17.3 6.5 %collective-permute-start.16 = (f32[10,8,1]{2,1,0:T(8,128)S(1)}, f32[10,8,1]{2,1,0:T(8,128)S(1)}, u32[]{:S(2)}, u32[]{:S(2)}) collective-permute-start(f32[10,8,1]{2,1,0:T(8,128)S(1)} %get-tuple-element.49), channel_id=1, source_target_pairs={{0,64},{1,65},{2,66},{3,67},{4,68},{5,69},{6,70},{7,71},{8,72},{9,... | collective-permute-start | bytes 968 | tf_op jit(solution)/shard_map/ppermute | solution.py:194
  23.9 6.4 %collective-permute-start.19 = (f32[10,8,1]{2,1,0:T(8,128)S(1)}, f32[10,8,1]{2,1,0:T(8,128)S(1)}, u32[]{:S(2)}, u32[]{:S(2)}) collective-permute-start(f32[10,8,1]{2,1,0:T(8,128)S(1)} %get-tuple-element.50), channel_id=1, source_target_pairs={{64,0},{65,1},{66,2},{67,3},{68,4},{69,5},{70,6},{71,7},{72,8},{73... | collective-permute-start | bytes 968 | tf_op jit(solution)/shard_map/ppermute | solution.py:195
  30.3 67.1 %copy-start.22 = (f32[8,16,128]{2,1,0:T(8,128)S(1)}, f32[8,16,128]{2,1,0:T(8,128)}, u32[]{:S(2)}) copy-start(f32[8,16,128]{2,1,0:T(8,128)} %get-tuple-element.25) | copy-start | bytes 196612
  30.3 80.3 %collective-permute-start = (f32[8,60,128]{2,1,0:T(8,128)}, f32[8,60,128]{2,1,0:T(8,128)S(1)}, u32[]{:S(2)}, u32[]{:S(2)}) collective-permute-start(f32[8,60,128]{2,1,0:T(8,128)} %get-tuple-element.20), channel_id=1, source_target_pairs={{0,2},{2,4},{4,6},{6,8},{8,10},{10,12},{12,14},{14,16},{16,18},{18... | collective-permute-start | bytes 737288 | tf_op jit(solution)/shard_map/ppermute | solution.py:194
  36.3 18.3 %copy-start.3 = (f32[10,16,128]{2,1,0:T(8,128)}, f32[10,16,128]{2,1,0:T(8,128)S(1)}, u32[]{:S(2)}) copy-start(f32[10,16,128]{2,1,0:T(8,128)S(1)} %collective-permute-done.6.refs_8_.refs_6_) | copy-start | bytes 245764
  36.3 77.4 %collective-permute-start.1 = (f32[8,60,128]{2,1,0:T(8,128)}, f32[8,60,128]{2,1,0:T(8,128)S(1)}, u32[]{:S(2)}, u32[]{:S(2)}) collective-permute-start(f32[8,60,128]{2,1,0:T(8,128)} %get-tuple-element.21), channel_id=1, source_target_pairs={{2,0},{4,2},{6,4},{8,6},{10,8},{12,10},{14,12},{16,14},{18,16},{20... | collective-permute-start | bytes 737288 | tf_op jit(solution)/shard_map/ppermute | solution.py:195
  38.3 16.4 %copy-start.4 = (f32[10,16,128]{2,1,0:T(8,128)}, f32[10,16,128]{2,1,0:T(8,128)S(1)}, u32[]{:S(2)}) copy-start(f32[10,16,128]{2,1,0:T(8,128)S(1)} %collective-permute-done.7.refs_9_.refs_7_) | copy-start | bytes 245764
  38.3 69.0 %collective-permute-start.4 = (f32[8,16,128]{2,1,0:T(8,128)}, f32[8,16,128]{2,1,0:T(8,128)S(1)}, u32[]{:S(2)}, u32[]{:S(2)}) collective-permute-start(f32[8,16,128]{2,1,0:T(8,128)} %get-tuple-element.24), channel_id=1, source_target_pairs={{0,1},{1,64},{64,65},{2,3},{3,66},{66,67},{4,5},{5,68},{68,69},{6,... | collective-permute-start | bytes 196616 | tf_op jit(solution)/shard_map/ppermute | solution.py:194
  39.6 15.1 %copy-start = (f32[10,60,128]{2,1,0:T(8,128)}, f32[10,60,128]{2,1,0:T(8,128)S(1)}, u32[]{:S(2)}) copy-start(f32[10,60,128]{2,1,0:T(8,128)S(1)} %collective-permute-done.2.refs_4_.refs_2_) | copy-start | bytes 921604
  39.6 57.8 %collective-permute-start.17 = (f32[10,1,256]{2,1,0:T(1,128)S(1)}, f32[10,1,256]{2,1,0:T(1,128)S(1)}, u32[]{:S(2)}, u32[]{:S(2)}) collective-permute-start(f32[10,1,256]{2,1,0:T(1,128)S(1)} %get-tuple-element.47), channel_id=1, source_target_pairs={{0,1},{1,2},{2,3},{3,4},{4,5},{5,6},{6,7},{7,8},{8,9},{9,10},{10,1... | collective-permute-start | bytes 30728 | tf_op jit(solution)/shard_map/ppermute | solution.py:194
  52.6 2.0 copy-start.1
  52.7 46.0 %collective-permute-start.18 = (f32[10,1,256]{2,1,0:T(1,128)S(1)}, f32[10,1,256]{2,1,0:T(1,128)S(1)}, u32[]{:S(2)}, u32[]{:S(2)}) collective-permute-start(f32[10,1,256]{2,1,0:T(1,128)S(1)} %get-tuple-element.48), channel_id=1, source_target_pairs={{1,0},{2,1},{3,2},{4,3},{5,4},{6,5},{7,6},{8,7},{9,8},{10,9},{11,1... | collective-permute-start | bytes 30728 | tf_op jit(solution)/shard_map/ppermute | solution.py:195
  97.4 11.3 %collective-permute-start.5 = (f32[8,16,128]{2,1,0:T(8,128)S(1)}, f32[8,16,128]{2,1,0:T(8,128)S(1)}, u32[]{:S(2)}, u32[]{:S(2)}) collective-permute-start(f32[8,16,128]{2,1,0:T(8,128)S(1)} %copy-done.22), channel_id=1, source_target_pairs={{1,0},{64,1},{65,64},{3,2},{66,3},{67,66},{5,4},{68,5},{69,68},{7,... | collective-permute-start | bytes 196616 | tf_op jit(solution)/shard_map/ppermute | solution.py:195
  98.7 69.7 %collective-permute-start.12 = (f32[8,60,128]{2,1,0:T(8,128)}, f32[8,60,128]{2,1,0:T(8,128)S(1)}, u32[]{:S(2)}, u32[]{:S(2)}) collective-permute-start(f32[8,60,128]{2,1,0:T(8,128)} %get-tuple-element.34), channel_id=1, source_target_pairs={{0,2},{2,4},{4,6},{6,8},{8,10},{10,12},{12,14},{14,16},{16,18},{18... | collective-permute-start | bytes 737288 | tf_op jit(solution)/shard_map/ppermute | solution.py:194
  107.3 6.4 %copy-start.12 = (f32[8,16,128]{2,1,0:T(8,128)}, f32[8,16,128]{2,1,0:T(8,128)S(1)}, u32[]{:S(2)}) copy-start(f32[8,16,128]{2,1,0:T(8,128)S(1)} %collective-permute-done.4.refs_6_) | copy-start | bytes 196612
  107.3 57.6 %collective-permute-start.14 = (f32[8,16,128]{2,1,0:T(8,128)}, f32[8,16,128]{2,1,0:T(8,128)S(1)}, u32[]{:S(2)}, u32[]{:S(2)}) collective-permute-start(f32[8,16,128]{2,1,0:T(8,128)} %get-tuple-element.36), channel_id=1, source_target_pairs={{0,1},{1,64},{64,65},{2,3},{3,66},{66,67},{4,5},{5,68},{68,69},{6,... | collective-permute-start | bytes 196616 | tf_op jit(solution)/shard_map/ppermute | solution.py:194
  108.7 5.0 %copy-start.15 = (f32[8,16,128]{2,1,0:T(8,128)}, f32[8,16,128]{2,1,0:T(8,128)S(1)}, u32[]{:S(2)}) copy-start(f32[8,16,128]{2,1,0:T(8,128)S(1)} %collective-permute-done.5.refs_7_) | copy-start | bytes 196612
  108.7 66.2 %collective-permute-start.13 = (f32[8,60,128]{2,1,0:T(8,128)}, f32[8,60,128]{2,1,0:T(8,128)S(1)}, u32[]{:S(2)}, u32[]{:S(2)}) collective-permute-start(f32[8,60,128]{2,1,0:T(8,128)} %get-tuple-element.35), channel_id=1, source_target_pairs={{2,0},{4,2},{6,4},{8,6},{10,8},{12,10},{14,12},{16,14},{18,16},{20... | collective-permute-start | bytes 737288 | tf_op jit(solution)/shard_map/ppermute | solution.py:195
  110.7 3.1 %copy-start.10 = (f32[8,60,128]{2,1,0:T(8,128)}, f32[8,60,128]{2,1,0:T(8,128)S(1)}, u32[]{:S(2)}) copy-start(f32[8,60,128]{2,1,0:T(8,128)S(1)} %collective-permute-done.refs_2_) | copy-start | bytes 737284
  110.7 56.4 %collective-permute-start.15 = (f32[8,16,128]{2,1,0:T(8,128)}, f32[8,16,128]{2,1,0:T(8,128)S(1)}, u32[]{:S(2)}, u32[]{:S(2)}) collective-permute-start(f32[8,16,128]{2,1,0:T(8,128)} %get-tuple-element.37), channel_id=1, source_target_pairs={{1,0},{64,1},{65,64},{3,2},{66,3},{67,66},{5,4},{68,5},{69,68},{7,... | collective-permute-start | bytes 196616 | tf_op jit(solution)/shard_map/ppermute | solution.py:195
  113.8 0.7 copy-start.11
  157.0 27.8 %collective-permute-start.8 = (f32[8,60,128]{2,1,0:T(8,128)}, f32[8,60,128]{2,1,0:T(8,128)S(1)}, u32[]{:S(2)}, u32[]{:S(2)}) collective-permute-start(f32[8,60,128]{2,1,0:T(8,128)} %get-tuple-element.29), channel_id=1, source_target_pairs={{0,2},{2,4},{4,6},{6,8},{8,10},{10,12},{12,14},{14,16},{16,18},{18... | collective-permute-start | bytes 737288 | tf_op jit(solution)/shard_map/ppermute | solution.py:194
  164.9 10.0 %copy-start.13 = (f32[8,16,128]{2,1,0:T(8,128)}, f32[8,16,128]{2,1,0:T(8,128)S(1)}, u32[]{:S(2)}) copy-start(f32[8,16,128]{2,1,0:T(8,128)S(1)} %collective-permute-done.14.refs_6_) | copy-start | bytes 196612
  164.9 19.9 %collective-permute-start.9 = (f32[8,60,128]{2,1,0:T(8,128)}, f32[8,60,128]{2,1,0:T(8,128)S(1)}, u32[]{:S(2)}, u32[]{:S(2)}) collective-permute-start(f32[8,60,128]{2,1,0:T(8,128)} %get-tuple-element.30), channel_id=1, source_target_pairs={{2,0},{4,2},{6,4},{8,6},{10,8},{12,10},{14,12},{16,14},{18,16},{20... | collective-permute-start | bytes 737288 | tf_op jit(solution)/shard_map/ppermute | solution.py:195
  167.0 7.9 %copy-start.14 = (f32[8,16,128]{2,1,0:T(8,128)}, f32[8,16,128]{2,1,0:T(8,128)S(1)}, u32[]{:S(2)}) copy-start(f32[8,16,128]{2,1,0:T(8,128)S(1)} %collective-permute-done.15.refs_7_) | copy-start | bytes 196612
  167.1 17.7 %collective-permute-start.10 = (f32[8,16,128]{2,1,0:T(8,128)}, f32[8,16,128]{2,1,0:T(8,128)S(1)}, u32[]{:S(2)}, u32[]{:S(2)}) collective-permute-start(f32[8,16,128]{2,1,0:T(8,128)} %get-tuple-element.31), channel_id=1, source_target_pairs={{0,1},{1,64},{64,65},{2,3},{3,66},{66,67},{4,5},{5,68},{68,69},{6,... | collective-permute-start | bytes 196616 | tf_op jit(solution)/shard_map/ppermute | solution.py:194
  168.4 6.6 %copy-start.6 = (f32[8,60,128]{2,1,0:T(8,128)}, f32[8,60,128]{2,1,0:T(8,128)S(1)}, u32[]{:S(2)}) copy-start(f32[8,60,128]{2,1,0:T(8,128)S(1)} %collective-permute-done.12.refs_2_) | copy-start | bytes 737284
  168.4 16.4 %collective-permute-start.11 = (f32[8,16,128]{2,1,0:T(8,128)}, f32[8,16,128]{2,1,0:T(8,128)S(1)}, u32[]{:S(2)}, u32[]{:S(2)}) collective-permute-start(f32[8,16,128]{2,1,0:T(8,128)} %get-tuple-element.32), channel_id=1, source_target_pairs={{1,0},{64,1},{65,64},{3,2},{66,3},{67,66},{5,4},{68,5},{69,68},{7,... | collective-permute-start | bytes 196616 | tf_op jit(solution)/shard_map/ppermute | solution.py:195
  174.9 0.7 copy-start.7
  184.8 0.6 copy-start.16
  184.8 0.6 copy-start.17
  184.8 0.7 copy-start.8
  184.8 0.8 copy-start.9
  185.6 16.6 %copy-start.19 = (s32[8,256]{1,0:T(8,128)S(1)}, s32[8,256]{1,0:T(8,128)}, u32[]{:S(2)}) copy-start(s32[8,256]{1,0:T(8,128)} %param.13) | copy-start | bytes 24580
  185.6 16.6 %copy-start.5 = (f32[8,8,256]{2,1,0:T(8,128)S(1)}, f32[8,8,256]{2,1,0:T(8,128)}, u32[]{:S(2)}) copy-start(f32[8,8,256]{2,1,0:T(8,128)} %param.11) | copy-start | bytes 196612
  202.6 17.4 %collective-permute-start.20 = (f32[8,8,1]{2,1,0:T(8,128)S(1)}, f32[8,8,1]{2,1,0:T(8,128)S(1)}, u32[]{:S(2)}, u32[]{:S(2)}) collective-permute-start(f32[8,8,1]{2,1,0:T(8,128)S(1)} %get-tuple-element.59), channel_id=1, source_target_pairs={{0,64},{1,65},{2,66},{3,67},{4,68},{5,69},{6,70},{7,71},{8,72},{9,... | collective-permute-start | bytes 776 | tf_op jit(solution)/shard_map/ppermute | solution.py:194
  203.9 16.1 %collective-permute-start.23 = (f32[8,8,1]{2,1,0:T(8,128)S(1)}, f32[8,8,1]{2,1,0:T(8,128)S(1)}, u32[]{:S(2)}, u32[]{:S(2)}) collective-permute-start(f32[8,8,1]{2,1,0:T(8,128)S(1)} %get-tuple-element.60), channel_id=1, source_target_pairs={{64,0},{65,1},{66,2},{67,3},{68,4},{69,5},{70,6},{71,7},{72,8},{73... | collective-permute-start | bytes 776 | tf_op jit(solution)/shard_map/ppermute | solution.py:195
  209.4 10.7 %collective-permute-start.21 = (f32[8,1,256]{2,1,0:T(1,128)S(1)}, f32[8,1,256]{2,1,0:T(1,128)S(1)}, u32[]{:S(2)}, u32[]{:S(2)}) collective-permute-start(f32[8,1,256]{2,1,0:T(1,128)S(1)} %get-tuple-element.61), channel_id=1, source_target_pairs={{0,1},{1,2},{2,3},{3,4},{4,5},{5,6},{6,7},{7,8},{8,9},{9,10},{10,1... | collective-permute-start | bytes 24584 | tf_op jit(solution)/shard_map/ppermute | solution.py:194
  218.0 9.2 %collective-permute-start.22 = (f32[8,1,256]{2,1,0:T(1,128)S(1)}, f32[8,1,256]{2,1,0:T(1,128)S(1)}, u32[]{:S(2)}, u32[]{:S(2)}) collective-permute-start(f32[8,1,256]{2,1,0:T(1,128)S(1)} %get-tuple-element.62), channel_id=1, source_target_pairs={{1,0},{2,1},{3,2},{4,3},{5,4},{6,5},{7,6},{8,7},{9,8},{10,9},{11,1... | collective-permute-start | bytes 24584 | tf_op jit(solution)/shard_map/ppermute | solution.py:195
  227.9 11.3 %collective-permute-start.24 = (f32[8,8,1]{2,1,0:T(8,128)S(1)}, f32[8,8,1]{2,1,0:T(8,128)S(1)}, u32[]{:S(2)}, u32[]{:S(2)}) collective-permute-start(f32[8,8,1]{2,1,0:T(8,128)S(1)} %get-tuple-element.53), channel_id=1, source_target_pairs={{0,64},{1,65},{2,66},{3,67},{4,68},{5,69},{6,70},{7,71},{8,72},{9,... | collective-permute-start | bytes 776 | tf_op jit(solution)/shard_map/ppermute | solution.py:194
  229.2 10.0 %collective-permute-start.27 = (f32[8,8,1]{2,1,0:T(8,128)S(1)}, f32[8,8,1]{2,1,0:T(8,128)S(1)}, u32[]{:S(2)}, u32[]{:S(2)}) collective-permute-start(f32[8,8,1]{2,1,0:T(8,128)S(1)} %get-tuple-element.54), channel_id=1, source_target_pairs={{64,0},{65,1},{66,2},{67,3},{68,4},{69,5},{70,6},{71,7},{72,8},{73... | collective-permute-start | bytes 776 | tf_op jit(solution)/shard_map/ppermute | solution.py:195
  234.7 4.5 %collective-permute-start.25 = (f32[8,1,256]{2,1,0:T(1,128)S(1)}, f32[8,1,256]{2,1,0:T(1,128)S(1)}, u32[]{:S(2)}, u32[]{:S(2)}) collective-permute-start(f32[8,1,256]{2,1,0:T(1,128)S(1)} %get-tuple-element.55), channel_id=1, source_target_pairs={{0,1},{1,2},{2,3},{3,4},{4,5},{5,6},{6,7},{7,8},{8,9},{9,10},{10,1... | collective-permute-start | bytes 24584 | tf_op jit(solution)/shard_map/ppermute | solution.py:194
  237.2 9.2 %collective-permute-start.26 = (f32[8,1,256]{2,1,0:T(1,128)S(1)}, f32[8,1,256]{2,1,0:T(1,128)S(1)}, u32[]{:S(2)}, u32[]{:S(2)}) collective-permute-start(f32[8,1,256]{2,1,0:T(1,128)S(1)} %get-tuple-element.56), channel_id=1, source_target_pairs={{1,0},{2,1},{3,2},{4,3},{5,4},{6,5},{7,6},{8,7},{9,8},{10,9},{11,1... | collective-permute-start | bytes 24584 | tf_op jit(solution)/shard_map/ppermute | solution.py:195

commit v3 on v1

--- a/solution.py
+++ b/solution.py
@@ -149,16 +149,17 @@
     return before, after
 
 
-def advection(tracers, wind_courant):
+def advection(tracers, wind_courant, soil_block):
     cols_axes = ("mp", "gy")
     rf, rl, cf, cl = edges(tracers, wind_courant)
     top, bot = exchange(rf, rl, "gx")
     left, right = exchange(cf, cl, cols_axes)
     mid = advect_step(tracers, wind_courant, top, bot, top, bot, left, right, left, right)
+    mid, soil_block = lax.optimization_barrier((mid, soil_block))
     srf, srl, scf, scl = edges(mid)
     stop, sbot = exchange(srf, srl, "gx")
     sleft, sright = exchange(scf, scl, cols_axes)
-    return advect_step(mid, wind_courant, stop, sbot, top, bot, sleft, sright, left, right)
+    return advect_step(mid, wind_courant, stop, sbot, top, bot, sleft, sright, left, right), soil_block
 
 
 def padded_2(block, sides, width):
@@ -246,7 +247,10 @@
     conductivity_table,
     exponent_table,
 ):
-    advected = advection(tracers, wind_courant)
+    saturated = lookup(soil_type, conductivity_table)
+    exponent = lookup(soil_type, exponent_table)
+    soil_block = jnp.concatenate([pressure_head, saturated[None], exponent[None]], axis=0)
+    advected, soil_block = advection(tracers, wind_courant, soil_block)
     received = lax.all_to_all(
         forcing_fields(advected), "gy", split_axis=1, concat_axis=2, tiled=True
     )
@@ -255,7 +259,7 @@
     exponent = lookup(soil_type, exponent_table)
     layers = pressure_head.shape[0]
     padded_head = padded_2(
-        jnp.concatenate([pressure_head, saturated[None], exponent[None]], axis=0),
+        soil_block,
         ((("gx", "gy"), 1), ("mp", 2)),
         1,
     )

time: 150 us -> 159 us (1.060)
  the two profiles are of different devices: /device:TPU:31 before, /device:TPU:119 now
where the time goes in v3:
time: 159 us; the launch traced here: 158 us
  starting transfers between devices  59.2 us (37%)
  Pallas kernels  50.3 us (32%)
  waiting for transfers between devices  36.1 us (23%)
  blocking collectives  5.27 us (3%)
  other arithmetic  3.23 us (2%)
  local copies, waits for them, and re-layouts  2.28 us (1%)
    ppermute x10, starting transfers between devices, exchange(): after = lax.ppermute(first, axes, shift_pairs(n, -1))  38.1 us
    pallas_call x2, Pallas kernels, advect_step(): pl.pallas_call(step_kernel, grid=(nsp // SB,), in_specs=[main, pl.BlockSp...  31.3 us
    ppermute x10, waiting for transfers between devices, exchange(): after = lax.ppermute(first, axes, shift_pairs(n, -1))  29 us
    ppermute x10, starting transfers between devices, exchange(): before = lax.ppermute(last, axes, shift_pairs(n, 1))  21.1 us
    pallas_call x2, Pallas kernels, edges(): pl.pallas_call(functools.partial(edge_kernel, nmain), grid=(total // nb,)...  19 us
    ppermute x10, waiting for transfers between devices, exchange(): before = lax.ppermute(last, axes, shift_pairs(n, 1))  7.07 us
    all_to_all x1, blocking collectives, on_device(): lax.all_to_all(forcing_fields(advected), 'gy', split_axis=1, concat_axis=...  5.27 us
  transfers between devices with their start and end apart: 20, of which 8 were waited for; matrix products, arithmetic and copies ran while one was open for 0% of the time, Pallas kernels for 6%

profile of v3, /device:TPU:119, one launch (start us, length us, event | category | flops | bytes accessed | tf_op | source)
XLA Modules:
  0.0 157.6 jit_solution(9906561797755090956)
XLA Ops:
  0.7 10.0 %shard_map.95 = (f32[18,60,128]{2,1,0:T(8,128)}, f32[18,60,128]{2,1,0:T(8,128)}, f32[18,16,128]{2,1,0:T(8,128)}, f32[18,16,128]{2,1,0:T(8,128)}) custom-call(f32[16,60,16,128]{3,2,1,0:T(8,128)} %f_ref.3, f32[2,60,16,128]{3,2,1,0:T(8,128)} %w_ref.3), custom_call_target="tpu_custom_call" | custom-call | flops 8847360 | bytes 8847360 | tf_op jit(solution)/shard_map/pallas_call | solution.py:69
  10.7 1.9 %collective-permute-start = (f32[18,60,128]{2,1,0:T(8,128)}, f32[18,60,128]{2,1,0:T(8,128)S(1)}, u32[]{:S(2)}, u32[]{:S(2)}) collective-permute-start(f32[18,60,128]{2,1,0:T(8,128)} %get-tuple-element.12), channel_id=1, source_target_pairs={{0,2},{2,4},{4,6},{6,8},{8,10},{10,12},{12,14},{14,16},{16,18},{18... | collective-permute-start | bytes 1658888 | tf_op jit(solution)/shard_map/ppermute | solution.py:147
  12.6 3.4 %collective-permute-start.1 = (f32[18,60,128]{2,1,0:T(8,128)}, f32[18,60,128]{2,1,0:T(8,128)S(1)}, u32[]{:S(2)}, u32[]{:S(2)}) collective-permute-start(f32[18,60,128]{2,1,0:T(8,128)} %get-tuple-element.13), channel_id=1, source_target_pairs={{2,0},{4,2},{6,4},{8,6},{10,8},{12,10},{14,12},{16,14},{18,16},{20... | collective-permute-start | bytes 1658888 | tf_op jit(solution)/shard_map/ppermute | solution.py:148
  15.9 1.3 collective-permute-start.2
  17.2 3.8 %collective-permute-start.3 = (f32[18,16,128]{2,1,0:T(8,128)}, f32[18,16,128]{2,1,0:T(8,128)S(1)}, u32[]{:S(2)}, u32[]{:S(2)}) collective-permute-start(f32[18,16,128]{2,1,0:T(8,128)} %get-tuple-element.15), channel_id=1, source_target_pairs={{1,0},{64,1},{65,64},{3,2},{66,3},{67,66},{5,4},{68,5},{69,68},{7,... | collective-permute-start | bytes 442376 | tf_op jit(solution)/shard_map/ppermute | solution.py:148
  21.1 0.1 select_reduce_fusion.1
  21.2 0.0 collective-permute-done.2.fleft_ref.wleft_ref
  21.2 1.0 collective-permute-done.3.fright_ref.wright_ref
  22.2 4.7 %collective-permute-done.ftop_ref.wtop_ref = f32[18,60,128]{2,1,0:T(8,128)S(1)} collective-permute-done((f32[18,60,128]{2,1,0:T(8,128)}, f32[18,60,128]{2,1,0:T(8,128)S(1)}, u32[]{:S(2)}, u32[]{:S(2)}) %collective-permute-start) | collective-permute-done | bytes 552992 | tf_op jit(solution)/shard_map/ppermute | solution.py:147
  27.0 6.2 %collective-permute-done.1.fbot_ref.wbot_ref = f32[18,60,128]{2,1,0:T(8,128)S(1)} collective-permute-done((f32[18,60,128]{2,1,0:T(8,128)}, f32[18,60,128]{2,1,0:T(8,128)S(1)}, u32[]{:S(2)}, u32[]{:S(2)}) %collective-permute-start.1) | collective-permute-done | bytes 552992 | tf_op jit(solution)/shard_map/ppermute | solution.py:148
  33.2 0.8 copy-done.1
  34.0 15.7 %shard_map.96.f_ref = f32[16,60,16,128]{3,2,1,0:T(8,128)} custom-call(f32[16,60,16,128]{3,2,1,0:T(8,128)} %f_ref.3, f32[2,60,16,128]{3,2,1,0:T(8,128)} %w_ref.3, f32[18,60,128]{2,1,0:T(8,128)} %copy-done, f32[18,60,128]{2,1,0:T(8,128)} %copy-done.1, f32[18,60,128]{2,1,0:T(8,128)} %copy-done, f32[18,60,128]{2,1,0:T(8,128)} %copy-done.1, ...), custom_call_target="tpu_custom_call" | custom-call | flops 39321600 | bytes 16711680 | tf_op jit(solution)/shard_map/pallas_call | solution.py:134
  49.7 3.5 %collective-permute-start.10 = (f32[10,1,256]{2,1,0:T(1,128)S(1)}, f32[10,1,256]{2,1,0:T(1,128)S(1)}, u32[]{:S(2)}, u32[]{:S(2)}) collective-permute-start(f32[10,1,256]{2,1,0:T(1,128)S(1)} %get-tuple-element.34), channel_id=1, source_target_pairs={{1,0},{2,1},{3,2},{4,3},{5,4},{6,5},{7,6},{8,7},{9,8},{10,9},{11,1... | collective-permute-start | bytes 30728 | tf_op jit(solution)/shard_map/ppermute | solution.py:148
  53.2 6.3 %collective-permute-start.9 = (f32[10,1,256]{2,1,0:T(1,128)S(1)}, f32[10,1,256]{2,1,0:T(1,128)S(1)}, u32[]{:S(2)}, u32[]{:S(2)}) collective-permute-start(f32[10,1,256]{2,1,0:T(1,128)S(1)} %get-tuple-element.33), channel_id=1, source_target_pairs={{0,1},{1,2},{2,3},{3,4},{4,5},{5,6},{6,7},{7,8},{8,9},{9,10},{10,1... | collective-permute-start | bytes 30728 | tf_op jit(solution)/shard_map/ppermute | solution.py:147
  59.5 0.1 fusion.72
  59.6 1.3 collective-permute-start.8
  60.9 9.0 %shard_map.97 = (f32[16,60,128]{2,1,0:T(8,128)}, f32[16,60,128]{2,1,0:T(8,128)}, f32[16,16,128]{2,1,0:T(8,128)}, f32[16,16,128]{2,1,0:T(8,128)}) custom-call(f32[16,60,16,128]{3,2,1,0:T(8,128)} %shard_map.96.f_ref), custom_call_target="tpu_custom_call" | custom-call | flops 7864320 | bytes 7864320 | tf_op jit(solution)/shard_map/pallas_call | solution.py:69
  69.9 5.5 %collective-permute-start.11 = (f32[10,8,1]{2,1,0:T(8,128)S(1)}, f32[10,8,1]{2,1,0:T(8,128)S(1)}, u32[]{:S(2)}, u32[]{:S(2)}) collective-permute-start(f32[10,8,1]{2,1,0:T(8,128)S(1)} %get-tuple-element.36), channel_id=1, source_target_pairs={{64,0},{65,1},{66,2},{67,3},{68,4},{69,5},{70,6},{71,7},{72,8},{73... | collective-permute-start | bytes 968 | tf_op jit(solution)/shard_map/ppermute | solution.py:148
  75.4 1.9 %collective-permute-start.4 = (f32[16,60,128]{2,1,0:T(8,128)}, f32[16,60,128]{2,1,0:T(8,128)S(1)}, u32[]{:S(2)}, u32[]{:S(2)}) collective-permute-start(f32[16,60,128]{2,1,0:T(8,128)} %get-tuple-element.17), channel_id=1, source_target_pairs={{0,2},{2,4},{4,6},{6,8},{8,10},{10,12},{12,14},{14,16},{16,18},{18... | collective-permute-start | bytes 1474568 | tf_op jit(solution)/shard_map/ppermute | solution.py:147
  77.3 0.0 collective-permute-done.8
  77.3 3.4 %collective-permute-start.5 = (f32[16,60,128]{2,1,0:T(8,128)}, f32[16,60,128]{2,1,0:T(8,128)S(1)}, u32[]{:S(2)}, u32[]{:S(2)}) collective-permute-start(f32[16,60,128]{2,1,0:T(8,128)} %get-tuple-element.18), channel_id=1, source_target_pairs={{2,0},{4,2},{6,4},{8,6},{10,8},{12,10},{14,12},{16,14},{18,16},{20... | collective-permute-start | bytes 1474568 | tf_op jit(solution)/shard_map/ppermute | solution.py:148
  80.7 0.0 collective-permute-done.11
  80.7 1.3 collective-permute-start.6
  82.0 0.0 collective-permute-done.10
  82.0 3.0 %collective-permute-start.7 = (f32[16,16,128]{2,1,0:T(8,128)}, f32[16,16,128]{2,1,0:T(8,128)S(1)}, u32[]{:S(2)}, u32[]{:S(2)}) collective-permute-start(f32[16,16,128]{2,1,0:T(8,128)} %get-tuple-element.20), channel_id=1, source_target_pairs={{1,0},{64,1},{65,64},{3,2},{66,3},{67,66},{5,4},{68,5},{69,68},{7,... | collective-permute-start | bytes 393224 | tf_op jit(solution)/shard_map/ppermute | solution.py:148
  85.1 0.1 maximum_bitcast_fusion.1
  85.2 0.2 fusion.3
  85.4 0.1 slice.308
  85.5 0.1 fusion.58
  85.6 0.0 copy-start.11
  85.6 0.0 copy-start.4
  85.6 0.0 collective-permute-done.6.fleft_ref
  85.6 0.6 collective-permute-done.7.fright_ref
  86.3 2.3 %collective-permute-done.4.ftop_ref = f32[16,60,128]{2,1,0:T(8,128)S(1)} collective-permute-done((f32[16,60,128]{2,1,0:T(8,128)}, f32[16,60,128]{2,1,0:T(8,128)S(1)}, u32[]{:S(2)}, u32[]{:S(2)}) %collective-permute-start.4) | collective-permute-done | bytes 491552 | tf_op jit(solution)/shard_map/ppermute | solution.py:147
  88.6 7.6 %collective-permute-done.5.fbot_ref = f32[16,60,128]{2,1,0:T(8,128)S(1)} collective-permute-done((f32[16,60,128]{2,1,0:T(8,128)}, f32[16,60,128]{2,1,0:T(8,128)S(1)}, u32[]{:S(2)}, u32[]{:S(2)}) %collective-permute-start.5) | collective-permute-done | bytes 491552 | tf_op jit(solution)/shard_map/ppermute | solution.py:148
  96.2 0.8 copy-done.6
  97.0 15.6 %shard_map.98 = f32[16,60,16,128]{3,2,1,0:T(8,128)} custom-call(f32[16,60,16,128]{3,2,1,0:T(8,128)} %shard_map.96.f_ref, f32[2,60,16,128]{3,2,1,0:T(8,128)} %w_ref.3, f32[16,60,128]{2,1,0:T(8,128)} %copy-done.5, f32[16,60,128]{2,1,0:T(8,128)} %copy-done.6, f32[18,60,128]{2,1,0:T(8,128)} %copy-done, f32[18,60,128]{2,1,0:T(8,128)} %copy-done.1, ...), custom_call_target="tpu_custom_call" | custom-call | flops 39321600 | bytes 16711680 | tf_op jit(solution)/shard_map/pallas_call | solution.py:134
  112.6 0.8 compare_select_fusion.17
  113.5 5.3 %all_to_all.15 = f32[3,16,128]{2,0,1:T(4,128)S(1)} all-to-all(f32[3,16,128]{2,0,1:T(4,128)S(1)} %copy.12), channel_id=1, replica_groups=mesh['mp'=2,'gx'=32,'gy'=2] {'gy'}, dimensions={1} | all-to-all | bytes 49152 | tf_op jit(solution)/shard_map/all_to_all | solution.py:254
  118.8 0.2 fusion.12
  119.0 0.1 fusion.77
  119.1 1.3 collective-permute-start.12
  120.4 5.5 %collective-permute-start.15 = (f32[8,8,1]{2,1,0:T(8,128)S(1)}, f32[8,8,1]{2,1,0:T(8,128)S(1)}, u32[]{:S(2)}, u32[]{:S(2)}) collective-permute-start(f32[8,8,1]{2,1,0:T(8,128)S(1)} %get-tuple-element.46), channel_id=1, source_target_pairs={{64,0},{65,1},{66,2},{67,3},{68,4},{69,5},{70,6},{71,7},{72,8},{73... | collective-permute-start | bytes 776 | tf_op jit(solution)/shard_map/ppermute | solution.py:148
  125.9 2.0 %collective-permute-start.13 = (f32[8,1,256]{2,1,0:T(1,128)S(1)}, f32[8,1,256]{2,1,0:T(1,128)S(1)}, u32[]{:S(2)}, u32[]{:S(2)}) collective-permute-start(f32[8,1,256]{2,1,0:T(1,128)S(1)} %get-tuple-element.47), channel_id=1, source_target_pairs={{0,1},{1,2},{2,3},{3,4},{4,5},{5,6},{6,7},{7,8},{8,9},{9,10},{10,1... | collective-permute-start | bytes 24584 | tf_op jit(solution)/shard_map/ppermute | solution.py:147
  127.9 2.7 %collective-permute-start.14 = (f32[8,1,256]{2,1,0:T(1,128)S(1)}, f32[8,1,256]{2,1,0:T(1,128)S(1)}, u32[]{:S(2)}, u32[]{:S(2)}) collective-permute-start(f32[8,1,256]{2,1,0:T(1,128)S(1)} %get-tuple-element.48), channel_id=1, source_target_pairs={{1,0},{2,1},{3,2},{4,3},{5,4},{6,5},{7,6},{8,7},{9,8},{10,9},{11,1... | collective-permute-start | bytes 24584 | tf_op jit(solution)/shard_map/ppermute | solution.py:148
  130.7 0.0 collective-permute-done.12
  130.7 0.0 collective-permute-done.15
  130.7 6.4 %collective-permute-done.14 = f32[8,1,256]{2,1,0:T(1,128)S(1)} collective-permute-done((f32[8,1,256]{2,1,0:T(1,128)S(1)}, f32[8,1,256]{2,1,0:T(1,128)S(1)}, u32[]{:S(2)}, u32[]{:S(2)}) %collective-permute-start.14) | collective-permute-done | bytes 8224 | tf_op jit(solution)/shard_map/ppermute | solution.py:148
  137.1 0.2 fusion.6
  137.3 0.1 fusion.59
  137.4 0.1 slice.322
  137.5 0.2 fusion.15
  137.7 0.1 fusion.74
  137.8 1.3 collective-permute-start.16
  139.1 5.5 %collective-permute-start.19 = (f32[8,8,1]{2,1,0:T(8,128)S(1)}, f32[8,8,1]{2,1,0:T(8,128)S(1)}, u32[]{:S(2)}, u32[]{:S(2)}) collective-permute-start(f32[8,8,1]{2,1,0:T(8,128)S(1)} %get-tuple-element.40), channel_id=1, source_target_pairs={{64,0},{65,1},{66,2},{67,3},{68,4},{69,5},{70,6},{71,7},{72,8},{73... | collective-permute-start | bytes 776 | tf_op jit(solution)/shard_map/ppermute | solution.py:148
  144.6 2.5 %collective-permute-start.17 = (f32[8,1,256]{2,1,0:T(1,128)S(1)}, f32[8,1,256]{2,1,0:T(1,128)S(1)}, u32[]{:S(2)}, u32[]{:S(2)}) collective-permute-start(f32[8,1,256]{2,1,0:T(1,128)S(1)} %get-tuple-element.41), channel_id=1, source_target_pairs={{0,1},{1,2},{2,3},{3,4},{4,5},{5,6},{6,7},{7,8},{8,9},{9,10},{10,1... | collective-permute-start | bytes 24584 | tf_op jit(solution)/shard_map/ppermute | solution.py:147
  147.1 1.9 %collective-permute-start.18 = (f32[8,1,256]{2,1,0:T(1,128)S(1)}, f32[8,1,256]{2,1,0:T(1,128)S(1)}, u32[]{:S(2)}, u32[]{:S(2)}) collective-permute-start(f32[8,1,256]{2,1,0:T(1,128)S(1)} %get-tuple-element.42), channel_id=1, source_target_pairs={{1,0},{2,1},{3,2},{4,3},{5,4},{6,5},{7,6},{8,7},{9,8},{10,9},{11,1... | collective-permute-start | bytes 24584 | tf_op jit(solution)/shard_map/ppermute | solution.py:148
  149.1 0.0 collective-permute-done.16
  149.1 0.0 collective-permute-done.19
  149.2 7.2 %collective-permute-done.18 = f32[8,1,256]{2,1,0:T(1,128)S(1)} collective-permute-done((f32[8,1,256]{2,1,0:T(1,128)S(1)}, f32[8,1,256]{2,1,0:T(1,128)S(1)}, u32[]{:S(2)}, u32[]{:S(2)}) %collective-permute-start.18) | collective-permute-done | bytes 8224 | tf_op jit(solution)/shard_map/ppermute | solution.py:148
  156.3 0.2 fusion.9
  156.5 0.1 fusion.60
  156.7 0.1 slice.336
  156.7 0.9 fusion.18
  (44 shorter events, 0.2 us)
Async XLA Ops:
  0.6 20.4 %copy-start.10 = (s32[8,256]{1,0:T(8,128)S(1)}, s32[8,256]{1,0:T(8,128)}, u32[]{:S(2)}) copy-start(s32[8,256]{1,0:T(8,128)} %param.12) | copy-start | bytes 24580
  0.6 20.4 %copy-start.12 = (f32[12]{0:T(128)S(1)}, f32[12]{0:T(128)}, u32[]{:S(2)}) copy-start(f32[12]{0:T(128)} %param.14) | copy-start | bytes 148
  0.7 20.4 %copy-start.13 = (f32[12]{0:T(128)S(1)}, f32[12]{0:T(128)}, u32[]{:S(2)}) copy-start(f32[12]{0:T(128)} %param.15) | copy-start | bytes 148
  0.7 20.5 %copy-start.7 = (f32[8,8,256]{2,1,0:T(8,128)S(1)}, f32[8,8,256]{2,1,0:T(8,128)}, u32[]{:S(2)}) copy-start(f32[8,8,256]{2,1,0:T(8,128)} %param.10) | copy-start | bytes 196612
  10.7 16.3 %collective-permute-start = (f32[18,60,128]{2,1,0:T(8,128)}, f32[18,60,128]{2,1,0:T(8,128)S(1)}, u32[]{:S(2)}, u32[]{:S(2)}) collective-permute-start(f32[18,60,128]{2,1,0:T(8,128)} %get-tuple-element.12), channel_id=1, source_target_pairs={{0,2},{2,4},{4,6},{6,8},{8,10},{10,12},{12,14},{14,16},{16,18},{18... | collective-permute-start | bytes 1658888 | tf_op jit(solution)/shard_map/ppermute | solution.py:147
  12.6 20.6 %collective-permute-start.1 = (f32[18,60,128]{2,1,0:T(8,128)}, f32[18,60,128]{2,1,0:T(8,128)S(1)}, u32[]{:S(2)}, u32[]{:S(2)}) collective-permute-start(f32[18,60,128]{2,1,0:T(8,128)} %get-tuple-element.13), channel_id=1, source_target_pairs={{2,0},{4,2},{6,4},{8,6},{10,8},{12,10},{14,12},{16,14},{18,16},{20... | collective-permute-start | bytes 1658888 | tf_op jit(solution)/shard_map/ppermute | solution.py:148
  15.9 5.2 %collective-permute-start.2 = (f32[18,16,128]{2,1,0:T(8,128)}, f32[18,16,128]{2,1,0:T(8,128)S(1)}, u32[]{:S(2)}, u32[]{:S(2)}) collective-permute-start(f32[18,16,128]{2,1,0:T(8,128)} %get-tuple-element.14), channel_id=1, source_target_pairs={{0,1},{1,64},{64,65},{2,3},{3,66},{66,67},{4,5},{5,68},{68,69},{6,... | collective-permute-start | bytes 442376 | tf_op jit(solution)/shard_map/ppermute | solution.py:147
  17.2 5.0 %collective-permute-start.3 = (f32[18,16,128]{2,1,0:T(8,128)}, f32[18,16,128]{2,1,0:T(8,128)S(1)}, u32[]{:S(2)}, u32[]{:S(2)}) collective-permute-start(f32[18,16,128]{2,1,0:T(8,128)} %get-tuple-element.15), channel_id=1, source_target_pairs={{1,0},{64,1},{65,64},{3,2},{66,3},{67,66},{5,4},{68,5},{69,68},{7,... | collective-permute-start | bytes 442376 | tf_op jit(solution)/shard_map/ppermute | solution.py:148
  21.2 12.0 %copy-start.2 = (f32[18,16,128]{2,1,0:T(8,128)}, f32[18,16,128]{2,1,0:T(8,128)S(1)}, u32[]{:S(2)}) copy-start(f32[18,16,128]{2,1,0:T(8,128)S(1)} %collective-permute-done.2.fleft_ref.wleft_ref) | copy-start | bytes 442372
  22.2 10.9 %copy-start.3 = (f32[18,16,128]{2,1,0:T(8,128)}, f32[18,16,128]{2,1,0:T(8,128)S(1)}, u32[]{:S(2)}) copy-start(f32[18,16,128]{2,1,0:T(8,128)S(1)} %collective-permute-done.3.fright_ref.wright_ref) | copy-start | bytes 442372
  27.0 6.2 %copy-start = (f32[18,60,128]{2,1,0:T(8,128)}, f32[18,60,128]{2,1,0:T(8,128)S(1)}, u32[]{:S(2)}) copy-start(f32[18,60,128]{2,1,0:T(8,128)S(1)} %collective-permute-done.ftop_ref.wtop_ref) | copy-start | bytes 1658884
  33.2 0.8 copy-start.1
  49.7 32.3 %collective-permute-start.10 = (f32[10,1,256]{2,1,0:T(1,128)S(1)}, f32[10,1,256]{2,1,0:T(1,128)S(1)}, u32[]{:S(2)}, u32[]{:S(2)}) collective-permute-start(f32[10,1,256]{2,1,0:T(1,128)S(1)} %get-tuple-element.34), channel_id=1, source_target_pairs={{1,0},{2,1},{3,2},{4,3},{5,4},{6,5},{7,6},{8,7},{9,8},{10,9},{11,1... | collective-permute-start | bytes 30728 | tf_op jit(solution)/shard_map/ppermute | solution.py:148
  53.2 31.9 %collective-permute-start.9 = (f32[10,1,256]{2,1,0:T(1,128)S(1)}, f32[10,1,256]{2,1,0:T(1,128)S(1)}, u32[]{:S(2)}, u32[]{:S(2)}) collective-permute-start(f32[10,1,256]{2,1,0:T(1,128)S(1)} %get-tuple-element.33), channel_id=1, source_target_pairs={{0,1},{1,2},{2,3},{3,4},{4,5},{5,6},{6,7},{7,8},{8,9},{9,10},{10,1... | collective-permute-start | bytes 30728 | tf_op jit(solution)/shard_map/ppermute | solution.py:147
  59.6 17.7 %collective-permute-start.8 = (f32[10,8,1]{2,1,0:T(8,128)S(1)}, f32[10,8,1]{2,1,0:T(8,128)S(1)}, u32[]{:S(2)}, u32[]{:S(2)}) collective-permute-start(f32[10,8,1]{2,1,0:T(8,128)S(1)} %get-tuple-element.35), channel_id=1, source_target_pairs={{0,64},{1,65},{2,66},{3,67},{4,68},{5,69},{6,70},{7,71},{8,72},{9,... | collective-permute-start | bytes 968 | tf_op jit(solution)/shard_map/ppermute | solution.py:147
  69.9 10.8 %collective-permute-start.11 = (f32[10,8,1]{2,1,0:T(8,128)S(1)}, f32[10,8,1]{2,1,0:T(8,128)S(1)}, u32[]{:S(2)}, u32[]{:S(2)}) collective-permute-start(f32[10,8,1]{2,1,0:T(8,128)S(1)} %get-tuple-element.36), channel_id=1, source_target_pairs={{64,0},{65,1},{66,2},{67,3},{68,4},{69,5},{70,6},{71,7},{72,8},{73... | collective-permute-start | bytes 968 | tf_op jit(solution)/shard_map/ppermute | solution.py:148
  75.4 13.2 %collective-permute-start.4 = (f32[16,60,128]{2,1,0:T(8,128)}, f32[16,60,128]{2,1,0:T(8,128)S(1)}, u32[]{:S(2)}, u32[]{:S(2)}) collective-permute-start(f32[16,60,128]{2,1,0:T(8,128)} %get-tuple-element.17), channel_id=1, source_target_pairs={{0,2},{2,4},{4,6},{6,8},{8,10},{10,12},{12,14},{14,16},{16,18},{18... | collective-permute-start | bytes 1474568 | tf_op jit(solution)/shard_map/ppermute | solution.py:147
  77.3 18.9 %collective-permute-start.5 = (f32[16,60,128]{2,1,0:T(8,128)}, f32[16,60,128]{2,1,0:T(8,128)S(1)}, u32[]{:S(2)}, u32[]{:S(2)}) collective-permute-start(f32[16,60,128]{2,1,0:T(8,128)} %get-tuple-element.18), channel_id=1, source_target_pairs={{2,0},{4,2},{6,4},{8,6},{10,8},{12,10},{14,12},{16,14},{18,16},{20... | collective-permute-start | bytes 1474568 | tf_op jit(solution)/shard_map/ppermute | solution.py:148
  80.7 4.9 %collective-permute-start.6 = (f32[16,16,128]{2,1,0:T(8,128)}, f32[16,16,128]{2,1,0:T(8,128)S(1)}, u32[]{:S(2)}, u32[]{:S(2)}) collective-permute-start(f32[16,16,128]{2,1,0:T(8,128)} %get-tuple-element.19), channel_id=1, source_target_pairs={{0,1},{1,64},{64,65},{2,3},{3,66},{66,67},{4,5},{5,68},{68,69},{6,... | collective-permute-start | bytes 393224 | tf_op jit(solution)/shard_map/ppermute | solution.py:147
  82.0 4.2 %collective-permute-start.7 = (f32[16,16,128]{2,1,0:T(8,128)}, f32[16,16,128]{2,1,0:T(8,128)S(1)}, u32[]{:S(2)}, u32[]{:S(2)}) collective-permute-start(f32[16,16,128]{2,1,0:T(8,128)} %get-tuple-element.20), channel_id=1, source_target_pairs={{1,0},{64,1},{65,64},{3,2},{66,3},{67,66},{5,4},{68,5},{69,68},{7,... | collective-permute-start | bytes 393224 | tf_op jit(solution)/shard_map/ppermute | solution.py:148
  85.6 33.2 %copy-start.11 = (s32[8,256]{1,0:T(8,128)S(1)}, s32[8,256]{1,0:T(8,128)}, u32[]{:S(2)}) copy-start(s32[8,256]{1,0:T(8,128)} %param.13) | copy-start | bytes 24580
  85.6 33.2 %copy-start.4 = (f32[8,8,256]{2,1,0:T(8,128)S(1)}, f32[8,8,256]{2,1,0:T(8,128)}, u32[]{:S(2)}) copy-start(f32[8,8,256]{2,1,0:T(8,128)} %param.11) | copy-start | bytes 196612
  85.6 10.6 %copy-start.8 = (f32[16,16,128]{2,1,0:T(8,128)}, f32[16,16,128]{2,1,0:T(8,128)S(1)}, u32[]{:S(2)}) copy-start(f32[16,16,128]{2,1,0:T(8,128)S(1)} %collective-permute-done.6.fleft_ref) | copy-start | bytes 393220
  86.3 9.9 %copy-start.9 = (f32[16,16,128]{2,1,0:T(8,128)}, f32[16,16,128]{2,1,0:T(8,128)S(1)}, u32[]{:S(2)}) copy-start(f32[16,16,128]{2,1,0:T(8,128)S(1)} %collective-permute-done.7.fright_ref) | copy-start | bytes 393220
  88.6 7.6 %copy-start.5 = (f32[16,60,128]{2,1,0:T(8,128)}, f32[16,60,128]{2,1,0:T(8,128)S(1)}, u32[]{:S(2)}) copy-start(f32[16,60,128]{2,1,0:T(8,128)S(1)} %collective-permute-done.4.ftop_ref) | copy-start | bytes 1474564
  96.2 0.8 copy-start.6
  119.1 11.6 %collective-permute-start.12 = (f32[8,8,1]{2,1,0:T(8,128)S(1)}, f32[8,8,1]{2,1,0:T(8,128)S(1)}, u32[]{:S(2)}, u32[]{:S(2)}) collective-permute-start(f32[8,8,1]{2,1,0:T(8,128)S(1)} %get-tuple-element.45), channel_id=1, source_target_pairs={{0,64},{1,65},{2,66},{3,67},{4,68},{5,69},{6,70},{7,71},{8,72},{9,... | collective-permute-start | bytes 776 | tf_op jit(solution)/shard_map/ppermute | solution.py:147
  120.4 10.3 %collective-permute-start.15 = (f32[8,8,1]{2,1,0:T(8,128)S(1)}, f32[8,8,1]{2,1,0:T(8,128)S(1)}, u32[]{:S(2)}, u32[]{:S(2)}) collective-permute-start(f32[8,8,1]{2,1,0:T(8,128)S(1)} %get-tuple-element.46), channel_id=1, source_target_pairs={{64,0},{65,1},{66,2},{67,3},{68,4},{69,5},{70,6},{71,7},{72,8},{73... | collective-permute-start | bytes 776 | tf_op jit(solution)/shard_map/ppermute | solution.py:148
  125.9 4.8 %collective-permute-start.13 = (f32[8,1,256]{2,1,0:T(1,128)S(1)}, f32[8,1,256]{2,1,0:T(1,128)S(1)}, u32[]{:S(2)}, u32[]{:S(2)}) collective-permute-start(f32[8,1,256]{2,1,0:T(1,128)S(1)} %get-tuple-element.47), channel_id=1, source_target_pairs={{0,1},{1,2},{2,3},{3,4},{4,5},{5,6},{6,7},{7,8},{8,9},{9,10},{10,1... | collective-permute-start | bytes 24584 | tf_op jit(solution)/shard_map/ppermute | solution.py:147
  127.9 9.2 %collective-permute-start.14 = (f32[8,1,256]{2,1,0:T(1,128)S(1)}, f32[8,1,256]{2,1,0:T(1,128)S(1)}, u32[]{:S(2)}, u32[]{:S(2)}) collective-permute-start(f32[8,1,256]{2,1,0:T(1,128)S(1)} %get-tuple-element.48), channel_id=1, source_target_pairs={{1,0},{2,1},{3,2},{4,3},{5,4},{6,5},{7,6},{8,7},{9,8},{10,9},{11,1... | collective-permute-start | bytes 24584 | tf_op jit(solution)/shard_map/ppermute | solution.py:148
  137.8 11.3 %collective-permute-start.16 = (f32[8,8,1]{2,1,0:T(8,128)S(1)}, f32[8,8,1]{2,1,0:T(8,128)S(1)}, u32[]{:S(2)}, u32[]{:S(2)}) collective-permute-start(f32[8,8,1]{2,1,0:T(8,128)S(1)} %get-tuple-element.39), channel_id=1, source_target_pairs={{0,64},{1,65},{2,66},{3,67},{4,68},{5,69},{6,70},{7,71},{8,72},{9,... | collective-permute-start | bytes 776 | tf_op jit(solution)/shard_map/ppermute | solution.py:147
  139.1 10.0 %collective-permute-start.19 = (f32[8,8,1]{2,1,0:T(8,128)S(1)}, f32[8,8,1]{2,1,0:T(8,128)S(1)}, u32[]{:S(2)}, u32[]{:S(2)}) collective-permute-start(f32[8,8,1]{2,1,0:T(8,128)S(1)} %get-tuple-element.40), channel_id=1, source_target_pairs={{64,0},{65,1},{66,2},{67,3},{68,4},{69,5},{70,6},{71,7},{72,8},{73... | collective-permute-start | bytes 776 | tf_op jit(solution)/shard_map/ppermute | solution.py:148
  144.6 4.5 %collective-permute-start.17 = (f32[8,1,256]{2,1,0:T(1,128)S(1)}, f32[8,1,256]{2,1,0:T(1,128)S(1)}, u32[]{:S(2)}, u32[]{:S(2)}) collective-permute-start(f32[8,1,256]{2,1,0:T(1,128)S(1)} %get-tuple-element.41), channel_id=1, source_target_pairs={{0,1},{1,2},{2,3},{3,4},{4,5},{5,6},{6,7},{7,8},{8,9},{9,10},{10,1... | collective-permute-start | bytes 24584 | tf_op jit(solution)/shard_map/ppermute | solution.py:147
  147.1 9.2 %collective-permute-start.18 = (f32[8,1,256]{2,1,0:T(1,128)S(1)}, f32[8,1,256]{2,1,0:T(1,128)S(1)}, u32[]{:S(2)}, u32[]{:S(2)}) collective-permute-start(f32[8,1,256]{2,1,0:T(1,128)S(1)} %get-tuple-element.42), channel_id=1, source_target_pairs={{1,0},{2,1},{3,2},{4,3},{5,4},{6,5},{7,6},{8,7},{9,8},{10,9},{11,1... | collective-permute-start | bytes 24584 | tf_op jit(solution)/shard_map/ppermute | solution.py:148

commit v4 on v1

--- a/solution.py
+++ b/solution.py
@@ -149,16 +149,140 @@
     return before, after
 
 
+def open_kernel(f_ref, w_ref, o_ref):
+    nb, nlev, rows, cols = f_ref.shape
+    row = lax.broadcasted_iota(jnp.int32, (rows, cols), 0)
+    lane = lax.broadcasted_iota(jnp.int32, (rows, cols), 1)
+    first_row = row == 0
+    last_row = row == rows - 1
+    first_lane = lane == 0
+    last_lane = lane == cols - 1
+    for lev in range(nlev):
+        u = w_ref[0, lev]
+        v = w_ref[1, lev]
+        u_prev = jnp.where(first_row, 0.0, pltpu.roll(u, 1, 0))
+        u_next = jnp.where(last_row, 0.0, pltpu.roll(u, rows - 1, 0))
+        v_prev = jnp.where(first_lane, 0.0, pltpu.roll(v, 1, 1))
+        v_next = jnp.where(last_lane, 0.0, pltpu.roll(v, cols - 1, 1))
+        pu = jnp.maximum(u, 0.0)
+        mu = jnp.minimum(u, 0.0)
+        pu_prev = jnp.maximum(u_prev, 0.0)
+        mu_next = jnp.minimum(u_next, 0.0)
+        pv = jnp.maximum(v, 0.0)
+        mv = jnp.minimum(v, 0.0)
+        pv_prev = jnp.maximum(v_prev, 0.0)
+        mv_next = jnp.minimum(v_next, 0.0)
+        for b in range(nb):
+            q = f_ref[b, lev]
+            q_prev = pltpu.roll(q, 1, 0)
+            q_next = pltpu.roll(q, rows - 1, 0)
+            q_w = pltpu.roll(q, 1, 1)
+            q_e = pltpu.roll(q, cols - 1, 1)
+            fxp = pu * q + mu_next * q_next
+            fxm = pu_prev * q_prev + mu * q
+            fyp = pv * q + mv_next * q_e
+            fym = pv_prev * q_w + mv * q
+            o_ref[b, lev] = q - (fxp - fxm) - (fyp - fym)
+
+
+def open_step(f, w):
+    nsp, nlev, rows, cols = f.shape
+    main = pl.BlockSpec((SB, nlev, rows, cols), lambda i: (i, 0, 0, 0))
+    return pl.pallas_call(
+        open_kernel,
+        grid=(nsp // SB,),
+        in_specs=[main, pl.BlockSpec(w.shape, lambda i: (0, 0, 0, 0))],
+        out_specs=main,
+        out_shape=jax.ShapeDtypeStruct(f.shape, f.dtype),
+        cost_estimate=pl.CostEstimate(flops=20 * f.size, bytes_accessed=4 * (2 * f.size + w.size),
+                                      transcendentals=0),
+    )(f, w)
+
+
+def fix_kernel(emit, s_ref, ftop_ref, fbot_ref, wtop_ref, wbot_ref, fleft_ref, fright_ref,
+               wleft_ref, wright_ref, o_ref, *edge_refs):
+    nb, nlev, rows, cols = s_ref.shape
+    row = lax.broadcasted_iota(jnp.int32, (rows, cols), 0)
+    lane = lax.broadcasted_iota(jnp.int32, (rows, cols), 1)
+    first_row = row == 0
+    last_row = row == rows - 1
+    first_lane = lane == 0
+    last_lane = lane == cols - 1
+
+    def to_first(x, lev):
+        return pltpu.roll(x, (cols - lev) % cols, 1) if lev else x
+
+    def to_last(x, lev):
+        sh = (cols - 1 - lev) % cols
+        return pltpu.roll(x, sh, 1) if sh else x
+
+    if emit:
+        rf_ref, rl_ref, cf_ref, cl_ref = edge_refs
+    wl = wleft_ref[1]
+    wr = wright_ref[1]
+    for b in range(nb):
+        acc_f = jnp.zeros((rows, cols), jnp.float32)
+        acc_l = jnp.zeros((rows, cols), jnp.float32)
+        fl = fleft_ref[b]
+        fr = fright_ref[b]
+        for lev in range(nlev):
+            x = s_ref[b, lev]
+            top = jnp.maximum(wtop_ref[0, pl.ds(lev, 1), :], 0.0) * ftop_ref[b, pl.ds(lev, 1), :]
+            bot = jnp.minimum(wbot_ref[0, pl.ds(lev, 1), :], 0.0) * fbot_ref[b, pl.ds(lev, 1), :]
+            left = jnp.maximum(to_first(wl, lev), 0.0) * to_first(fl, lev)
+            right = jnp.minimum(to_last(wr, lev), 0.0) * to_last(fr, lev)
+            x = jnp.where(first_row, x + top, x)
+            x = jnp.where(last_row, x - bot, x)
+            x = jnp.where(first_lane, x + left, x)
+            x = jnp.where(last_lane, x - right, x)
+            o_ref[b, lev] = x
+            if emit:
+                rf_ref[b, pl.ds(lev, 1), :] = x[0:1, :]
+                rl_ref[b, pl.ds(lev, 1), :] = x[rows - 1:rows, :]
+                at_lev = lane == lev
+                acc_f = jnp.where(at_lev, pltpu.roll(x, lev, 1) if lev else x, acc_f)
+                acc_l = jnp.where(at_lev, pltpu.roll(x, (lev + 1) % cols, 1), acc_l)
+        if emit:
+            cf_ref[b] = acc_f
+            cl_ref[b] = acc_l
+
+
+def fix_step(s, ftop, fbot, wtop, wbot, fleft, fright, wleft, wright, emit):
+    nsp, nlev, rows, cols = s.shape
+    main = pl.BlockSpec((SB, nlev, rows, cols), lambda i: (i, 0, 0, 0))
+    rowspec = pl.BlockSpec((SB, nlev, cols), lambda i: (i, 0, 0))
+    colspec = pl.BlockSpec((SB, rows, cols), lambda i: (i, 0, 0))
+    wrowspec = pl.BlockSpec((2, nlev, cols), lambda i: (wtop.shape[0] // 2 - 1, 0, 0))
+    wcolspec = pl.BlockSpec((2, rows, cols), lambda i: (wleft.shape[0] // 2 - 1, 0, 0))
+    out_shape = [jax.ShapeDtypeStruct(s.shape, s.dtype)]
+    out_specs = [main]
+    if emit:
+        out_shape += [jax.ShapeDtypeStruct((nsp, nlev, cols), s.dtype)] * 2
+        out_shape += [jax.ShapeDtypeStruct((nsp, rows, cols), s.dtype)] * 2
+        out_specs += [rowspec, rowspec, colspec, colspec]
+    return pl.pallas_call(
+        functools.partial(fix_kernel, emit),
+        grid=(nsp // SB,),
+        in_specs=[main, rowspec, rowspec, wrowspec, wrowspec, colspec, colspec, wcolspec, wcolspec],
+        out_specs=out_specs,
+        out_shape=out_shape,
+        input_output_aliases={0: 0},
+        cost_estimate=pl.CostEstimate(flops=8 * s.size, bytes_accessed=8 * s.size, transcendentals=0),
+    )(s, ftop, fbot, wtop, wbot, fleft, fright, wleft, wright)
+
+
 def advection(tracers, wind_courant):
     cols_axes = ("mp", "gy")
     rf, rl, cf, cl = edges(tracers, wind_courant)
     top, bot = exchange(rf, rl, "gx")
     left, right = exchange(cf, cl, cols_axes)
-    mid = advect_step(tracers, wind_courant, top, bot, top, bot, left, right, left, right)
-    srf, srl, scf, scl = edges(mid)
+    mid = open_step(tracers, wind_courant)
+    mid, srf, srl, scf, scl = fix_step(mid, top, bot, top, bot, left, right, left, right, True)
     stop, sbot = exchange(srf, srl, "gx")
     sleft, sright = exchange(scf, scl, cols_axes)
-    return advect_step(mid, wind_courant, stop, sbot, top, bot, sleft, sright, left, right)
+    out = open_step(mid, wind_courant)
+    (out,) = fix_step(out, stop, sbot, top, bot, sleft, sright, left, right, False)
+    return out
 
 
 def padded_2(block, sides, width):

time: 150 us -> 213 us (1.42)
  Pallas kernels: 50.3 us -> 116 us
  waiting for transfers between devices: 30.5 us -> 22.2 us
  starting transfers between devices: 55.7 us -> 59.5 us
    pallas_call x2 -> x4, Pallas kernels: 31.3 us -> 106 us  [the longest x2 81.8 us: fix_step(): pl.pallas_call(functools.partial(fix_kernel, emit), grid=(nsp // SB,), in...]
    pallas_call x2 -> x1, Pallas kernels: 19 us -> 9.99 us  [edges(): pl.pallas_call(functools.partial(edge_kernel, nmain), grid=(total // nb,)...]
    ppermute x10, waiting for transfers between devices: 15.9 us -> 10.1 us  [exchange(): after = lax.ppermute(first, axes, shift_pairs(n, -1))]
    ppermute x10, starting transfers between devices: 21.6 us -> 26.1 us  [exchange(): before = lax.ppermute(last, axes, shift_pairs(n, 1))]
    ppermute x10, waiting for transfers between devices: 14.6 us -> 12 us  [exchange(): before = lax.ppermute(last, axes, shift_pairs(n, 1))]
  transfers between devices with their start and end apart: 20 -> 20, of which waited for: 6 -> 3; matrix products, arithmetic and copies ran while one was open for 1% -> 0% of each run, Pallas kernels for 17% -> 45%
where the time goes in v4:
time: 213 us; the launch traced here: 212 us
  Pallas kernels  116 us (54%)
  starting transfers between devices  59.5 us (28%)
  waiting for transfers between devices  22.2 us (10%)
  blocking collectives  5.09 us (2%)
  local copies, waits for them, and re-layouts  3.94 us (2%)
  other arithmetic  3.25 us (2%)
    pallas_call x2, Pallas kernels, fix_step(): pl.pallas_call(functools.partial(fix_kernel, emit), grid=(nsp // SB,), in...  81.8 us
    ppermute x10, starting transfers between devices, exchange(): after = lax.ppermute(first, axes, shift_pairs(n, -1))  33.4 us
    ppermute x10, starting transfers between devices, exchange(): before = lax.ppermute(last, axes, shift_pairs(n, 1))  26.1 us
    pallas_call x2, Pallas kernels, open_step(): pl.pallas_call(open_kernel, grid=(nsp // SB,), in_specs=[main, pl.BlockSp...  24.6 us
    ppermute x10, waiting for transfers between devices, exchange(): before = lax.ppermute(last, axes, shift_pairs(n, 1))  12 us
    ppermute x10, waiting for transfers between devices, exchange(): after = lax.ppermute(first, axes, shift_pairs(n, -1))  10.1 us
    pallas_call x1, Pallas kernels, edges(): pl.pallas_call(functools.partial(edge_kernel, nmain), grid=(total // nb,)...  9.99 us
    all_to_all x1, blocking collectives, on_device(): lax.all_to_all(forcing_fields(advected), 'gy', split_axis=1, concat_axis=...  5.09 us
  transfers between devices with their start and end apart: 20, of which 3 were waited for; matrix products, arithmetic and copies ran while one was open for 0% of the time, Pallas kernels for 45%

profile of v4, /device:TPU:31, one launch (start us, length us, event | category | flops | bytes accessed | tf_op | source)
XLA Modules:
  0.0 211.6 jit_solution(6249544463448090356)
XLA Ops:
  0.7 10.0 %shard_map.96 = (f32[18,60,128]{2,1,0:T(8,128)}, f32[18,60,128]{2,1,0:T(8,128)}, f32[18,16,128]{2,1,0:T(8,128)}, f32[18,16,128]{2,1,0:T(8,128)}) custom-call(f32[16,60,16,128]{3,2,1,0:T(8,128)} %f_ref.3, f32[2,60,16,128]{3,2,1,0:T(8,128)} %w_ref.3), custom_call_target="tpu_custom_call" | custom-call | flops 8847360 | bytes 8847360 | tf_op jit(solution)/shard_map/pallas_call | solution.py:69
  10.7 3.4 %collective-permute-start = (f32[18,60,128]{2,1,0:T(8,128)}, f32[18,60,128]{2,1,0:T(8,128)S(1)}, u32[]{:S(2)}, u32[]{:S(2)}) collective-permute-start(f32[18,60,128]{2,1,0:T(8,128)} %get-tuple-element.11), channel_id=1, source_target_pairs={{0,2},{2,4},{4,6},{6,8},{8,10},{10,12},{12,14},{14,16},{16,18},{18... | collective-permute-start | bytes 1658888 | tf_op jit(solution)/shard_map/ppermute | solution.py:147
  14.1 1.9 collective-permute-start.1
  16.0 1.3 collective-permute-start.2
  17.4 0.1 select_reduce_fusion.1
  17.5 0.1 fusion.70
  17.6 1.3 collective-permute-start.8
  18.9 6.5 %collective-permute-start.11 = (f32[10,8,1]{2,1,0:T(8,128)S(1)}, f32[10,8,1]{2,1,0:T(8,128)S(1)}, u32[]{:S(2)}, u32[]{:S(2)}) collective-permute-start(f32[10,8,1]{2,1,0:T(8,128)S(1)} %get-tuple-element.32), channel_id=1, source_target_pairs={{64,0},{65,1},{66,2},{67,3},{68,4},{69,5},{70,6},{71,7},{72,8},{73... | collective-permute-start | bytes 968 | tf_op jit(solution)/shard_map/ppermute | solution.py:148
  25.4 12.0 %collective-permute-done.8 = f32[10,8,1]{2,1,0:T(8,128)S(1)} collective-permute-done((f32[10,8,1]{2,1,0:T(8,128)S(1)}, f32[10,8,1]{2,1,0:T(8,128)S(1)}, u32[]{:S(2)}, u32[]{:S(2)}) %collective-permute-start.8) | collective-permute-done | bytes 352 | tf_op jit(solution)/shard_map/ppermute | solution.py:147
  37.4 1.3 collective-permute-start.3
  38.7 0.0 collective-permute-done.11
  38.7 2.5 %collective-permute-start.10 = (f32[10,1,256]{2,1,0:T(1,128)S(1)}, f32[10,1,256]{2,1,0:T(1,128)S(1)}, u32[]{:S(2)}, u32[]{:S(2)}) collective-permute-start(f32[10,1,256]{2,1,0:T(1,128)S(1)} %get-tuple-element.30), channel_id=1, source_target_pairs={{1,0},{2,1},{3,2},{4,3},{5,4},{6,5},{7,6},{8,7},{9,8},{10,9},{11,1... | collective-permute-start | bytes 30728 | tf_op jit(solution)/shard_map/ppermute | solution.py:148
  41.2 0.0 collective-permute-done.2.fleft_ref.wleft_ref
  41.2 5.2 %collective-permute-start.9 = (f32[10,1,256]{2,1,0:T(1,128)S(1)}, f32[10,1,256]{2,1,0:T(1,128)S(1)}, u32[]{:S(2)}, u32[]{:S(2)}) collective-permute-start(f32[10,1,256]{2,1,0:T(1,128)S(1)} %get-tuple-element.29), channel_id=1, source_target_pairs={{0,1},{1,2},{2,3},{3,4},{4,5},{5,6},{6,7},{7,8},{8,9},{9,10},{10,1... | collective-permute-start | bytes 30728 | tf_op jit(solution)/shard_map/ppermute | solution.py:147
  46.5 12.3 %shard_map.95.s_ref = f32[16,60,16,128]{3,2,1,0:T(8,128)} custom-call(f32[16,60,16,128]{3,2,1,0:T(8,128)} %f_ref.3, f32[2,60,16,128]{3,2,1,0:T(8,128)} %w_ref.3), custom_call_target="tpu_custom_call" | custom-call | flops 39321600 | bytes 16711680 | tf_op jit(solution)/shard_map/pallas_call | solution.py:191
  58.8 0.0 collective-permute-done.3.fright_ref.wright_ref
  58.9 0.6 copy-done.4
  59.5 0.3 copy-done
  59.7 0.8 copy-done.1
  60.6 70.4 %shard_map.97 = (f32[16,60,16,128]{3,2,1,0:T(8,128)}, f32[16,60,128]{2,1,0:T(8,128)}, f32[16,60,128]{2,1,0:T(8,128)}, f32[16,16,128]{2,1,0:T(8,128)}, f32[16,16,128]{2,1,0:T(8,128)}) custom-call(f32[16,60,16,128]{3,2,1,0:T(8,128)} %shard_map.95.s_ref, f32[18,60,128]{2,1,0:T(8,128)} %copy-done, ...), custom_call_target="tpu_custom_call", output_to_operand_aliasing={{0}: (0, {})} | custom-call | flops 15728640 | bytes 15728640 | tf_op jit(solution)/shard_map/pallas_call | solution.py:263
  130.9 1.9 collective-permute-start.4
  132.8 3.4 %collective-permute-start.5 = (f32[16,60,128]{2,1,0:T(8,128)}, f32[16,60,128]{2,1,0:T(8,128)S(1)}, u32[]{:S(2)}, u32[]{:S(2)}) collective-permute-start(f32[16,60,128]{2,1,0:T(8,128)} %get-tuple-element.17), channel_id=1, source_target_pairs={{2,0},{4,2},{6,4},{8,6},{10,8},{12,10},{14,12},{16,14},{18,16},{20... | collective-permute-start | bytes 1474568 | tf_op jit(solution)/shard_map/ppermute | solution.py:148
  136.2 0.0 collective-permute-done.9
  136.2 0.1 maximum_bitcast_fusion.1
  136.3 0.2 fusion.3
  136.5 0.1 slice.312
  136.6 1.3 collective-permute-start.6
  137.9 3.0 %collective-permute-start.7 = (f32[16,16,128]{2,1,0:T(8,128)}, f32[16,16,128]{2,1,0:T(8,128)S(1)}, u32[]{:S(2)}, u32[]{:S(2)}) collective-permute-start(f32[16,16,128]{2,1,0:T(8,128)} %get-tuple-element.19), channel_id=1, source_target_pairs={{1,0},{64,1},{65,64},{3,2},{66,3},{67,66},{5,4},{68,5},{69,68},{7,... | collective-permute-start | bytes 393224 | tf_op jit(solution)/shard_map/ppermute | solution.py:148
  141.0 0.1 fusion.58
  141.1 12.3 %shard_map.98.s_ref = f32[16,60,16,128]{3,2,1,0:T(8,128)} custom-call(f32[16,60,16,128]{3,2,1,0:T(8,128)} %get-tuple-element.15.f_ref, f32[2,60,16,128]{3,2,1,0:T(8,128)} %w_ref.3), custom_call_target="tpu_custom_call" | custom-call | flops 39321600 | bytes 16711680 | tf_op jit(solution)/shard_map/pallas_call | solution.py:191
  153.3 0.0 collective-permute-done.6.fleft_ref
  153.3 0.0 collective-permute-done.7.fright_ref
  153.4 0.0 collective-permute-done.5.fbot_ref
  153.4 0.6 copy-done.8
  154.0 0.0 copy-done.9
  154.0 0.2 copy-done.6
  154.2 0.8 copy-done.7
  155.0 11.5 %shard_map.99 = f32[16,60,16,128]{3,2,1,0:T(8,128)} custom-call(f32[16,60,16,128]{3,2,1,0:T(8,128)} %shard_map.98.s_ref, f32[16,60,128]{2,1,0:T(8,128)} %copy-done.6, f32[16,60,128]{2,1,0:T(8,128)} %copy-done.7, f32[18,60,128]{2,1,0:T(8,128)} %copy-done, f32[18,60,128]{2,1,0:T(8,128)} %copy-done.1, ...), custom_call_target="tpu_custom_call", output_to_operand_aliasing={{}: (0, {})} | custom-call | flops 15728640 | bytes 15728640 | tf_op jit(solution)/shard_map/pallas_call | solution.py:263
  166.5 0.8 compare_select_fusion.17
  167.3 5.1 %all_to_all.15 = f32[3,16,128]{2,0,1:T(4,128)S(1)} all-to-all(f32[3,16,128]{2,0,1:T(4,128)S(1)} %copy.14), channel_id=1, replica_groups=mesh['mp'=2,'gx'=32,'gy'=2] {'gy'}, dimensions={1} | all-to-all | bytes 49152 | tf_op jit(solution)/shard_map/all_to_all | solution.py:374
  172.4 0.2 fusion.12
  172.7 0.1 fusion.75
  172.8 1.3 collective-permute-start.12
  174.1 5.5 %collective-permute-start.15 = (f32[8,8,1]{2,1,0:T(8,128)S(1)}, f32[8,8,1]{2,1,0:T(8,128)S(1)}, u32[]{:S(2)}, u32[]{:S(2)}) collective-permute-start(f32[8,8,1]{2,1,0:T(8,128)S(1)} %get-tuple-element.42), channel_id=1, source_target_pairs={{64,0},{65,1},{66,2},{67,3},{68,4},{69,5},{70,6},{71,7},{72,8},{73... | collective-permute-start | bytes 776 | tf_op jit(solution)/shard_map/ppermute | solution.py:148
  179.6 6.5 %collective-permute-start.13 = (f32[8,1,256]{2,1,0:T(1,128)S(1)}, f32[8,1,256]{2,1,0:T(1,128)S(1)}, u32[]{:S(2)}, u32[]{:S(2)}) collective-permute-start(f32[8,1,256]{2,1,0:T(1,128)S(1)} %get-tuple-element.43), channel_id=1, source_target_pairs={{0,1},{1,2},{2,3},{3,4},{4,5},{5,6},{6,7},{7,8},{8,9},{9,10},{10,1... | collective-permute-start | bytes 24584 | tf_op jit(solution)/shard_map/ppermute | solution.py:147
  186.1 1.9 collective-permute-start.14
  188.1 0.0 collective-permute-done.12
  188.1 5.1 %collective-permute-done.14 = f32[8,1,256]{2,1,0:T(1,128)S(1)} collective-permute-done((f32[8,1,256]{2,1,0:T(1,128)S(1)}, f32[8,1,256]{2,1,0:T(1,128)S(1)}, u32[]{:S(2)}, u32[]{:S(2)}) %collective-permute-start.14) | collective-permute-done | bytes 8224 | tf_op jit(solution)/shard_map/ppermute | solution.py:148
  193.2 0.2 fusion.6
  193.4 0.1 fusion.59
  193.5 0.1 slice.326
  193.6 0.2 fusion.15
  193.8 0.1 fusion.72
  193.9 1.3 collective-permute-start.16
  195.2 5.5 %collective-permute-start.19 = (f32[8,8,1]{2,1,0:T(8,128)S(1)}, f32[8,8,1]{2,1,0:T(8,128)S(1)}, u32[]{:S(2)}, u32[]{:S(2)}) collective-permute-start(f32[8,8,1]{2,1,0:T(8,128)S(1)} %get-tuple-element.36), channel_id=1, source_target_pairs={{64,0},{65,1},{66,2},{67,3},{68,4},{69,5},{70,6},{71,7},{72,8},{73... | collective-permute-start | bytes 776 | tf_op jit(solution)/shard_map/ppermute | solution.py:148
  200.7 2.5 %collective-permute-start.17 = (f32[8,1,256]{2,1,0:T(1,128)S(1)}, f32[8,1,256]{2,1,0:T(1,128)S(1)}, u32[]{:S(2)}, u32[]{:S(2)}) collective-permute-start(f32[8,1,256]{2,1,0:T(1,128)S(1)} %get-tuple-element.37), channel_id=1, source_target_pairs={{0,1},{1,2},{2,3},{3,4},{4,5},{5,6},{6,7},{7,8},{8,9},{9,10},{10,1... | collective-permute-start | bytes 24584 | tf_op jit(solution)/shard_map/ppermute | solution.py:147
  203.2 1.9 collective-permute-start.18
  205.2 0.0 collective-permute-done.16
  205.2 0.0 collective-permute-done.19
  205.3 5.1 %collective-permute-done.18 = f32[8,1,256]{2,1,0:T(1,128)S(1)} collective-permute-done((f32[8,1,256]{2,1,0:T(1,128)S(1)}, f32[8,1,256]{2,1,0:T(1,128)S(1)}, u32[]{:S(2)}, u32[]{:S(2)}) %collective-permute-start.18) | collective-permute-done | bytes 8224 | tf_op jit(solution)/shard_map/ppermute | solution.py:148
  210.3 0.2 fusion.9
  210.5 0.1 fusion.60
  210.6 0.1 slice.340
  210.7 0.9 fusion.18
  (45 shorter events, 0.2 us)
Async XLA Ops:
  0.6 16.7 %copy-start.10 = (s32[8,256]{1,0:T(8,128)S(1)}, s32[8,256]{1,0:T(8,128)}, u32[]{:S(2)}) copy-start(s32[8,256]{1,0:T(8,128)} %param.12) | copy-start | bytes 24580
  0.6 16.7 %copy-start.12 = (f32[12]{0:T(128)S(1)}, f32[12]{0:T(128)}, u32[]{:S(2)}) copy-start(f32[12]{0:T(128)} %param.14) | copy-start | bytes 148
  0.7 16.7 %copy-start.13 = (f32[12]{0:T(128)S(1)}, f32[12]{0:T(128)}, u32[]{:S(2)}) copy-start(f32[12]{0:T(128)} %param.15) | copy-start | bytes 148
  0.7 16.8 %copy-start.2 = (f32[8,8,256]{2,1,0:T(8,128)S(1)}, f32[8,8,256]{2,1,0:T(8,128)}, u32[]{:S(2)}) copy-start(f32[8,8,256]{2,1,0:T(8,128)} %param.10) | copy-start | bytes 196612
  10.7 48.2 %collective-permute-start = (f32[18,60,128]{2,1,0:T(8,128)}, f32[18,60,128]{2,1,0:T(8,128)S(1)}, u32[]{:S(2)}, u32[]{:S(2)}) collective-permute-start(f32[18,60,128]{2,1,0:T(8,128)} %get-tuple-element.11), channel_id=1, source_target_pairs={{0,2},{2,4},{4,6},{6,8},{8,10},{10,12},{12,14},{14,16},{16,18},{18... | collective-permute-start | bytes 1658888 | tf_op jit(solution)/shard_map/ppermute | solution.py:147
  14.1 44.7 %collective-permute-start.1 = (f32[18,60,128]{2,1,0:T(8,128)}, f32[18,60,128]{2,1,0:T(8,128)S(1)}, u32[]{:S(2)}, u32[]{:S(2)}) collective-permute-start(f32[18,60,128]{2,1,0:T(8,128)} %get-tuple-element.12), channel_id=1, source_target_pairs={{2,0},{4,2},{6,4},{8,6},{10,8},{12,10},{14,12},{16,14},{18,16},{20... | collective-permute-start | bytes 1658888 | tf_op jit(solution)/shard_map/ppermute | solution.py:148
  16.0 25.2 %collective-permute-start.2 = (f32[18,16,128]{2,1,0:T(8,128)}, f32[18,16,128]{2,1,0:T(8,128)S(1)}, u32[]{:S(2)}, u32[]{:S(2)}) collective-permute-start(f32[18,16,128]{2,1,0:T(8,128)} %get-tuple-element.13), channel_id=1, source_target_pairs={{0,1},{1,64},{64,65},{2,3},{3,66},{66,67},{4,5},{5,68},{68,69},{6,... | collective-permute-start | bytes 442376 | tf_op jit(solution)/shard_map/ppermute | solution.py:147
  17.6 19.9 %collective-permute-start.8 = (f32[10,8,1]{2,1,0:T(8,128)S(1)}, f32[10,8,1]{2,1,0:T(8,128)S(1)}, u32[]{:S(2)}, u32[]{:S(2)}) collective-permute-start(f32[10,8,1]{2,1,0:T(8,128)S(1)} %get-tuple-element.31), channel_id=1, source_target_pairs={{0,64},{1,65},{2,66},{3,67},{4,68},{5,69},{6,70},{7,71},{8,72},{9,... | collective-permute-start | bytes 968 | tf_op jit(solution)/shard_map/ppermute | solution.py:147
  18.9 19.9 %collective-permute-start.11 = (f32[10,8,1]{2,1,0:T(8,128)S(1)}, f32[10,8,1]{2,1,0:T(8,128)S(1)}, u32[]{:S(2)}, u32[]{:S(2)}) collective-permute-start(f32[10,8,1]{2,1,0:T(8,128)S(1)} %get-tuple-element.32), channel_id=1, source_target_pairs={{64,0},{65,1},{66,2},{67,3},{68,4},{69,5},{70,6},{71,7},{72,8},{73... | collective-permute-start | bytes 968 | tf_op jit(solution)/shard_map/ppermute | solution.py:148
  37.4 21.4 %collective-permute-start.3 = (f32[18,16,128]{2,1,0:T(8,128)}, f32[18,16,128]{2,1,0:T(8,128)S(1)}, u32[]{:S(2)}, u32[]{:S(2)}) collective-permute-start(f32[18,16,128]{2,1,0:T(8,128)} %get-tuple-element.14), channel_id=1, source_target_pairs={{1,0},{64,1},{65,64},{3,2},{66,3},{67,66},{5,4},{68,5},{69,68},{7,... | collective-permute-start | bytes 442376 | tf_op jit(solution)/shard_map/ppermute | solution.py:148
  38.7 97.5 %collective-permute-start.10 = (f32[10,1,256]{2,1,0:T(1,128)S(1)}, f32[10,1,256]{2,1,0:T(1,128)S(1)}, u32[]{:S(2)}, u32[]{:S(2)}) collective-permute-start(f32[10,1,256]{2,1,0:T(1,128)S(1)} %get-tuple-element.30), channel_id=1, source_target_pairs={{1,0},{2,1},{3,2},{4,3},{5,4},{6,5},{7,6},{8,7},{9,8},{10,9},{11,1... | collective-permute-start | bytes 30728 | tf_op jit(solution)/shard_map/ppermute | solution.py:148
  41.2 17.5 %copy-start.3 = (f32[18,16,128]{2,1,0:T(8,128)}, f32[18,16,128]{2,1,0:T(8,128)S(1)}, u32[]{:S(2)}) copy-start(f32[18,16,128]{2,1,0:T(8,128)S(1)} %collective-permute-done.2.fleft_ref.wleft_ref) | copy-start | bytes 442372
  41.2 95.0 %collective-permute-start.9 = (f32[10,1,256]{2,1,0:T(1,128)S(1)}, f32[10,1,256]{2,1,0:T(1,128)S(1)}, u32[]{:S(2)}, u32[]{:S(2)}) collective-permute-start(f32[10,1,256]{2,1,0:T(1,128)S(1)} %get-tuple-element.29), channel_id=1, source_target_pairs={{0,1},{1,2},{2,3},{3,4},{4,5},{5,6},{6,7},{7,8},{8,9},{9,10},{10,1... | collective-permute-start | bytes 30728 | tf_op jit(solution)/shard_map/ppermute | solution.py:147
  58.8 0.6 copy-start.4
  58.8 0.9 copy-start
  59.7 0.8 copy-start.1
  130.9 22.4 %collective-permute-start.4 = (f32[16,60,128]{2,1,0:T(8,128)}, f32[16,60,128]{2,1,0:T(8,128)S(1)}, u32[]{:S(2)}, u32[]{:S(2)}) collective-permute-start(f32[16,60,128]{2,1,0:T(8,128)} %get-tuple-element.16), channel_id=1, source_target_pairs={{0,2},{2,4},{4,6},{6,8},{8,10},{10,12},{12,14},{14,16},{16,18},{18... | collective-permute-start | bytes 1474568 | tf_op jit(solution)/shard_map/ppermute | solution.py:147
  132.8 20.5 %collective-permute-start.5 = (f32[16,60,128]{2,1,0:T(8,128)}, f32[16,60,128]{2,1,0:T(8,128)S(1)}, u32[]{:S(2)}, u32[]{:S(2)}) collective-permute-start(f32[16,60,128]{2,1,0:T(8,128)} %get-tuple-element.17), channel_id=1, source_target_pairs={{2,0},{4,2},{6,4},{8,6},{10,8},{12,10},{14,12},{16,14},{18,16},{20... | collective-permute-start | bytes 1474568 | tf_op jit(solution)/shard_map/ppermute | solution.py:148
  136.6 16.7 %collective-permute-start.6 = (f32[16,16,128]{2,1,0:T(8,128)}, f32[16,16,128]{2,1,0:T(8,128)S(1)}, u32[]{:S(2)}, u32[]{:S(2)}) collective-permute-start(f32[16,16,128]{2,1,0:T(8,128)} %get-tuple-element.18), channel_id=1, source_target_pairs={{0,1},{1,64},{64,65},{2,3},{3,66},{66,67},{4,5},{5,68},{68,69},{6,... | collective-permute-start | bytes 393224 | tf_op jit(solution)/shard_map/ppermute | solution.py:147
  137.9 15.4 %collective-permute-start.7 = (f32[16,16,128]{2,1,0:T(8,128)}, f32[16,16,128]{2,1,0:T(8,128)S(1)}, u32[]{:S(2)}, u32[]{:S(2)}) collective-permute-start(f32[16,16,128]{2,1,0:T(8,128)} %get-tuple-element.19), channel_id=1, source_target_pairs={{1,0},{64,1},{65,64},{3,2},{66,3},{67,66},{5,4},{68,5},{69,68},{7,... | collective-permute-start | bytes 393224 | tf_op jit(solution)/shard_map/ppermute | solution.py:148
  153.3 19.1 %copy-start.11 = (s32[8,256]{1,0:T(8,128)S(1)}, s32[8,256]{1,0:T(8,128)}, u32[]{:S(2)}) copy-start(s32[8,256]{1,0:T(8,128)} %param.13) | copy-start | bytes 24580
  153.3 19.1 %copy-start.5 = (f32[8,8,256]{2,1,0:T(8,128)S(1)}, f32[8,8,256]{2,1,0:T(8,128)}, u32[]{:S(2)}) copy-start(f32[8,8,256]{2,1,0:T(8,128)} %param.11) | copy-start | bytes 196612
  153.3 0.7 copy-start.8
  153.3 0.7 copy-start.9
  153.4 0.8 copy-start.6
  154.2 0.8 copy-start.7
  172.8 15.3 %collective-permute-start.12 = (f32[8,8,1]{2,1,0:T(8,128)S(1)}, f32[8,8,1]{2,1,0:T(8,128)S(1)}, u32[]{:S(2)}, u32[]{:S(2)}) collective-permute-start(f32[8,8,1]{2,1,0:T(8,128)S(1)} %get-tuple-element.41), channel_id=1, source_target_pairs={{0,64},{1,65},{2,66},{3,67},{4,68},{5,69},{6,70},{7,71},{8,72},{9,... | collective-permute-start | bytes 776 | tf_op jit(solution)/shard_map/ppermute | solution.py:147
  174.1 14.0 %collective-permute-start.15 = (f32[8,8,1]{2,1,0:T(8,128)S(1)}, f32[8,8,1]{2,1,0:T(8,128)S(1)}, u32[]{:S(2)}, u32[]{:S(2)}) collective-permute-start(f32[8,8,1]{2,1,0:T(8,128)S(1)} %get-tuple-element.42), channel_id=1, source_target_pairs={{64,0},{65,1},{66,2},{67,3},{68,4},{69,5},{70,6},{71,7},{72,8},{73... | collective-permute-start | bytes 776 | tf_op jit(solution)/shard_map/ppermute | solution.py:148
  179.6 8.6 %collective-permute-start.13 = (f32[8,1,256]{2,1,0:T(1,128)S(1)}, f32[8,1,256]{2,1,0:T(1,128)S(1)}, u32[]{:S(2)}, u32[]{:S(2)}) collective-permute-start(f32[8,1,256]{2,1,0:T(1,128)S(1)} %get-tuple-element.43), channel_id=1, source_target_pairs={{0,1},{1,2},{2,3},{3,4},{4,5},{5,6},{6,7},{7,8},{8,9},{9,10},{10,1... | collective-permute-start | bytes 24584 | tf_op jit(solution)/shard_map/ppermute | solution.py:147
  186.1 7.1 %collective-permute-start.14 = (f32[8,1,256]{2,1,0:T(1,128)S(1)}, f32[8,1,256]{2,1,0:T(1,128)S(1)}, u32[]{:S(2)}, u32[]{:S(2)}) collective-permute-start(f32[8,1,256]{2,1,0:T(1,128)S(1)} %get-tuple-element.44), channel_id=1, source_target_pairs={{1,0},{2,1},{3,2},{4,3},{5,4},{6,5},{7,6},{8,7},{9,8},{10,9},{11,1... | collective-permute-start | bytes 24584 | tf_op jit(solution)/shard_map/ppermute | solution.py:148
  193.9 11.3 %collective-permute-start.16 = (f32[8,8,1]{2,1,0:T(8,128)S(1)}, f32[8,8,1]{2,1,0:T(8,128)S(1)}, u32[]{:S(2)}, u32[]{:S(2)}) collective-permute-start(f32[8,8,1]{2,1,0:T(8,128)S(1)} %get-tuple-element.35), channel_id=1, source_target_pairs={{0,64},{1,65},{2,66},{3,67},{4,68},{5,69},{6,70},{7,71},{8,72},{9,... | collective-permute-start | bytes 776 | tf_op jit(solution)/shard_map/ppermute | solution.py:147
  195.2 10.0 %collective-permute-start.19 = (f32[8,8,1]{2,1,0:T(8,128)S(1)}, f32[8,8,1]{2,1,0:T(8,128)S(1)}, u32[]{:S(2)}, u32[]{:S(2)}) collective-permute-start(f32[8,8,1]{2,1,0:T(8,128)S(1)} %get-tuple-element.36), channel_id=1, source_target_pairs={{64,0},{65,1},{66,2},{67,3},{68,4},{69,5},{70,6},{71,7},{72,8},{73... | collective-permute-start | bytes 776 | tf_op jit(solution)/shard_map/ppermute | solution.py:148
  200.7 4.5 %collective-permute-start.17 = (f32[8,1,256]{2,1,0:T(1,128)S(1)}, f32[8,1,256]{2,1,0:T(1,128)S(1)}, u32[]{:S(2)}, u32[]{:S(2)}) collective-permute-start(f32[8,1,256]{2,1,0:T(1,128)S(1)} %get-tuple-element.37), channel_id=1, source_target_pairs={{0,1},{1,2},{2,3},{3,4},{4,5},{5,6},{6,7},{7,8},{8,9},{9,10},{10,1... | collective-permute-start | bytes 24584 | tf_op jit(solution)/shard_map/ppermute | solution.py:147
  203.2 7.1 %collective-permute-start.18 = (f32[8,1,256]{2,1,0:T(1,128)S(1)}, f32[8,1,256]{2,1,0:T(1,128)S(1)}, u32[]{:S(2)}, u32[]{:S(2)}) collective-permute-start(f32[8,1,256]{2,1,0:T(1,128)S(1)} %get-tuple-element.38), channel_id=1, source_target_pairs={{1,0},{2,1},{3,2},{4,3},{5,4},{6,5},{7,6},{8,7},{9,8},{10,9},{11,1... | collective-permute-start | bytes 24584 | tf_op jit(solution)/shard_map/ppermute | solution.py:148

commit v5 on v4

--- a/solution.py
+++ b/solution.py
@@ -277,7 +277,8 @@
     top, bot = exchange(rf, rl, "gx")
     left, right = exchange(cf, cl, cols_axes)
     mid = open_step(tracers, wind_courant)
-    mid, srf, srl, scf, scl = fix_step(mid, top, bot, top, bot, left, right, left, right, True)
+    (mid,) = fix_step(mid, top, bot, top, bot, left, right, left, right, False)
+    srf, srl, scf, scl = edges(mid)
     stop, sbot = exchange(srf, srl, "gx")
     sleft, sright = exchange(scf, scl, cols_axes)
     out = open_step(mid, wind_courant)

time: 213 us -> 164 us (0.77)
  Pallas kernels: 116 us -> 66.5 us
    pallas_call x2, Pallas kernels: 81.8 us -> 23 us  [fix_step(): pl.pallas_call(functools.partial(fix_kernel, emit), grid=(nsp // SB,), in...]
    pallas_call x1 -> x2, Pallas kernels: 9.99 us -> 19 us  [edges(): pl.pallas_call(functools.partial(edge_kernel, nmain), grid=(total // nb,)...]
  transfers between devices with their start and end apart: 20 -> 20, of which waited for: 3 -> 3; matrix products, arithmetic and copies ran while one was open for 0% -> 0% of each run, Pallas kernels for 45% -> 28%
where the time goes in v5:
time: 164 us; the launch traced here: 162 us
  Pallas kernels  66.5 us (41%)
  starting transfers between devices  59.5 us (36%)
  waiting for transfers between devices  22.2 us (14%)
  blocking collectives  5.09 us (3%)
  local copies, waits for them, and re-layouts  3.94 us (2%)
  other arithmetic  3.25 us (2%)
    ppermute x10, starting transfers between devices, exchange(): after = lax.ppermute(first, axes, shift_pairs(n, -1))  33.4 us
    ppermute x10, starting transfers between devices, exchange(): before = lax.ppermute(last, axes, shift_pairs(n, 1))  26 us
    pallas_call x2, Pallas kernels, open_step(): pl.pallas_call(open_kernel, grid=(nsp // SB,), in_specs=[main, pl.BlockSp...  24.6 us
    pallas_call x2, Pallas kernels, fix_step(): pl.pallas_call(functools.partial(fix_kernel, emit), grid=(nsp // SB,), in...  23 us
    pallas_call x2, Pallas kernels, edges(): pl.pallas_call(functools.partial(edge_kernel, nmain), grid=(total // nb,)...  19 us
    ppermute x10, waiting for transfers between devices, exchange(): before = lax.ppermute(last, axes, shift_pairs(n, 1))  12 us
    ppermute x10, waiting for transfers between devices, exchange(): after = lax.ppermute(first, axes, shift_pairs(n, -1))  10.1 us
    all_to_all x1, blocking collectives, on_device(): lax.all_to_all(forcing_fields(advected), 'gy', split_axis=1, concat_axis=...  5.09 us
  transfers between devices with their start and end apart: 20, of which 3 were waited for; matrix products, arithmetic and copies ran while one was open for 0% of the time, Pallas kernels for 28%

profile of v5, /device:TPU:31, one launch (start us, length us, event | category | flops | bytes accessed | tf_op | source)
XLA Modules:
  0.0 161.7 jit_solution(7185502842695047215)
XLA Ops:
  0.7 10.0 %shard_map.96 = (f32[18,60,128]{2,1,0:T(8,128)}, f32[18,60,128]{2,1,0:T(8,128)}, f32[18,16,128]{2,1,0:T(8,128)}, f32[18,16,128]{2,1,0:T(8,128)}) custom-call(f32[16,60,16,128]{3,2,1,0:T(8,128)} %f_ref.3, f32[2,60,16,128]{3,2,1,0:T(8,128)} %w_ref.3), custom_call_target="tpu_custom_call" | custom-call | flops 8847360 | bytes 8847360 | tf_op jit(solution)/shard_map/pallas_call | solution.py:69
  10.7 3.4 %collective-permute-start = (f32[18,60,128]{2,1,0:T(8,128)}, f32[18,60,128]{2,1,0:T(8,128)S(1)}, u32[]{:S(2)}, u32[]{:S(2)}) collective-permute-start(f32[18,60,128]{2,1,0:T(8,128)} %get-tuple-element.10), channel_id=1, source_target_pairs={{0,2},{2,4},{4,6},{6,8},{8,10},{10,12},{12,14},{14,16},{16,18},{18... | collective-permute-start | bytes 1658888 | tf_op jit(solution)/shard_map/ppermute | solution.py:147
  14.1 1.9 %collective-permute-start.1 = (f32[18,60,128]{2,1,0:T(8,128)}, f32[18,60,128]{2,1,0:T(8,128)S(1)}, u32[]{:S(2)}, u32[]{:S(2)}) collective-permute-start(f32[18,60,128]{2,1,0:T(8,128)} %get-tuple-element.11), channel_id=1, source_target_pairs={{2,0},{4,2},{6,4},{8,6},{10,8},{12,10},{14,12},{16,14},{18,16},{20... | collective-permute-start | bytes 1658888 | tf_op jit(solution)/shard_map/ppermute | solution.py:148
  16.0 1.3 collective-permute-start.2
  17.4 0.1 select_reduce_fusion.1
  17.5 0.1 fusion.70
  17.6 1.3 collective-permute-start.8
  18.9 6.5 %collective-permute-start.11 = (f32[10,8,1]{2,1,0:T(8,128)S(1)}, f32[10,8,1]{2,1,0:T(8,128)S(1)}, u32[]{:S(2)}, u32[]{:S(2)}) collective-permute-start(f32[10,8,1]{2,1,0:T(8,128)S(1)} %get-tuple-element.30), channel_id=1, source_target_pairs={{64,0},{65,1},{66,2},{67,3},{68,4},{69,5},{70,6},{71,7},{72,8},{73... | collective-permute-start | bytes 968 | tf_op jit(solution)/shard_map/ppermute | solution.py:148
  25.4 12.0 %collective-permute-done.8 = f32[10,8,1]{2,1,0:T(8,128)S(1)} collective-permute-done((f32[10,8,1]{2,1,0:T(8,128)S(1)}, f32[10,8,1]{2,1,0:T(8,128)S(1)}, u32[]{:S(2)}, u32[]{:S(2)}) %collective-permute-start.8) | collective-permute-done | bytes 352 | tf_op jit(solution)/shard_map/ppermute | solution.py:147
  37.4 1.3 collective-permute-start.3
  38.7 2.5 %collective-permute-start.10 = (f32[10,1,256]{2,1,0:T(1,128)S(1)}, f32[10,1,256]{2,1,0:T(1,128)S(1)}, u32[]{:S(2)}, u32[]{:S(2)}) collective-permute-start(f32[10,1,256]{2,1,0:T(1,128)S(1)} %get-tuple-element.28), channel_id=1, source_target_pairs={{1,0},{2,1},{3,2},{4,3},{5,4},{6,5},{7,6},{8,7},{9,8},{10,9},{11,1... | collective-permute-start | bytes 30728 | tf_op jit(solution)/shard_map/ppermute | solution.py:148
  41.2 5.2 %collective-permute-start.9 = (f32[10,1,256]{2,1,0:T(1,128)S(1)}, f32[10,1,256]{2,1,0:T(1,128)S(1)}, u32[]{:S(2)}, u32[]{:S(2)}) collective-permute-start(f32[10,1,256]{2,1,0:T(1,128)S(1)} %get-tuple-element.27), channel_id=1, source_target_pairs={{0,1},{1,2},{2,3},{3,4},{4,5},{5,6},{6,7},{7,8},{8,9},{9,10},{10,1... | collective-permute-start | bytes 30728 | tf_op jit(solution)/shard_map/ppermute | solution.py:147
  46.5 12.3 %shard_map.95.s_ref = f32[16,60,16,128]{3,2,1,0:T(8,128)} custom-call(f32[16,60,16,128]{3,2,1,0:T(8,128)} %f_ref.3, f32[2,60,16,128]{3,2,1,0:T(8,128)} %w_ref.3), custom_call_target="tpu_custom_call" | custom-call | flops 39321600 | bytes 16711680 | tf_op jit(solution)/shard_map/pallas_call | solution.py:191
  58.8 0.0 collective-permute-done.3.fright_ref.wright_ref
  58.9 0.6 copy-done.4
  59.5 0.3 copy-done
  59.7 0.8 copy-done.1
  60.6 11.5 %shard_map.97.f_ref = f32[16,60,16,128]{3,2,1,0:T(8,128)} custom-call(f32[16,60,16,128]{3,2,1,0:T(8,128)} %shard_map.95.s_ref, f32[18,60,128]{2,1,0:T(8,128)} %copy-done, f32[18,60,128]{2,1,0:T(8,128)} %copy-done.1, f32[18,60,128]{2,1,0:T(8,128)} %copy-done, f32[18,60,128]{2,1,0:T(8,128)} %copy-done.1, ...), custom_call_target="tpu_custom_call", output_to_operand_aliasing={{}: (0, {})} | custom-call | flops 15728640 | bytes 15728640 | tf_op jit(solution)/shard_map/pallas_call | solution.py:263
  72.1 9.0 %shard_map.99 = (f32[16,60,128]{2,1,0:T(8,128)}, f32[16,60,128]{2,1,0:T(8,128)}, f32[16,16,128]{2,1,0:T(8,128)}, f32[16,16,128]{2,1,0:T(8,128)}) custom-call(f32[16,60,16,128]{3,2,1,0:T(8,128)} %shard_map.97.f_ref), custom_call_target="tpu_custom_call" | custom-call | flops 7864320 | bytes 7864320 | tf_op jit(solution)/shard_map/pallas_call | solution.py:69
  81.1 1.9 %collective-permute-start.4 = (f32[16,60,128]{2,1,0:T(8,128)}, f32[16,60,128]{2,1,0:T(8,128)S(1)}, u32[]{:S(2)}, u32[]{:S(2)}) collective-permute-start(f32[16,60,128]{2,1,0:T(8,128)} %get-tuple-element.14), channel_id=1, source_target_pairs={{0,2},{2,4},{4,6},{6,8},{8,10},{10,12},{12,14},{14,16},{16,18},{18... | collective-permute-start | bytes 1474568 | tf_op jit(solution)/shard_map/ppermute | solution.py:147
  83.0 3.4 %collective-permute-start.5 = (f32[16,60,128]{2,1,0:T(8,128)}, f32[16,60,128]{2,1,0:T(8,128)S(1)}, u32[]{:S(2)}, u32[]{:S(2)}) collective-permute-start(f32[16,60,128]{2,1,0:T(8,128)} %get-tuple-element.15), channel_id=1, source_target_pairs={{2,0},{4,2},{6,4},{8,6},{10,8},{12,10},{14,12},{16,14},{18,16},{20... | collective-permute-start | bytes 1474568 | tf_op jit(solution)/shard_map/ppermute | solution.py:148
  86.4 0.0 collective-permute-done.10
  86.4 0.0 collective-permute-done.9
  86.4 0.1 maximum_bitcast_fusion.1
  86.5 0.2 fusion.3
  86.7 0.1 slice.312
  86.8 1.3 collective-permute-start.6
  88.1 3.0 %collective-permute-start.7 = (f32[16,16,128]{2,1,0:T(8,128)}, f32[16,16,128]{2,1,0:T(8,128)S(1)}, u32[]{:S(2)}, u32[]{:S(2)}) collective-permute-start(f32[16,16,128]{2,1,0:T(8,128)} %get-tuple-element.17), channel_id=1, source_target_pairs={{1,0},{64,1},{65,64},{3,2},{66,3},{67,66},{5,4},{68,5},{69,68},{7,... | collective-permute-start | bytes 393224 | tf_op jit(solution)/shard_map/ppermute | solution.py:148
  91.1 0.1 fusion.58
  91.2 12.3 %shard_map.98.s_ref = f32[16,60,16,128]{3,2,1,0:T(8,128)} custom-call(f32[16,60,16,128]{3,2,1,0:T(8,128)} %shard_map.97.f_ref, f32[2,60,16,128]{3,2,1,0:T(8,128)} %w_ref.3), custom_call_target="tpu_custom_call" | custom-call | flops 39321600 | bytes 16711680 | tf_op jit(solution)/shard_map/pallas_call | solution.py:191
  103.5 0.0 collective-permute-done.6.fleft_ref
  103.5 0.0 collective-permute-done.4.ftop_ref
  103.5 0.0 collective-permute-done.5.fbot_ref
  103.5 0.6 copy-done.8
  104.1 0.0 copy-done.9
  104.2 0.2 copy-done.6
  104.4 0.8 copy-done.7
  105.2 11.5 %shard_map.100 = f32[16,60,16,128]{3,2,1,0:T(8,128)} custom-call(f32[16,60,16,128]{3,2,1,0:T(8,128)} %shard_map.98.s_ref, f32[16,60,128]{2,1,0:T(8,128)} %copy-done.6, f32[16,60,128]{2,1,0:T(8,128)} %copy-done.7, f32[18,60,128]{2,1,0:T(8,128)} %copy-done, f32[18,60,128]{2,1,0:T(8,128)} %copy-done.1, ...), custom_call_target="tpu_custom_call", output_to_operand_aliasing={{}: (0, {})} | custom-call | flops 15728640 | bytes 15728640 | tf_op jit(solution)/shard_map/pallas_call | solution.py:263
  116.6 0.8 compare_select_fusion.17
  117.5 5.1 %all_to_all.15 = f32[3,16,128]{2,0,1:T(4,128)S(1)} all-to-all(f32[3,16,128]{2,0,1:T(4,128)S(1)} %copy.14), channel_id=1, replica_groups=mesh['mp'=2,'gx'=32,'gy'=2] {'gy'}, dimensions={1} | all-to-all | bytes 49152 | tf_op jit(solution)/shard_map/all_to_all | solution.py:375
  122.6 0.2 fusion.12
  122.8 0.1 fusion.75
  122.9 1.3 collective-permute-start.12
  124.2 5.5 %collective-permute-start.15 = (f32[8,8,1]{2,1,0:T(8,128)S(1)}, f32[8,8,1]{2,1,0:T(8,128)S(1)}, u32[]{:S(2)}, u32[]{:S(2)}) collective-permute-start(f32[8,8,1]{2,1,0:T(8,128)S(1)} %get-tuple-element.40), channel_id=1, source_target_pairs={{64,0},{65,1},{66,2},{67,3},{68,4},{69,5},{70,6},{71,7},{72,8},{73... | collective-permute-start | bytes 776 | tf_op jit(solution)/shard_map/ppermute | solution.py:148
  129.7 6.5 %collective-permute-start.13 = (f32[8,1,256]{2,1,0:T(1,128)S(1)}, f32[8,1,256]{2,1,0:T(1,128)S(1)}, u32[]{:S(2)}, u32[]{:S(2)}) collective-permute-start(f32[8,1,256]{2,1,0:T(1,128)S(1)} %get-tuple-element.41), channel_id=1, source_target_pairs={{0,1},{1,2},{2,3},{3,4},{4,5},{5,6},{6,7},{7,8},{8,9},{9,10},{10,1... | collective-permute-start | bytes 24584 | tf_op jit(solution)/shard_map/ppermute | solution.py:147
  136.3 1.9 %collective-permute-start.14 = (f32[8,1,256]{2,1,0:T(1,128)S(1)}, f32[8,1,256]{2,1,0:T(1,128)S(1)}, u32[]{:S(2)}, u32[]{:S(2)}) collective-permute-start(f32[8,1,256]{2,1,0:T(1,128)S(1)} %get-tuple-element.42), channel_id=1, source_target_pairs={{1,0},{2,1},{3,2},{4,3},{5,4},{6,5},{7,6},{8,7},{9,8},{10,9},{11,1... | collective-permute-start | bytes 24584 | tf_op jit(solution)/shard_map/ppermute | solution.py:148
  138.2 0.0 collective-permute-done.12
  138.3 0.0 collective-permute-done.15
  138.3 5.1 %collective-permute-done.14 = f32[8,1,256]{2,1,0:T(1,128)S(1)} collective-permute-done((f32[8,1,256]{2,1,0:T(1,128)S(1)}, f32[8,1,256]{2,1,0:T(1,128)S(1)}, u32[]{:S(2)}, u32[]{:S(2)}) %collective-permute-start.14) | collective-permute-done | bytes 8224 | tf_op jit(solution)/shard_map/ppermute | solution.py:148
  143.4 0.2 fusion.6
  143.6 0.1 fusion.59
  143.7 0.1 slice.326
  143.8 0.2 fusion.15
  144.0 0.1 fusion.72
  144.1 1.3 collective-permute-start.16
  145.4 5.5 %collective-permute-start.19 = (f32[8,8,1]{2,1,0:T(8,128)S(1)}, f32[8,8,1]{2,1,0:T(8,128)S(1)}, u32[]{:S(2)}, u32[]{:S(2)}) collective-permute-start(f32[8,8,1]{2,1,0:T(8,128)S(1)} %get-tuple-element.34), channel_id=1, source_target_pairs={{64,0},{65,1},{66,2},{67,3},{68,4},{69,5},{70,6},{71,7},{72,8},{73... | collective-permute-start | bytes 776 | tf_op jit(solution)/shard_map/ppermute | solution.py:148
  150.9 2.5 %collective-permute-start.17 = (f32[8,1,256]{2,1,0:T(1,128)S(1)}, f32[8,1,256]{2,1,0:T(1,128)S(1)}, u32[]{:S(2)}, u32[]{:S(2)}) collective-permute-start(f32[8,1,256]{2,1,0:T(1,128)S(1)} %get-tuple-element.35), channel_id=1, source_target_pairs={{0,1},{1,2},{2,3},{3,4},{4,5},{5,6},{6,7},{7,8},{8,9},{9,10},{10,1... | collective-permute-start | bytes 24584 | tf_op jit(solution)/shard_map/ppermute | solution.py:147
  153.4 1.9 %collective-permute-start.18 = (f32[8,1,256]{2,1,0:T(1,128)S(1)}, f32[8,1,256]{2,1,0:T(1,128)S(1)}, u32[]{:S(2)}, u32[]{:S(2)}) collective-permute-start(f32[8,1,256]{2,1,0:T(1,128)S(1)} %get-tuple-element.36), channel_id=1, source_target_pairs={{1,0},{2,1},{3,2},{4,3},{5,4},{6,5},{7,6},{8,7},{9,8},{10,9},{11,1... | collective-permute-start | bytes 24584 | tf_op jit(solution)/shard_map/ppermute | solution.py:148
  155.4 0.0 collective-permute-done.19
  155.4 5.1 %collective-permute-done.18 = f32[8,1,256]{2,1,0:T(1,128)S(1)} collective-permute-done((f32[8,1,256]{2,1,0:T(1,128)S(1)}, f32[8,1,256]{2,1,0:T(1,128)S(1)}, u32[]{:S(2)}, u32[]{:S(2)}) %collective-permute-start.18) | collective-permute-done | bytes 8224 | tf_op jit(solution)/shard_map/ppermute | solution.py:148
  160.5 0.2 fusion.9
  160.7 0.1 fusion.60
  160.8 0.1 slice.340
  160.9 0.9 fusion.18
  (46 shorter events, 0.3 us)
Async XLA Ops:
  0.6 16.7 %copy-start.10 = (s32[8,256]{1,0:T(8,128)S(1)}, s32[8,256]{1,0:T(8,128)}, u32[]{:S(2)}) copy-start(s32[8,256]{1,0:T(8,128)} %param.12) | copy-start | bytes 24580
  0.6 16.7 %copy-start.12 = (f32[12]{0:T(128)S(1)}, f32[12]{0:T(128)}, u32[]{:S(2)}) copy-start(f32[12]{0:T(128)} %param.14) | copy-start | bytes 148
  0.7 16.7 %copy-start.13 = (f32[12]{0:T(128)S(1)}, f32[12]{0:T(128)}, u32[]{:S(2)}) copy-start(f32[12]{0:T(128)} %param.15) | copy-start | bytes 148
  0.7 16.8 %copy-start.2 = (f32[8,8,256]{2,1,0:T(8,128)S(1)}, f32[8,8,256]{2,1,0:T(8,128)}, u32[]{:S(2)}) copy-start(f32[8,8,256]{2,1,0:T(8,128)} %param.10) | copy-start | bytes 196612
  10.7 48.2 %collective-permute-start = (f32[18,60,128]{2,1,0:T(8,128)}, f32[18,60,128]{2,1,0:T(8,128)S(1)}, u32[]{:S(2)}, u32[]{:S(2)}) collective-permute-start(f32[18,60,128]{2,1,0:T(8,128)} %get-tuple-element.10), channel_id=1, source_target_pairs={{0,2},{2,4},{4,6},{6,8},{8,10},{10,12},{12,14},{14,16},{16,18},{18... | collective-permute-start | bytes 1658888 | tf_op jit(solution)/shard_map/ppermute | solution.py:147
  14.1 44.7 %collective-permute-start.1 = (f32[18,60,128]{2,1,0:T(8,128)}, f32[18,60,128]{2,1,0:T(8,128)S(1)}, u32[]{:S(2)}, u32[]{:S(2)}) collective-permute-start(f32[18,60,128]{2,1,0:T(8,128)} %get-tuple-element.11), channel_id=1, source_target_pairs={{2,0},{4,2},{6,4},{8,6},{10,8},{12,10},{14,12},{16,14},{18,16},{20... | collective-permute-start | bytes 1658888 | tf_op jit(solution)/shard_map/ppermute | solution.py:148
  16.0 25.2 %collective-permute-start.2 = (f32[18,16,128]{2,1,0:T(8,128)}, f32[18,16,128]{2,1,0:T(8,128)S(1)}, u32[]{:S(2)}, u32[]{:S(2)}) collective-permute-start(f32[18,16,128]{2,1,0:T(8,128)} %get-tuple-element.12), channel_id=1, source_target_pairs={{0,1},{1,64},{64,65},{2,3},{3,66},{66,67},{4,5},{5,68},{68,69},{6,... | collective-permute-start | bytes 442376 | tf_op jit(solution)/shard_map/ppermute | solution.py:147
  17.6 19.9 %collective-permute-start.8 = (f32[10,8,1]{2,1,0:T(8,128)S(1)}, f32[10,8,1]{2,1,0:T(8,128)S(1)}, u32[]{:S(2)}, u32[]{:S(2)}) collective-permute-start(f32[10,8,1]{2,1,0:T(8,128)S(1)} %get-tuple-element.29), channel_id=1, source_target_pairs={{0,64},{1,65},{2,66},{3,67},{4,68},{5,69},{6,70},{7,71},{8,72},{9,... | collective-permute-start | bytes 968 | tf_op jit(solution)/shard_map/ppermute | solution.py:147
  18.9 19.9 %collective-permute-start.11 = (f32[10,8,1]{2,1,0:T(8,128)S(1)}, f32[10,8,1]{2,1,0:T(8,128)S(1)}, u32[]{:S(2)}, u32[]{:S(2)}) collective-permute-start(f32[10,8,1]{2,1,0:T(8,128)S(1)} %get-tuple-element.30), channel_id=1, source_target_pairs={{64,0},{65,1},{66,2},{67,3},{68,4},{69,5},{70,6},{71,7},{72,8},{73... | collective-permute-start | bytes 968 | tf_op jit(solution)/shard_map/ppermute | solution.py:148
  37.4 21.4 %collective-permute-start.3 = (f32[18,16,128]{2,1,0:T(8,128)}, f32[18,16,128]{2,1,0:T(8,128)S(1)}, u32[]{:S(2)}, u32[]{:S(2)}) collective-permute-start(f32[18,16,128]{2,1,0:T(8,128)} %get-tuple-element.13), channel_id=1, source_target_pairs={{1,0},{64,1},{65,64},{3,2},{66,3},{67,66},{5,4},{68,5},{69,68},{7,... | collective-permute-start | bytes 442376 | tf_op jit(solution)/shard_map/ppermute | solution.py:148
  38.7 47.6 %collective-permute-start.10 = (f32[10,1,256]{2,1,0:T(1,128)S(1)}, f32[10,1,256]{2,1,0:T(1,128)S(1)}, u32[]{:S(2)}, u32[]{:S(2)}) collective-permute-start(f32[10,1,256]{2,1,0:T(1,128)S(1)} %get-tuple-element.28), channel_id=1, source_target_pairs={{1,0},{2,1},{3,2},{4,3},{5,4},{6,5},{7,6},{8,7},{9,8},{10,9},{11,1... | collective-permute-start | bytes 30728 | tf_op jit(solution)/shard_map/ppermute | solution.py:148
  41.2 17.5 %copy-start.3 = (f32[18,16,128]{2,1,0:T(8,128)}, f32[18,16,128]{2,1,0:T(8,128)S(1)}, u32[]{:S(2)}) copy-start(f32[18,16,128]{2,1,0:T(8,128)S(1)} %collective-permute-done.2.fleft_ref.wleft_ref) | copy-start | bytes 442372
  41.2 45.1 %collective-permute-start.9 = (f32[10,1,256]{2,1,0:T(1,128)S(1)}, f32[10,1,256]{2,1,0:T(1,128)S(1)}, u32[]{:S(2)}, u32[]{:S(2)}) collective-permute-start(f32[10,1,256]{2,1,0:T(1,128)S(1)} %get-tuple-element.27), channel_id=1, source_target_pairs={{0,1},{1,2},{2,3},{3,4},{4,5},{5,6},{6,7},{7,8},{8,9},{9,10},{10,1... | collective-permute-start | bytes 30728 | tf_op jit(solution)/shard_map/ppermute | solution.py:147
  58.8 0.6 copy-start.4
  58.8 0.9 copy-start
  59.7 0.8 copy-start.1
  81.1 22.4 %collective-permute-start.4 = (f32[16,60,128]{2,1,0:T(8,128)}, f32[16,60,128]{2,1,0:T(8,128)S(1)}, u32[]{:S(2)}, u32[]{:S(2)}) collective-permute-start(f32[16,60,128]{2,1,0:T(8,128)} %get-tuple-element.14), channel_id=1, source_target_pairs={{0,2},{2,4},{4,6},{6,8},{8,10},{10,12},{12,14},{14,16},{16,18},{18... | collective-permute-start | bytes 1474568 | tf_op jit(solution)/shard_map/ppermute | solution.py:147
  83.0 20.5 %collective-permute-start.5 = (f32[16,60,128]{2,1,0:T(8,128)}, f32[16,60,128]{2,1,0:T(8,128)S(1)}, u32[]{:S(2)}, u32[]{:S(2)}) collective-permute-start(f32[16,60,128]{2,1,0:T(8,128)} %get-tuple-element.15), channel_id=1, source_target_pairs={{2,0},{4,2},{6,4},{8,6},{10,8},{12,10},{14,12},{16,14},{18,16},{20... | collective-permute-start | bytes 1474568 | tf_op jit(solution)/shard_map/ppermute | solution.py:148
  86.8 16.7 %collective-permute-start.6 = (f32[16,16,128]{2,1,0:T(8,128)}, f32[16,16,128]{2,1,0:T(8,128)S(1)}, u32[]{:S(2)}, u32[]{:S(2)}) collective-permute-start(f32[16,16,128]{2,1,0:T(8,128)} %get-tuple-element.16), channel_id=1, source_target_pairs={{0,1},{1,64},{64,65},{2,3},{3,66},{66,67},{4,5},{5,68},{68,69},{6,... | collective-permute-start | bytes 393224 | tf_op jit(solution)/shard_map/ppermute | solution.py:147
  88.1 15.4 %collective-permute-start.7 = (f32[16,16,128]{2,1,0:T(8,128)}, f32[16,16,128]{2,1,0:T(8,128)S(1)}, u32[]{:S(2)}, u32[]{:S(2)}) collective-permute-start(f32[16,16,128]{2,1,0:T(8,128)} %get-tuple-element.17), channel_id=1, source_target_pairs={{1,0},{64,1},{65,64},{3,2},{66,3},{67,66},{5,4},{68,5},{69,68},{7,... | collective-permute-start | bytes 393224 | tf_op jit(solution)/shard_map/ppermute | solution.py:148
  103.5 19.1 %copy-start.11 = (s32[8,256]{1,0:T(8,128)S(1)}, s32[8,256]{1,0:T(8,128)}, u32[]{:S(2)}) copy-start(s32[8,256]{1,0:T(8,128)} %param.13) | copy-start | bytes 24580
  103.5 19.1 %copy-start.5 = (f32[8,8,256]{2,1,0:T(8,128)S(1)}, f32[8,8,256]{2,1,0:T(8,128)}, u32[]{:S(2)}) copy-start(f32[8,8,256]{2,1,0:T(8,128)} %param.11) | copy-start | bytes 196612
  103.5 0.7 copy-start.8
  103.5 0.7 copy-start.9
  103.5 0.8 copy-start.6
  104.4 0.8 copy-start.7
  122.9 15.3 %collective-permute-start.12 = (f32[8,8,1]{2,1,0:T(8,128)S(1)}, f32[8,8,1]{2,1,0:T(8,128)S(1)}, u32[]{:S(2)}, u32[]{:S(2)}) collective-permute-start(f32[8,8,1]{2,1,0:T(8,128)S(1)} %get-tuple-element.39), channel_id=1, source_target_pairs={{0,64},{1,65},{2,66},{3,67},{4,68},{5,69},{6,70},{7,71},{8,72},{9,... | collective-permute-start | bytes 776 | tf_op jit(solution)/shard_map/ppermute | solution.py:147
  124.2 14.0 %collective-permute-start.15 = (f32[8,8,1]{2,1,0:T(8,128)S(1)}, f32[8,8,1]{2,1,0:T(8,128)S(1)}, u32[]{:S(2)}, u32[]{:S(2)}) collective-permute-start(f32[8,8,1]{2,1,0:T(8,128)S(1)} %get-tuple-element.40), channel_id=1, source_target_pairs={{64,0},{65,1},{66,2},{67,3},{68,4},{69,5},{70,6},{71,7},{72,8},{73... | collective-permute-start | bytes 776 | tf_op jit(solution)/shard_map/ppermute | solution.py:148
  129.7 8.6 %collective-permute-start.13 = (f32[8,1,256]{2,1,0:T(1,128)S(1)}, f32[8,1,256]{2,1,0:T(1,128)S(1)}, u32[]{:S(2)}, u32[]{:S(2)}) collective-permute-start(f32[8,1,256]{2,1,0:T(1,128)S(1)} %get-tuple-element.41), channel_id=1, source_target_pairs={{0,1},{1,2},{2,3},{3,4},{4,5},{5,6},{6,7},{7,8},{8,9},{9,10},{10,1... | collective-permute-start | bytes 24584 | tf_op jit(solution)/shard_map/ppermute | solution.py:147
  136.3 7.1 %collective-permute-start.14 = (f32[8,1,256]{2,1,0:T(1,128)S(1)}, f32[8,1,256]{2,1,0:T(1,128)S(1)}, u32[]{:S(2)}, u32[]{:S(2)}) collective-permute-start(f32[8,1,256]{2,1,0:T(1,128)S(1)} %get-tuple-element.42), channel_id=1, source_target_pairs={{1,0},{2,1},{3,2},{4,3},{5,4},{6,5},{7,6},{8,7},{9,8},{10,9},{11,1... | collective-permute-start | bytes 24584 | tf_op jit(solution)/shard_map/ppermute | solution.py:148
  144.1 11.3 %collective-permute-start.16 = (f32[8,8,1]{2,1,0:T(8,128)S(1)}, f32[8,8,1]{2,1,0:T(8,128)S(1)}, u32[]{:S(2)}, u32[]{:S(2)}) collective-permute-start(f32[8,8,1]{2,1,0:T(8,128)S(1)} %get-tuple-element.33), channel_id=1, source_target_pairs={{0,64},{1,65},{2,66},{3,67},{4,68},{5,69},{6,70},{7,71},{8,72},{9,... | collective-permute-start | bytes 776 | tf_op jit(solution)/shard_map/ppermute | solution.py:147
  145.4 10.0 %collective-permute-start.19 = (f32[8,8,1]{2,1,0:T(8,128)S(1)}, f32[8,8,1]{2,1,0:T(8,128)S(1)}, u32[]{:S(2)}, u32[]{:S(2)}) collective-permute-start(f32[8,8,1]{2,1,0:T(8,128)S(1)} %get-tuple-element.34), channel_id=1, source_target_pairs={{64,0},{65,1},{66,2},{67,3},{68,4},{69,5},{70,6},{71,7},{72,8},{73... | collective-permute-start | bytes 776 | tf_op jit(solution)/shard_map/ppermute | solution.py:148
  150.9 4.5 %collective-permute-start.17 = (f32[8,1,256]{2,1,0:T(1,128)S(1)}, f32[8,1,256]{2,1,0:T(1,128)S(1)}, u32[]{:S(2)}, u32[]{:S(2)}) collective-permute-start(f32[8,1,256]{2,1,0:T(1,128)S(1)} %get-tuple-element.35), channel_id=1, source_target_pairs={{0,1},{1,2},{2,3},{3,4},{4,5},{5,6},{6,7},{7,8},{8,9},{9,10},{10,1... | collective-permute-start | bytes 24584 | tf_op jit(solution)/shard_map/ppermute | solution.py:147
  153.4 7.1 %collective-permute-start.18 = (f32[8,1,256]{2,1,0:T(1,128)S(1)}, f32[8,1,256]{2,1,0:T(1,128)S(1)}, u32[]{:S(2)}, u32[]{:S(2)}) collective-permute-start(f32[8,1,256]{2,1,0:T(1,128)S(1)} %get-tuple-element.36), channel_id=1, source_target_pairs={{1,0},{2,1},{3,2},{4,3},{5,4},{6,5},{7,6},{8,7},{9,8},{10,9},{11,1... | collective-permute-start | bytes 24584 | tf_op jit(solution)/shard_map/ppermute | solution.py:148

commit v6 on v1

--- a/solution.py
+++ b/solution.py
@@ -77,11 +77,12 @@
     )(*args)
 
 
-def step_kernel(f_ref, w_ref, ftop_ref, fbot_ref, wtop_ref, wbot_ref,
-                fleft_ref, fright_ref, wleft_ref, wright_ref, o_ref):
+def step_kernel(emit, f_ref, w_ref, ftop_ref, fbot_ref, wtop_ref, wbot_ref,
+                fleft_ref, fright_ref, wleft_ref, wright_ref, o_ref, *edge_refs):
     nb, nlev, rows, cols = f_ref.shape
     row = lax.broadcasted_iota(jnp.int32, (rows, cols), 0)
     lane = lax.broadcasted_iota(jnp.int32, (rows, cols), 1)
+    sub = lax.broadcasted_iota(jnp.int32, (8, cols), 0)
     first_row = row == 0
     last_row = row == rows - 1
     first_lane = lane == 0
@@ -91,9 +92,15 @@
         return pltpu.roll(x, (cols - lev) % cols, 1) if lev else x
 
     def to_last(x, lev):
-        s = (cols - 1 - lev) % cols
-        return pltpu.roll(x, s, 1) if s else x
-
+        sh = (cols - 1 - lev) % cols
+        return pltpu.roll(x, sh, 1) if sh else x
+
+    zero_tile = jnp.zeros((8, cols), jnp.float32)
+    zero_plane = jnp.zeros((rows, cols), jnp.float32)
+    acc_rf = [zero_tile] * nb
+    acc_rl = [zero_tile] * nb
+    acc_cf = [zero_plane] * nb
+    acc_cl = [zero_plane] * nb
     for lev in range(nlev):
         u = w_ref[0, lev]
         v = w_ref[1, lev]
@@ -109,6 +116,8 @@
         mv = jnp.minimum(v, 0.0)
         pv_prev = jnp.maximum(v_prev, 0.0)
         mv_next = jnp.minimum(v_next, 0.0)
+        at_lev = lane == lev
+        at_sub = sub == lev % 8
         for b in range(nb):
             q = f_ref[b, lev]
             q_prev = jnp.where(first_row, ftop_ref[b, pl.ds(lev, 1), :], pltpu.roll(q, 1, 0))
@@ -119,25 +128,49 @@
             fxm = pu_prev * q_prev + mu * q
             fyp = pv * q + mv_next * q_e
             fym = pv_prev * q_w + mv * q
-            o_ref[b, lev] = q - (fxp - fxm) - (fyp - fym)
-
-
-def advect_step(f, w, ftop, fbot, wtop, wbot, fleft, fright, wleft, wright):
+            new = q - (fxp - fxm) - (fyp - fym)
+            o_ref[b, lev] = new
+            if emit:
+                acc_rf[b] = jnp.where(at_sub, new[0:1, :], acc_rf[b])
+                acc_rl[b] = jnp.where(at_sub, new[rows - 1:rows, :], acc_rl[b])
+                acc_cf[b] = jnp.where(at_lev, pltpu.roll(new, lev, 1) if lev else new, acc_cf[b])
+                acc_cl[b] = jnp.where(at_lev, pltpu.roll(new, (lev + 1) % cols, 1), acc_cl[b])
+        if emit and (lev % 8 == 7 or lev == nlev - 1):
+            rf_ref, rl_ref = edge_refs[0], edge_refs[1]
+            base = (lev // 8) * 8
+            for b in range(nb):
+                rf_ref[b, base:base + 8, :] = acc_rf[b]
+                rl_ref[b, base:base + 8, :] = acc_rl[b]
+    if emit:
+        cf_ref, cl_ref = edge_refs[2], edge_refs[3]
+        for b in range(nb):
+            cf_ref[b] = acc_cf[b]
+            cl_ref[b] = acc_cl[b]
+
+
+def advect_step(f, w, ftop, fbot, wtop, wbot, fleft, fright, wleft, wright, emit=False):
     nsp, nlev, rows, cols = f.shape
     main = pl.BlockSpec((SB, nlev, rows, cols), lambda i: (i, 0, 0, 0))
-    rowspec = pl.BlockSpec((SB, nlev, cols), lambda i: (i, 0, 0))
+    rowspec = pl.BlockSpec((SB, ftop.shape[1], cols), lambda i: (i, 0, 0))
     colspec = pl.BlockSpec((SB, rows, cols), lambda i: (i, 0, 0))
     wblock = nsp // 2
-    wrowspec = pl.BlockSpec((2, nlev, cols), lambda i: (wblock, 0, 0))
+    wrowspec = pl.BlockSpec((2, wtop.shape[1], cols), lambda i: (wblock, 0, 0))
     wcolspec = pl.BlockSpec((2, rows, cols), lambda i: (wblock, 0, 0))
     nbytes = 4 * (2 * f.size + w.size)
+    out_shape = [jax.ShapeDtypeStruct(f.shape, f.dtype)]
+    out_specs = [main]
+    if emit:
+        padded_lev = ((nlev + 7) // 8) * 8
+        out_shape += [jax.ShapeDtypeStruct((nsp, padded_lev, cols), f.dtype)] * 2
+        out_shape += [jax.ShapeDtypeStruct((nsp, rows, cols), f.dtype)] * 2
+        out_specs += [pl.BlockSpec((SB, padded_lev, cols), lambda i: (i, 0, 0))] * 2 + [colspec] * 2
     return pl.pallas_call(
-        step_kernel,
+        functools.partial(step_kernel, emit),
         grid=(nsp // SB,),
         in_specs=[main, pl.BlockSpec(w.shape, lambda i: (0, 0, 0, 0)), rowspec, rowspec, wrowspec, wrowspec,
                   colspec, colspec, wcolspec, wcolspec],
-        out_specs=main,
-        out_shape=jax.ShapeDtypeStruct(f.shape, f.dtype),
+        out_specs=out_specs,
+        out_shape=out_shape,
         cost_estimate=pl.CostEstimate(flops=20 * f.size, bytes_accessed=nbytes, transcendentals=0),
     )(f, w, ftop, fbot, wtop, wbot, fleft, fright, wleft, wright)
 
@@ -154,11 +187,11 @@
     rf, rl, cf, cl = edges(tracers, wind_courant)
     top, bot = exchange(rf, rl, "gx")
     left, right = exchange(cf, cl, cols_axes)
-    mid = advect_step(tracers, wind_courant, top, bot, top, bot, left, right, left, right)
-    srf, srl, scf, scl = edges(mid)
+    mid, srf, srl, scf, scl = advect_step(tracers, wind_courant, top, bot, top, bot, left, right, left, right,
+                                          emit=True)
     stop, sbot = exchange(srf, srl, "gx")
     sleft, sright = exchange(scf, scl, cols_axes)
-    return advect_step(mid, wind_courant, stop, sbot, top, bot, sleft, sright, left, right)
+    return advect_step(mid, wind_courant, stop, sbot, top, bot, sleft, sright, left, right)[0]
 
 
 def padded_2(block, sides, width):

time: 150 us -> 208 us (1.39)
  Pallas kernels: 50.3 us -> 108 us
    pallas_call x2, Pallas kernels: 31.3 us -> 98.3 us  [advect_step(): pl.pallas_call(functools.partial(step_kernel, emit), grid=(nsp // SB,), i...]
    pallas_call x2 -> x1, Pallas kernels: 19 us -> 9.99 us  [edges(): pl.pallas_call(functools.partial(edge_kernel, nmain), grid=(total // nb,)...]
  transfers between devices with their start and end apart: 20 -> 20, of which waited for: 6 -> 6; matrix products, arithmetic and copies ran while one was open for 1% -> 0% of each run, Pallas kernels for 17% -> 40%
where the time goes in v6:
time: 208 us; the launch traced here: 207 us
  Pallas kernels  108 us (52%)
  starting transfers between devices  55.7 us (27%)
  waiting for transfers between devices  30.5 us (15%)
  blocking collectives  4.65 us (2%)
  other arithmetic  3.25 us (2%)
  local copies, waits for them, and re-layouts  3.11 us (1%)
    pallas_call x2, Pallas kernels, advect_step(): pl.pallas_call(functools.partial(step_kernel, emit), grid=(nsp // SB,), i...  98.3 us
    ppermute x10, starting transfers between devices, exchange(): after = lax.ppermute(first, axes, shift_pairs(n, -1))  34.2 us
    ppermute x10, starting transfers between devices, exchange(): before = lax.ppermute(last, axes, shift_pairs(n, 1))  21.6 us
    ppermute x10, waiting for transfers between devices, exchange(): after = lax.ppermute(first, axes, shift_pairs(n, -1))  15.9 us
    ppermute x10, waiting for transfers between devices, exchange(): before = lax.ppermute(last, axes, shift_pairs(n, 1))  14.6 us
    pallas_call x1, Pallas kernels, edges(): pl.pallas_call(functools.partial(edge_kernel, nmain), grid=(total // nb,)...  9.99 us
    all_to_all x1, blocking collectives, on_device(): lax.all_to_all(forcing_fields(advected), 'gy', split_axis=1, concat_axis=...  4.65 us
  transfers between devices with their start and end apart: 20, of which 6 were waited for; matrix products, arithmetic and copies ran while one was open for 0% of the time, Pallas kernels for 40%

profile of v6, /device:TPU:31, one launch (start us, length us, event | category | flops | bytes accessed | tf_op | source)
XLA Modules:
  0.0 206.7 jit_solution(5977019361544892490)
XLA Ops:
  0.7 10.0 %shard_map.95 = (f32[18,60,128]{2,1,0:T(8,128)}, f32[18,60,128]{2,1,0:T(8,128)}, f32[18,16,128]{2,1,0:T(8,128)}, f32[18,16,128]{2,1,0:T(8,128)}) custom-call(f32[16,60,16,128]{3,2,1,0:T(8,128)} %f_ref.3, f32[2,60,16,128]{3,2,1,0:T(8,128)} %w_ref.3), custom_call_target="tpu_custom_call" | custom-call | flops 8847360 | bytes 8847360 | tf_op jit(solution)/shard_map/pallas_call | solution.py:69
  10.7 3.4 %collective-permute-start = (f32[18,60,128]{2,1,0:T(8,128)}, f32[18,60,128]{2,1,0:T(8,128)S(1)}, u32[]{:S(2)}, u32[]{:S(2)}) collective-permute-start(f32[18,60,128]{2,1,0:T(8,128)} %get-tuple-element.11), channel_id=1, source_target_pairs={{0,2},{2,4},{4,6},{6,8},{8,10},{10,12},{12,14},{14,16},{16,18},{18... | collective-permute-start | bytes 1658888 | tf_op jit(solution)/shard_map/ppermute | solution.py:180
  14.1 1.9 collective-permute-start.1
  16.0 1.3 collective-permute-start.2
  17.4 0.1 select_reduce_fusion.1
  17.5 0.1 fusion.70
  17.6 1.3 collective-permute-start.8
  18.9 6.5 %collective-permute-start.11 = (f32[10,8,1]{2,1,0:T(8,128)S(1)}, f32[10,8,1]{2,1,0:T(8,128)S(1)}, u32[]{:S(2)}, u32[]{:S(2)}) collective-permute-start(f32[10,8,1]{2,1,0:T(8,128)S(1)} %get-tuple-element.32), channel_id=1, source_target_pairs={{64,0},{65,1},{66,2},{67,3},{68,4},{69,5},{70,6},{71,7},{72,8},{73... | collective-permute-start | bytes 968 | tf_op jit(solution)/shard_map/ppermute | solution.py:181
  25.4 12.0 %collective-permute-done.8 = f32[10,8,1]{2,1,0:T(8,128)S(1)} collective-permute-done((f32[10,8,1]{2,1,0:T(8,128)S(1)}, f32[10,8,1]{2,1,0:T(8,128)S(1)}, u32[]{:S(2)}, u32[]{:S(2)}) %collective-permute-start.8) | collective-permute-done | bytes 352 | tf_op jit(solution)/shard_map/ppermute | solution.py:180
  37.4 1.3 collective-permute-start.3
  38.7 0.0 collective-permute-done.11
  38.7 2.5 %collective-permute-start.10 = (f32[10,1,256]{2,1,0:T(1,128)S(1)}, f32[10,1,256]{2,1,0:T(1,128)S(1)}, u32[]{:S(2)}, u32[]{:S(2)}) collective-permute-start(f32[10,1,256]{2,1,0:T(1,128)S(1)} %get-tuple-element.30), channel_id=1, source_target_pairs={{1,0},{2,1},{3,2},{4,3},{5,4},{6,5},{7,6},{8,7},{9,8},{10,9},{11,1... | collective-permute-start | bytes 30728 | tf_op jit(solution)/shard_map/ppermute | solution.py:181
  41.2 0.0 collective-permute-done.2.fleft_ref.wleft_ref
  41.2 5.2 %collective-permute-start.9 = (f32[10,1,256]{2,1,0:T(1,128)S(1)}, f32[10,1,256]{2,1,0:T(1,128)S(1)}, u32[]{:S(2)}, u32[]{:S(2)}) collective-permute-start(f32[10,1,256]{2,1,0:T(1,128)S(1)} %get-tuple-element.29), channel_id=1, source_target_pairs={{0,1},{1,2},{2,3},{3,4},{4,5},{5,6},{6,7},{7,8},{8,9},{9,10},{10,1... | collective-permute-start | bytes 30728 | tf_op jit(solution)/shard_map/ppermute | solution.py:180
  46.5 0.0 collective-permute-done.3.fright_ref.wright_ref
  46.5 0.0 collective-permute-done.ftop_ref.wtop_ref
  46.6 0.0 collective-permute-done.1.fbot_ref.wbot_ref
  46.6 0.6 copy-done.4
  47.2 0.3 copy-done
  47.4 0.8 copy-done.1
  48.3 82.6 %shard_map.96 = (f32[16,60,16,128]{3,2,1,0:T(8,128)}, f32[16,64,128]{2,1,0:T(8,128)}, f32[16,64,128]{2,1,0:T(8,128)}, f32[16,16,128]{2,1,0:T(8,128)}, f32[16,16,128]{2,1,0:T(8,128)}) custom-call(f32[16,60,16,128]{3,2,1,0:T(8,128)} %f_ref.3, f32[2,60,16,128]{3,2,1,0:T(8,128)} %w_ref.3, f32[18,60,128]{2,1,0:T(8,128)} %copy-done, f32[18,60,128]{2,1,0:T(8,128)} %copy-done.1, ...), custom_call_target="tpu_custom_call" | custom-call | flops 39321600 | bytes 16711680 | tf_op jit(solution)/shard_map/pallas_call | solution.py:167
  130.9 1.9 collective-permute-start.4
  132.8 3.4 %collective-permute-start.5 = (f32[16,64,128]{2,1,0:T(8,128)}, f32[16,64,128]{2,1,0:T(8,128)S(1)}, u32[]{:S(2)}, u32[]{:S(2)}) collective-permute-start(f32[16,64,128]{2,1,0:T(8,128)} %get-tuple-element.17), channel_id=1, source_target_pairs={{2,0},{4,2},{6,4},{8,6},{10,8},{12,10},{14,12},{16,14},{18,16},{20... | collective-permute-start | bytes 1572872 | tf_op jit(solution)/shard_map/ppermute | solution.py:181
  136.2 0.0 collective-permute-done.10
  136.2 0.0 collective-permute-done.9
  136.2 0.1 maximum_bitcast_fusion.1
  136.3 0.2 fusion.3
  136.5 0.1 slice.312
  136.6 1.3 collective-permute-start.6
  137.9 3.0 %collective-permute-start.7 = (f32[16,16,128]{2,1,0:T(8,128)}, f32[16,16,128]{2,1,0:T(8,128)S(1)}, u32[]{:S(2)}, u32[]{:S(2)}) collective-permute-start(f32[16,16,128]{2,1,0:T(8,128)} %get-tuple-element.19), channel_id=1, source_target_pairs={{1,0},{64,1},{65,64},{3,2},{66,3},{67,66},{5,4},{68,5},{69,68},{7,... | collective-permute-start | bytes 393224 | tf_op jit(solution)/shard_map/ppermute | solution.py:181
  140.9 0.1 fusion.58
  141.0 0.0 collective-permute-done.6.fleft_ref
  141.0 1.0 collective-permute-done.7.fright_ref
  142.1 2.5 %collective-permute-done.4.ftop_ref = f32[16,64,128]{2,1,0:T(8,128)S(1)} collective-permute-done((f32[16,64,128]{2,1,0:T(8,128)}, f32[16,64,128]{2,1,0:T(8,128)S(1)}, u32[]{:S(2)}, u32[]{:S(2)}) %collective-permute-start.4) | collective-permute-done | bytes 524320 | tf_op jit(solution)/shard_map/ppermute | solution.py:180
  144.6 5.5 %collective-permute-done.5.fbot_ref = f32[16,64,128]{2,1,0:T(8,128)S(1)} collective-permute-done((f32[16,64,128]{2,1,0:T(8,128)}, f32[16,64,128]{2,1,0:T(8,128)S(1)}, u32[]{:S(2)}, u32[]{:S(2)}) %collective-permute-start.5) | collective-permute-done | bytes 524320 | tf_op jit(solution)/shard_map/ppermute | solution.py:181
  150.1 0.8 copy-done.7
  150.9 15.7 %shard_map.97 = f32[16,60,16,128]{3,2,1,0:T(8,128)} custom-call(f32[16,60,16,128]{3,2,1,0:T(8,128)} %get-tuple-element.15.f_ref, f32[2,60,16,128]{3,2,1,0:T(8,128)} %w_ref.3, f32[16,64,128]{2,1,0:T(8,128)} %copy-done.6, f32[16,64,128]{2,1,0:T(8,128)} %copy-done.7, f32[18,60,128]{2,1,0:T(8,128)} %copy-done, f32[18,60,128]{2,1,0:T(8,128)} %copy-done.1, ...), custom_call_target="tpu_custom_call" | custom-call | flops 39321600 | bytes 16711680 | tf_op jit(solution)/shard_map/pallas_call | solution.py:167
  166.6 0.8 compare_select_fusion.17
  167.4 4.7 %all_to_all.15 = f32[3,16,128]{2,0,1:T(4,128)S(1)} all-to-all(f32[3,16,128]{2,0,1:T(4,128)S(1)} %copy.12), channel_id=1, replica_groups=mesh['mp'=2,'gx'=32,'gy'=2] {'gy'}, dimensions={1} | all-to-all | bytes 49152 | tf_op jit(solution)/shard_map/all_to_all | solution.py:283
  172.1 0.2 fusion.12
  172.3 0.1 fusion.75
  172.4 1.3 collective-permute-start.12
  173.7 5.5 %collective-permute-start.15 = (f32[8,8,1]{2,1,0:T(8,128)S(1)}, f32[8,8,1]{2,1,0:T(8,128)S(1)}, u32[]{:S(2)}, u32[]{:S(2)}) collective-permute-start(f32[8,8,1]{2,1,0:T(8,128)S(1)} %get-tuple-element.42), channel_id=1, source_target_pairs={{64,0},{65,1},{66,2},{67,3},{68,4},{69,5},{70,6},{71,7},{72,8},{73... | collective-permute-start | bytes 776 | tf_op jit(solution)/shard_map/ppermute | solution.py:181
  179.2 2.1 %collective-permute-start.13 = (f32[8,1,256]{2,1,0:T(1,128)S(1)}, f32[8,1,256]{2,1,0:T(1,128)S(1)}, u32[]{:S(2)}, u32[]{:S(2)}) collective-permute-start(f32[8,1,256]{2,1,0:T(1,128)S(1)} %get-tuple-element.43), channel_id=1, source_target_pairs={{0,1},{1,2},{2,3},{3,4},{4,5},{5,6},{6,7},{7,8},{8,9},{9,10},{10,1... | collective-permute-start | bytes 24584 | tf_op jit(solution)/shard_map/ppermute | solution.py:180
  181.3 2.7 %collective-permute-start.14 = (f32[8,1,256]{2,1,0:T(1,128)S(1)}, f32[8,1,256]{2,1,0:T(1,128)S(1)}, u32[]{:S(2)}, u32[]{:S(2)}) collective-permute-start(f32[8,1,256]{2,1,0:T(1,128)S(1)} %get-tuple-element.44), channel_id=1, source_target_pairs={{1,0},{2,1},{3,2},{4,3},{5,4},{6,5},{7,6},{8,7},{9,8},{10,9},{11,1... | collective-permute-start | bytes 24584 | tf_op jit(solution)/shard_map/ppermute | solution.py:181
  184.0 0.0 collective-permute-done.12
  184.0 0.0 collective-permute-done.15
  184.1 4.3 %collective-permute-done.14 = f32[8,1,256]{2,1,0:T(1,128)S(1)} collective-permute-done((f32[8,1,256]{2,1,0:T(1,128)S(1)}, f32[8,1,256]{2,1,0:T(1,128)S(1)}, u32[]{:S(2)}, u32[]{:S(2)}) %collective-permute-start.14) | collective-permute-done | bytes 8224 | tf_op jit(solution)/shard_map/ppermute | solution.py:181
  188.4 0.2 fusion.6
  188.6 0.1 fusion.59
  188.7 0.1 slice.326
  188.8 0.2 fusion.15
  189.0 0.1 fusion.72
  189.1 1.3 collective-permute-start.16
  190.4 5.5 %collective-permute-start.19 = (f32[8,8,1]{2,1,0:T(8,128)S(1)}, f32[8,8,1]{2,1,0:T(8,128)S(1)}, u32[]{:S(2)}, u32[]{:S(2)}) collective-permute-start(f32[8,8,1]{2,1,0:T(8,128)S(1)} %get-tuple-element.36), channel_id=1, source_target_pairs={{64,0},{65,1},{66,2},{67,3},{68,4},{69,5},{70,6},{71,7},{72,8},{73... | collective-permute-start | bytes 776 | tf_op jit(solution)/shard_map/ppermute | solution.py:181
  195.9 2.5 %collective-permute-start.17 = (f32[8,1,256]{2,1,0:T(1,128)S(1)}, f32[8,1,256]{2,1,0:T(1,128)S(1)}, u32[]{:S(2)}, u32[]{:S(2)}) collective-permute-start(f32[8,1,256]{2,1,0:T(1,128)S(1)} %get-tuple-element.37), channel_id=1, source_target_pairs={{0,1},{1,2},{2,3},{3,4},{4,5},{5,6},{6,7},{7,8},{8,9},{9,10},{10,1... | collective-permute-start | bytes 24584 | tf_op jit(solution)/shard_map/ppermute | solution.py:180
  198.4 1.9 collective-permute-start.18
  200.4 0.0 collective-permute-done.19
  200.4 0.0 collective-permute-done.17
  200.4 5.1 %collective-permute-done.18 = f32[8,1,256]{2,1,0:T(1,128)S(1)} collective-permute-done((f32[8,1,256]{2,1,0:T(1,128)S(1)}, f32[8,1,256]{2,1,0:T(1,128)S(1)}, u32[]{:S(2)}, u32[]{:S(2)}) %collective-permute-start.18) | collective-permute-done | bytes 8224 | tf_op jit(solution)/shard_map/ppermute | solution.py:181
  205.5 0.2 fusion.9
  205.7 0.1 fusion.60
  205.8 0.1 slice.340
  205.9 0.9 fusion.18
  (43 shorter events, 0.2 us)
Async XLA Ops:
  0.6 16.7 %copy-start.10 = (s32[8,256]{1,0:T(8,128)S(1)}, s32[8,256]{1,0:T(8,128)}, u32[]{:S(2)}) copy-start(s32[8,256]{1,0:T(8,128)} %param.12) | copy-start | bytes 24580
  0.6 16.7 %copy-start.12 = (f32[12]{0:T(128)S(1)}, f32[12]{0:T(128)}, u32[]{:S(2)}) copy-start(f32[12]{0:T(128)} %param.14) | copy-start | bytes 148
  0.7 16.7 %copy-start.13 = (f32[12]{0:T(128)S(1)}, f32[12]{0:T(128)}, u32[]{:S(2)}) copy-start(f32[12]{0:T(128)} %param.15) | copy-start | bytes 148
  0.7 16.8 %copy-start.2 = (f32[8,8,256]{2,1,0:T(8,128)S(1)}, f32[8,8,256]{2,1,0:T(8,128)}, u32[]{:S(2)}) copy-start(f32[8,8,256]{2,1,0:T(8,128)} %param.10) | copy-start | bytes 196612
  10.7 35.9 %collective-permute-start = (f32[18,60,128]{2,1,0:T(8,128)}, f32[18,60,128]{2,1,0:T(8,128)S(1)}, u32[]{:S(2)}, u32[]{:S(2)}) collective-permute-start(f32[18,60,128]{2,1,0:T(8,128)} %get-tuple-element.11), channel_id=1, source_target_pairs={{0,2},{2,4},{4,6},{6,8},{8,10},{10,12},{12,14},{14,16},{16,18},{18... | collective-permute-start | bytes 1658888 | tf_op jit(solution)/shard_map/ppermute | solution.py:180
  14.1 32.4 %collective-permute-start.1 = (f32[18,60,128]{2,1,0:T(8,128)}, f32[18,60,128]{2,1,0:T(8,128)S(1)}, u32[]{:S(2)}, u32[]{:S(2)}) collective-permute-start(f32[18,60,128]{2,1,0:T(8,128)} %get-tuple-element.12), channel_id=1, source_target_pairs={{2,0},{4,2},{6,4},{8,6},{10,8},{12,10},{14,12},{16,14},{18,16},{20... | collective-permute-start | bytes 1658888 | tf_op jit(solution)/shard_map/ppermute | solution.py:181
  16.0 25.2 %collective-permute-start.2 = (f32[18,16,128]{2,1,0:T(8,128)}, f32[18,16,128]{2,1,0:T(8,128)S(1)}, u32[]{:S(2)}, u32[]{:S(2)}) collective-permute-start(f32[18,16,128]{2,1,0:T(8,128)} %get-tuple-element.13), channel_id=1, source_target_pairs={{0,1},{1,64},{64,65},{2,3},{3,66},{66,67},{4,5},{5,68},{68,69},{6,... | collective-permute-start | bytes 442376 | tf_op jit(solution)/shard_map/ppermute | solution.py:180
  17.6 19.9 %collective-permute-start.8 = (f32[10,8,1]{2,1,0:T(8,128)S(1)}, f32[10,8,1]{2,1,0:T(8,128)S(1)}, u32[]{:S(2)}, u32[]{:S(2)}) collective-permute-start(f32[10,8,1]{2,1,0:T(8,128)S(1)} %get-tuple-element.31), channel_id=1, source_target_pairs={{0,64},{1,65},{2,66},{3,67},{4,68},{5,69},{6,70},{7,71},{8,72},{9,... | collective-permute-start | bytes 968 | tf_op jit(solution)/shard_map/ppermute | solution.py:180
  18.9 19.9 %collective-permute-start.11 = (f32[10,8,1]{2,1,0:T(8,128)S(1)}, f32[10,8,1]{2,1,0:T(8,128)S(1)}, u32[]{:S(2)}, u32[]{:S(2)}) collective-permute-start(f32[10,8,1]{2,1,0:T(8,128)S(1)} %get-tuple-element.32), channel_id=1, source_target_pairs={{64,0},{65,1},{66,2},{67,3},{68,4},{69,5},{70,6},{71,7},{72,8},{73... | collective-permute-start | bytes 968 | tf_op jit(solution)/shard_map/ppermute | solution.py:181
  37.4 9.1 %collective-permute-start.3 = (f32[18,16,128]{2,1,0:T(8,128)}, f32[18,16,128]{2,1,0:T(8,128)S(1)}, u32[]{:S(2)}, u32[]{:S(2)}) collective-permute-start(f32[18,16,128]{2,1,0:T(8,128)} %get-tuple-element.14), channel_id=1, source_target_pairs={{1,0},{64,1},{65,64},{3,2},{66,3},{67,66},{5,4},{68,5},{69,68},{7,... | collective-permute-start | bytes 442376 | tf_op jit(solution)/shard_map/ppermute | solution.py:181
  38.7 97.4 %collective-permute-start.10 = (f32[10,1,256]{2,1,0:T(1,128)S(1)}, f32[10,1,256]{2,1,0:T(1,128)S(1)}, u32[]{:S(2)}, u32[]{:S(2)}) collective-permute-start(f32[10,1,256]{2,1,0:T(1,128)S(1)} %get-tuple-element.30), channel_id=1, source_target_pairs={{1,0},{2,1},{3,2},{4,3},{5,4},{6,5},{7,6},{8,7},{9,8},{10,9},{11,1... | collective-permute-start | bytes 30728 | tf_op jit(solution)/shard_map/ppermute | solution.py:181
  41.2 5.3 %copy-start.3 = (f32[18,16,128]{2,1,0:T(8,128)}, f32[18,16,128]{2,1,0:T(8,128)S(1)}, u32[]{:S(2)}) copy-start(f32[18,16,128]{2,1,0:T(8,128)S(1)} %collective-permute-done.2.fleft_ref.wleft_ref) | copy-start | bytes 442372
  41.2 94.9 %collective-permute-start.9 = (f32[10,1,256]{2,1,0:T(1,128)S(1)}, f32[10,1,256]{2,1,0:T(1,128)S(1)}, u32[]{:S(2)}, u32[]{:S(2)}) collective-permute-start(f32[10,1,256]{2,1,0:T(1,128)S(1)} %get-tuple-element.29), channel_id=1, source_target_pairs={{0,1},{1,2},{2,3},{3,4},{4,5},{5,6},{6,7},{7,8},{8,9},{9,10},{10,1... | collective-permute-start | bytes 30728 | tf_op jit(solution)/shard_map/ppermute | solution.py:180
  46.5 0.6 copy-start.4
  46.5 0.9 copy-start
  47.4 0.8 copy-start.1
  130.9 13.7 %collective-permute-start.4 = (f32[16,64,128]{2,1,0:T(8,128)}, f32[16,64,128]{2,1,0:T(8,128)S(1)}, u32[]{:S(2)}, u32[]{:S(2)}) collective-permute-start(f32[16,64,128]{2,1,0:T(8,128)} %get-tuple-element.16), channel_id=1, source_target_pairs={{0,2},{2,4},{4,6},{6,8},{8,10},{10,12},{12,14},{14,16},{16,18},{18... | collective-permute-start | bytes 1572872 | tf_op jit(solution)/shard_map/ppermute | solution.py:180
  132.8 17.3 %collective-permute-start.5 = (f32[16,64,128]{2,1,0:T(8,128)}, f32[16,64,128]{2,1,0:T(8,128)S(1)}, u32[]{:S(2)}, u32[]{:S(2)}) collective-permute-start(f32[16,64,128]{2,1,0:T(8,128)} %get-tuple-element.17), channel_id=1, source_target_pairs={{2,0},{4,2},{6,4},{8,6},{10,8},{12,10},{14,12},{16,14},{18,16},{20... | collective-permute-start | bytes 1572872 | tf_op jit(solution)/shard_map/ppermute | solution.py:181
  136.6 4.4 %collective-permute-start.6 = (f32[16,16,128]{2,1,0:T(8,128)}, f32[16,16,128]{2,1,0:T(8,128)S(1)}, u32[]{:S(2)}, u32[]{:S(2)}) collective-permute-start(f32[16,16,128]{2,1,0:T(8,128)} %get-tuple-element.18), channel_id=1, source_target_pairs={{0,1},{1,64},{64,65},{2,3},{3,66},{66,67},{4,5},{5,68},{68,69},{6,... | collective-permute-start | bytes 393224 | tf_op jit(solution)/shard_map/ppermute | solution.py:180
  137.9 4.2 %collective-permute-start.7 = (f32[16,16,128]{2,1,0:T(8,128)}, f32[16,16,128]{2,1,0:T(8,128)S(1)}, u32[]{:S(2)}, u32[]{:S(2)}) collective-permute-start(f32[16,16,128]{2,1,0:T(8,128)} %get-tuple-element.19), channel_id=1, source_target_pairs={{1,0},{64,1},{65,64},{3,2},{66,3},{67,66},{5,4},{68,5},{69,68},{7,... | collective-permute-start | bytes 393224 | tf_op jit(solution)/shard_map/ppermute | solution.py:181
  141.0 9.1 %copy-start.8 = (f32[16,16,128]{2,1,0:T(8,128)}, f32[16,16,128]{2,1,0:T(8,128)S(1)}, u32[]{:S(2)}) copy-start(f32[16,16,128]{2,1,0:T(8,128)S(1)} %collective-permute-done.6.fleft_ref) | copy-start | bytes 393220
  142.1 8.0 %copy-start.9 = (f32[16,16,128]{2,1,0:T(8,128)}, f32[16,16,128]{2,1,0:T(8,128)S(1)}, u32[]{:S(2)}) copy-start(f32[16,16,128]{2,1,0:T(8,128)S(1)} %collective-permute-done.7.fright_ref) | copy-start | bytes 393220
  144.6 5.5 %copy-start.6 = (f32[16,64,128]{2,1,0:T(8,128)}, f32[16,64,128]{2,1,0:T(8,128)S(1)}, u32[]{:S(2)}) copy-start(f32[16,64,128]{2,1,0:T(8,128)S(1)} %collective-permute-done.4.ftop_ref) | copy-start | bytes 1572868
  150.1 0.8 copy-start.7
  150.9 21.2 %copy-start.11 = (s32[8,256]{1,0:T(8,128)S(1)}, s32[8,256]{1,0:T(8,128)}, u32[]{:S(2)}) copy-start(s32[8,256]{1,0:T(8,128)} %param.13) | copy-start | bytes 24580
  150.9 21.2 %copy-start.5 = (f32[8,8,256]{2,1,0:T(8,128)S(1)}, f32[8,8,256]{2,1,0:T(8,128)}, u32[]{:S(2)}) copy-start(f32[8,8,256]{2,1,0:T(8,128)} %param.11) | copy-start | bytes 196612
  172.4 11.6 %collective-permute-start.12 = (f32[8,8,1]{2,1,0:T(8,128)S(1)}, f32[8,8,1]{2,1,0:T(8,128)S(1)}, u32[]{:S(2)}, u32[]{:S(2)}) collective-permute-start(f32[8,8,1]{2,1,0:T(8,128)S(1)} %get-tuple-element.41), channel_id=1, source_target_pairs={{0,64},{1,65},{2,66},{3,67},{4,68},{5,69},{6,70},{7,71},{8,72},{9,... | collective-permute-start | bytes 776 | tf_op jit(solution)/shard_map/ppermute | solution.py:180
  173.7 10.3 %collective-permute-start.15 = (f32[8,8,1]{2,1,0:T(8,128)S(1)}, f32[8,8,1]{2,1,0:T(8,128)S(1)}, u32[]{:S(2)}, u32[]{:S(2)}) collective-permute-start(f32[8,8,1]{2,1,0:T(8,128)S(1)} %get-tuple-element.42), channel_id=1, source_target_pairs={{64,0},{65,1},{66,2},{67,3},{68,4},{69,5},{70,6},{71,7},{72,8},{73... | collective-permute-start | bytes 776 | tf_op jit(solution)/shard_map/ppermute | solution.py:181
  179.2 4.8 %collective-permute-start.13 = (f32[8,1,256]{2,1,0:T(1,128)S(1)}, f32[8,1,256]{2,1,0:T(1,128)S(1)}, u32[]{:S(2)}, u32[]{:S(2)}) collective-permute-start(f32[8,1,256]{2,1,0:T(1,128)S(1)} %get-tuple-element.43), channel_id=1, source_target_pairs={{0,1},{1,2},{2,3},{3,4},{4,5},{5,6},{6,7},{7,8},{8,9},{9,10},{10,1... | collective-permute-start | bytes 24584 | tf_op jit(solution)/shard_map/ppermute | solution.py:180
  181.3 7.1 %collective-permute-start.14 = (f32[8,1,256]{2,1,0:T(1,128)S(1)}, f32[8,1,256]{2,1,0:T(1,128)S(1)}, u32[]{:S(2)}, u32[]{:S(2)}) collective-permute-start(f32[8,1,256]{2,1,0:T(1,128)S(1)} %get-tuple-element.44), channel_id=1, source_target_pairs={{1,0},{2,1},{3,2},{4,3},{5,4},{6,5},{7,6},{8,7},{9,8},{10,9},{11,1... | collective-permute-start | bytes 24584 | tf_op jit(solution)/shard_map/ppermute | solution.py:181
  189.1 11.3 %collective-permute-start.16 = (f32[8,8,1]{2,1,0:T(8,128)S(1)}, f32[8,8,1]{2,1,0:T(8,128)S(1)}, u32[]{:S(2)}, u32[]{:S(2)}) collective-permute-start(f32[8,8,1]{2,1,0:T(8,128)S(1)} %get-tuple-element.35), channel_id=1, source_target_pairs={{0,64},{1,65},{2,66},{3,67},{4,68},{5,69},{6,70},{7,71},{8,72},{9,... | collective-permute-start | bytes 776 | tf_op jit(solution)/shard_map/ppermute | solution.py:180
  190.4 10.0 %collective-permute-start.19 = (f32[8,8,1]{2,1,0:T(8,128)S(1)}, f32[8,8,1]{2,1,0:T(8,128)S(1)}, u32[]{:S(2)}, u32[]{:S(2)}) collective-permute-start(f32[8,8,1]{2,1,0:T(8,128)S(1)} %get-tuple-element.36), channel_id=1, source_target_pairs={{64,0},{65,1},{66,2},{67,3},{68,4},{69,5},{70,6},{71,7},{72,8},{73... | collective-permute-start | bytes 776 | tf_op jit(solution)/shard_map/ppermute | solution.py:181
  195.9 4.5 %collective-permute-start.17 = (f32[8,1,256]{2,1,0:T(1,128)S(1)}, f32[8,1,256]{2,1,0:T(1,128)S(1)}, u32[]{:S(2)}, u32[]{:S(2)}) collective-permute-start(f32[8,1,256]{2,1,0:T(1,128)S(1)} %get-tuple-element.37), channel_id=1, source_target_pairs={{0,1},{1,2},{2,3},{3,4},{4,5},{5,6},{6,7},{7,8},{8,9},{9,10},{10,1... | collective-permute-start | bytes 24584 | tf_op jit(solution)/shard_map/ppermute | solution.py:180
  198.4 7.1 %collective-permute-start.18 = (f32[8,1,256]{2,1,0:T(1,128)S(1)}, f32[8,1,256]{2,1,0:T(1,128)S(1)}, u32[]{:S(2)}, u32[]{:S(2)}) collective-permute-start(f32[8,1,256]{2,1,0:T(1,128)S(1)} %get-tuple-element.38), channel_id=1, source_target_pairs={{1,0},{2,1},{3,2},{4,3},{5,4},{6,5},{7,6},{8,7},{9,8},{10,9},{11,1... | collective-permute-start | bytes 24584 | tf_op jit(solution)/shard_map/ppermute | solution.py:181

commit v7 on v1

--- a/solution.py
+++ b/solution.py
@@ -7,7 +7,7 @@
 from jax.sharding import PartitionSpec as P
 
 SWEEPS = 3
-SB = 2
+SB = 4
 EB = 4
 
 

time: 150 us -> 146 us (0.973)
  Pallas kernels: 50.3 us -> 46.6 us
    pallas_call x2, Pallas kernels: 31.3 us -> 27.6 us  [advect_step(): pl.pallas_call(step_kernel, grid=(nsp // SB,), in_specs=[main, pl.BlockSp...]
  transfers between devices with their start and end apart: 20 -> 20, of which waited for: 6 -> 6; matrix products, arithmetic and copies ran while one was open for 1% -> 1% of each run, Pallas kernels for 17% -> 16%
where the time goes in v7:
time: 146 us; the launch traced here: 145 us
  starting transfers between devices  55.7 us (38%)
  Pallas kernels  46.6 us (32%)
  waiting for transfers between devices  30.5 us (21%)
  blocking collectives  4.65 us (3%)
  other arithmetic  3.25 us (2%)
  local copies, waits for them, and re-layouts  3.12 us (2%)
    ppermute x10, starting transfers between devices, exchange(): after = lax.ppermute(first, axes, shift_pairs(n, -1))  34.2 us
    pallas_call x2, Pallas kernels, advect_step(): pl.pallas_call(step_kernel, grid=(nsp // SB,), in_specs=[main, pl.BlockSp...  27.6 us
    ppermute x10, starting transfers between devices, exchange(): before = lax.ppermute(last, axes, shift_pairs(n, 1))  21.6 us
    pallas_call x2, Pallas kernels, edges(): pl.pallas_call(functools.partial(edge_kernel, nmain), grid=(total // nb,)...  19 us
    ppermute x10, waiting for transfers between devices, exchange(): after = lax.ppermute(first, axes, shift_pairs(n, -1))  15.9 us
    ppermute x10, waiting for transfers between devices, exchange(): before = lax.ppermute(last, axes, shift_pairs(n, 1))  14.6 us
    all_to_all x1, blocking collectives, on_device(): lax.all_to_all(forcing_fields(advected), 'gy', split_axis=1, concat_axis=...  4.65 us
  transfers between devices with their start and end apart: 20, of which 6 were waited for; matrix products, arithmetic and copies ran while one was open for 1% of the time, Pallas kernels for 16%

profile of v7, /device:TPU:31, one launch (start us, length us, event | category | flops | bytes accessed | tf_op | source)
XLA Modules:
  0.0 145.1 jit_solution(6934383557850080070)
XLA Ops:
  0.7 10.0 %shard_map.95 = (f32[18,60,128]{2,1,0:T(8,128)}, f32[18,60,128]{2,1,0:T(8,128)}, f32[18,16,128]{2,1,0:T(8,128)}, f32[18,16,128]{2,1,0:T(8,128)}) custom-call(f32[16,60,16,128]{3,2,1,0:T(8,128)} %f_ref.3, f32[2,60,16,128]{3,2,1,0:T(8,128)} %w_ref.3), custom_call_target="tpu_custom_call" | custom-call | flops 8847360 | bytes 8847360 | tf_op jit(solution)/shard_map/pallas_call | solution.py:69
  10.7 3.4 %collective-permute-start = (f32[18,60,128]{2,1,0:T(8,128)}, f32[18,60,128]{2,1,0:T(8,128)S(1)}, u32[]{:S(2)}, u32[]{:S(2)}) collective-permute-start(f32[18,60,128]{2,1,0:T(8,128)} %get-tuple-element.10), channel_id=1, source_target_pairs={{0,2},{2,4},{4,6},{6,8},{8,10},{10,12},{12,14},{14,16},{16,18},{18... | collective-permute-start | bytes 1658888 | tf_op jit(solution)/shard_map/ppermute | solution.py:147
  14.1 1.9 %collective-permute-start.1 = (f32[18,60,128]{2,1,0:T(8,128)}, f32[18,60,128]{2,1,0:T(8,128)S(1)}, u32[]{:S(2)}, u32[]{:S(2)}) collective-permute-start(f32[18,60,128]{2,1,0:T(8,128)} %get-tuple-element.11), channel_id=1, source_target_pairs={{2,0},{4,2},{6,4},{8,6},{10,8},{12,10},{14,12},{16,14},{18,16},{20... | collective-permute-start | bytes 1658888 | tf_op jit(solution)/shard_map/ppermute | solution.py:148
  16.0 1.3 collective-permute-start.2
  17.4 0.1 select_reduce_fusion.1
  17.5 0.1 fusion.70
  17.6 1.3 collective-permute-start.8
  18.9 6.5 %collective-permute-start.11 = (f32[10,8,1]{2,1,0:T(8,128)S(1)}, f32[10,8,1]{2,1,0:T(8,128)S(1)}, u32[]{:S(2)}, u32[]{:S(2)}) collective-permute-start(f32[10,8,1]{2,1,0:T(8,128)S(1)} %get-tuple-element.30), channel_id=1, source_target_pairs={{64,0},{65,1},{66,2},{67,3},{68,4},{69,5},{70,6},{71,7},{72,8},{73... | collective-permute-start | bytes 968 | tf_op jit(solution)/shard_map/ppermute | solution.py:148
  25.4 12.0 %collective-permute-done.8 = f32[10,8,1]{2,1,0:T(8,128)S(1)} collective-permute-done((f32[10,8,1]{2,1,0:T(8,128)S(1)}, f32[10,8,1]{2,1,0:T(8,128)S(1)}, u32[]{:S(2)}, u32[]{:S(2)}) %collective-permute-start.8) | collective-permute-done | bytes 352 | tf_op jit(solution)/shard_map/ppermute | solution.py:147
  37.4 1.3 collective-permute-start.3
  38.7 0.0 collective-permute-done.11
  38.7 2.5 %collective-permute-start.10 = (f32[10,1,256]{2,1,0:T(1,128)S(1)}, f32[10,1,256]{2,1,0:T(1,128)S(1)}, u32[]{:S(2)}, u32[]{:S(2)}) collective-permute-start(f32[10,1,256]{2,1,0:T(1,128)S(1)} %get-tuple-element.28), channel_id=1, source_target_pairs={{1,0},{2,1},{3,2},{4,3},{5,4},{6,5},{7,6},{8,7},{9,8},{10,9},{11,1... | collective-permute-start | bytes 30728 | tf_op jit(solution)/shard_map/ppermute | solution.py:148
  41.2 0.0 collective-permute-done.2.fleft_ref.wleft_ref
  41.2 5.2 %collective-permute-start.9 = (f32[10,1,256]{2,1,0:T(1,128)S(1)}, f32[10,1,256]{2,1,0:T(1,128)S(1)}, u32[]{:S(2)}, u32[]{:S(2)}) collective-permute-start(f32[10,1,256]{2,1,0:T(1,128)S(1)} %get-tuple-element.27), channel_id=1, source_target_pairs={{0,1},{1,2},{2,3},{3,4},{4,5},{5,6},{6,7},{7,8},{8,9},{9,10},{10,1... | collective-permute-start | bytes 30728 | tf_op jit(solution)/shard_map/ppermute | solution.py:147
  46.5 0.0 collective-permute-done.ftop_ref.wtop_ref
  46.6 0.0 collective-permute-done.1.fbot_ref.wbot_ref
  46.6 0.6 copy-done.4
  47.2 0.3 copy-done
  47.4 0.8 copy-done.1
  48.3 13.7 %shard_map.96.f_ref = f32[16,60,16,128]{3,2,1,0:T(8,128)} custom-call(f32[16,60,16,128]{3,2,1,0:T(8,128)} %f_ref.3, f32[2,60,16,128]{3,2,1,0:T(8,128)} %w_ref.3, f32[18,60,128]{2,1,0:T(8,128)} %copy-done, f32[18,60,128]{2,1,0:T(8,128)} %copy-done.1, f32[18,60,128]{2,1,0:T(8,128)} %copy-done, f32[18,60,128]{2,1,0:T(8,128)} %copy-done.1, ...), custom_call_target="tpu_custom_call" | custom-call | flops 39321600 | bytes 16711680 | tf_op jit(solution)/shard_map/pallas_call | solution.py:134
  62.0 9.0 %shard_map.97 = (f32[16,60,128]{2,1,0:T(8,128)}, f32[16,60,128]{2,1,0:T(8,128)}, f32[16,16,128]{2,1,0:T(8,128)}, f32[16,16,128]{2,1,0:T(8,128)}) custom-call(f32[16,60,16,128]{3,2,1,0:T(8,128)} %shard_map.96.f_ref), custom_call_target="tpu_custom_call" | custom-call | flops 7864320 | bytes 7864320 | tf_op jit(solution)/shard_map/pallas_call | solution.py:69
  71.0 1.9 %collective-permute-start.4 = (f32[16,60,128]{2,1,0:T(8,128)}, f32[16,60,128]{2,1,0:T(8,128)S(1)}, u32[]{:S(2)}, u32[]{:S(2)}) collective-permute-start(f32[16,60,128]{2,1,0:T(8,128)} %get-tuple-element.14), channel_id=1, source_target_pairs={{0,2},{2,4},{4,6},{6,8},{8,10},{10,12},{12,14},{14,16},{16,18},{18... | collective-permute-start | bytes 1474568 | tf_op jit(solution)/shard_map/ppermute | solution.py:147
  72.9 3.4 %collective-permute-start.5 = (f32[16,60,128]{2,1,0:T(8,128)}, f32[16,60,128]{2,1,0:T(8,128)S(1)}, u32[]{:S(2)}, u32[]{:S(2)}) collective-permute-start(f32[16,60,128]{2,1,0:T(8,128)} %get-tuple-element.15), channel_id=1, source_target_pairs={{2,0},{4,2},{6,4},{8,6},{10,8},{12,10},{14,12},{16,14},{18,16},{20... | collective-permute-start | bytes 1474568 | tf_op jit(solution)/shard_map/ppermute | solution.py:148
  76.3 0.0 collective-permute-done.10
  76.3 0.0 collective-permute-done.9
  76.3 0.1 maximum_bitcast_fusion.1
  76.4 0.2 fusion.3
  76.6 0.1 slice.312
  76.7 1.3 collective-permute-start.6
  78.0 3.0 %collective-permute-start.7 = (f32[16,16,128]{2,1,0:T(8,128)}, f32[16,16,128]{2,1,0:T(8,128)S(1)}, u32[]{:S(2)}, u32[]{:S(2)}) collective-permute-start(f32[16,16,128]{2,1,0:T(8,128)} %get-tuple-element.17), channel_id=1, source_target_pairs={{1,0},{64,1},{65,64},{3,2},{66,3},{67,66},{5,4},{68,5},{69,68},{7,... | collective-permute-start | bytes 393224 | tf_op jit(solution)/shard_map/ppermute | solution.py:148
  81.0 0.1 fusion.58
  81.1 0.0 copy-start.11
  81.1 0.0 copy-start.5
  81.2 0.0 collective-permute-done.6.fleft_ref
  81.2 1.0 collective-permute-done.7.fright_ref
  82.2 2.5 %collective-permute-done.4.ftop_ref = f32[16,60,128]{2,1,0:T(8,128)S(1)} collective-permute-done((f32[16,60,128]{2,1,0:T(8,128)}, f32[16,60,128]{2,1,0:T(8,128)S(1)}, u32[]{:S(2)}, u32[]{:S(2)}) %collective-permute-start.4) | collective-permute-done | bytes 491552 | tf_op jit(solution)/shard_map/ppermute | solution.py:147
  84.7 5.5 %collective-permute-done.5.fbot_ref = f32[16,60,128]{2,1,0:T(8,128)S(1)} collective-permute-done((f32[16,60,128]{2,1,0:T(8,128)}, f32[16,60,128]{2,1,0:T(8,128)S(1)}, u32[]{:S(2)}, u32[]{:S(2)}) %collective-permute-start.5) | collective-permute-done | bytes 491552 | tf_op jit(solution)/shard_map/ppermute | solution.py:148
  90.2 0.8 copy-done.7
  91.0 13.9 %shard_map.98 = f32[16,60,16,128]{3,2,1,0:T(8,128)} custom-call(f32[16,60,16,128]{3,2,1,0:T(8,128)} %shard_map.96.f_ref, f32[2,60,16,128]{3,2,1,0:T(8,128)} %w_ref.3, f32[16,60,128]{2,1,0:T(8,128)} %copy-done.6, f32[16,60,128]{2,1,0:T(8,128)} %copy-done.7, f32[18,60,128]{2,1,0:T(8,128)} %copy-done, f32[18,60,128]{2,1,0:T(8,128)} %copy-done.1, ...), custom_call_target="tpu_custom_call" | custom-call | flops 39321600 | bytes 16711680 | tf_op jit(solution)/shard_map/pallas_call | solution.py:134
  104.9 0.8 compare_select_fusion.17
  105.7 4.7 %all_to_all.15 = f32[3,16,128]{2,0,1:T(4,128)S(1)} all-to-all(f32[3,16,128]{2,0,1:T(4,128)S(1)} %copy.12), channel_id=1, replica_groups=mesh['mp'=2,'gx'=32,'gy'=2] {'gy'}, dimensions={1} | all-to-all | bytes 49152 | tf_op jit(solution)/shard_map/all_to_all | solution.py:250
  110.4 0.2 fusion.12
  110.6 0.1 fusion.75
  110.7 1.3 collective-permute-start.12
  112.0 5.5 %collective-permute-start.15 = (f32[8,8,1]{2,1,0:T(8,128)S(1)}, f32[8,8,1]{2,1,0:T(8,128)S(1)}, u32[]{:S(2)}, u32[]{:S(2)}) collective-permute-start(f32[8,8,1]{2,1,0:T(8,128)S(1)} %get-tuple-element.40), channel_id=1, source_target_pairs={{64,0},{65,1},{66,2},{67,3},{68,4},{69,5},{70,6},{71,7},{72,8},{73... | collective-permute-start | bytes 776 | tf_op jit(solution)/shard_map/ppermute | solution.py:148
  117.5 2.1 %collective-permute-start.13 = (f32[8,1,256]{2,1,0:T(1,128)S(1)}, f32[8,1,256]{2,1,0:T(1,128)S(1)}, u32[]{:S(2)}, u32[]{:S(2)}) collective-permute-start(f32[8,1,256]{2,1,0:T(1,128)S(1)} %get-tuple-element.41), channel_id=1, source_target_pairs={{0,1},{1,2},{2,3},{3,4},{4,5},{5,6},{6,7},{7,8},{8,9},{9,10},{10,1... | collective-permute-start | bytes 24584 | tf_op jit(solution)/shard_map/ppermute | solution.py:147
  119.6 2.7 %collective-permute-start.14 = (f32[8,1,256]{2,1,0:T(1,128)S(1)}, f32[8,1,256]{2,1,0:T(1,128)S(1)}, u32[]{:S(2)}, u32[]{:S(2)}) collective-permute-start(f32[8,1,256]{2,1,0:T(1,128)S(1)} %get-tuple-element.42), channel_id=1, source_target_pairs={{1,0},{2,1},{3,2},{4,3},{5,4},{6,5},{7,6},{8,7},{9,8},{10,9},{11,1... | collective-permute-start | bytes 24584 | tf_op jit(solution)/shard_map/ppermute | solution.py:148
  122.4 0.0 collective-permute-done.13
  122.4 4.3 %collective-permute-done.14 = f32[8,1,256]{2,1,0:T(1,128)S(1)} collective-permute-done((f32[8,1,256]{2,1,0:T(1,128)S(1)}, f32[8,1,256]{2,1,0:T(1,128)S(1)}, u32[]{:S(2)}, u32[]{:S(2)}) %collective-permute-start.14) | collective-permute-done | bytes 8224 | tf_op jit(solution)/shard_map/ppermute | solution.py:148
  126.7 0.2 fusion.6
  126.9 0.1 fusion.59
  127.0 0.1 slice.326
  127.1 0.2 fusion.15
  127.3 0.1 fusion.72
  127.4 1.3 collective-permute-start.16
  128.7 5.5 %collective-permute-start.19 = (f32[8,8,1]{2,1,0:T(8,128)S(1)}, f32[8,8,1]{2,1,0:T(8,128)S(1)}, u32[]{:S(2)}, u32[]{:S(2)}) collective-permute-start(f32[8,8,1]{2,1,0:T(8,128)S(1)} %get-tuple-element.34), channel_id=1, source_target_pairs={{64,0},{65,1},{66,2},{67,3},{68,4},{69,5},{70,6},{71,7},{72,8},{73... | collective-permute-start | bytes 776 | tf_op jit(solution)/shard_map/ppermute | solution.py:148
  134.2 2.5 %collective-permute-start.17 = (f32[8,1,256]{2,1,0:T(1,128)S(1)}, f32[8,1,256]{2,1,0:T(1,128)S(1)}, u32[]{:S(2)}, u32[]{:S(2)}) collective-permute-start(f32[8,1,256]{2,1,0:T(1,128)S(1)} %get-tuple-element.35), channel_id=1, source_target_pairs={{0,1},{1,2},{2,3},{3,4},{4,5},{5,6},{6,7},{7,8},{8,9},{9,10},{10,1... | collective-permute-start | bytes 24584 | tf_op jit(solution)/shard_map/ppermute | solution.py:147
  136.7 1.9 %collective-permute-start.18 = (f32[8,1,256]{2,1,0:T(1,128)S(1)}, f32[8,1,256]{2,1,0:T(1,128)S(1)}, u32[]{:S(2)}, u32[]{:S(2)}) collective-permute-start(f32[8,1,256]{2,1,0:T(1,128)S(1)} %get-tuple-element.36), channel_id=1, source_target_pairs={{1,0},{2,1},{3,2},{4,3},{5,4},{6,5},{7,6},{8,7},{9,8},{10,9},{11,1... | collective-permute-start | bytes 24584 | tf_op jit(solution)/shard_map/ppermute | solution.py:148
  138.7 0.0 collective-permute-done.19
  138.7 5.1 %collective-permute-done.18 = f32[8,1,256]{2,1,0:T(1,128)S(1)} collective-permute-done((f32[8,1,256]{2,1,0:T(1,128)S(1)}, f32[8,1,256]{2,1,0:T(1,128)S(1)}, u32[]{:S(2)}, u32[]{:S(2)}) %collective-permute-start.18) | collective-permute-done | bytes 8224 | tf_op jit(solution)/shard_map/ppermute | solution.py:148
  143.8 0.2 fusion.9
  144.0 0.1 fusion.60
  144.1 0.1 slice.340
  144.2 0.9 fusion.18
  (44 shorter events, 0.2 us)
Async XLA Ops:
  0.6 16.7 %copy-start.10 = (s32[8,256]{1,0:T(8,128)S(1)}, s32[8,256]{1,0:T(8,128)}, u32[]{:S(2)}) copy-start(s32[8,256]{1,0:T(8,128)} %param.12) | copy-start | bytes 24580
  0.6 16.7 %copy-start.12 = (f32[12]{0:T(128)S(1)}, f32[12]{0:T(128)}, u32[]{:S(2)}) copy-start(f32[12]{0:T(128)} %param.14) | copy-start | bytes 148
  0.7 16.7 %copy-start.13 = (f32[12]{0:T(128)S(1)}, f32[12]{0:T(128)}, u32[]{:S(2)}) copy-start(f32[12]{0:T(128)} %param.15) | copy-start | bytes 148
  0.7 16.8 %copy-start.2 = (f32[8,8,256]{2,1,0:T(8,128)S(1)}, f32[8,8,256]{2,1,0:T(8,128)}, u32[]{:S(2)}) copy-start(f32[8,8,256]{2,1,0:T(8,128)} %param.10) | copy-start | bytes 196612
  10.7 35.9 %collective-permute-start = (f32[18,60,128]{2,1,0:T(8,128)}, f32[18,60,128]{2,1,0:T(8,128)S(1)}, u32[]{:S(2)}, u32[]{:S(2)}) collective-permute-start(f32[18,60,128]{2,1,0:T(8,128)} %get-tuple-element.10), channel_id=1, source_target_pairs={{0,2},{2,4},{4,6},{6,8},{8,10},{10,12},{12,14},{14,16},{16,18},{18... | collective-permute-start | bytes 1658888 | tf_op jit(solution)/shard_map/ppermute | solution.py:147
  14.1 32.4 %collective-permute-start.1 = (f32[18,60,128]{2,1,0:T(8,128)}, f32[18,60,128]{2,1,0:T(8,128)S(1)}, u32[]{:S(2)}, u32[]{:S(2)}) collective-permute-start(f32[18,60,128]{2,1,0:T(8,128)} %get-tuple-element.11), channel_id=1, source_target_pairs={{2,0},{4,2},{6,4},{8,6},{10,8},{12,10},{14,12},{16,14},{18,16},{20... | collective-permute-start | bytes 1658888 | tf_op jit(solution)/shard_map/ppermute | solution.py:148
  16.0 25.2 %collective-permute-start.2 = (f32[18,16,128]{2,1,0:T(8,128)}, f32[18,16,128]{2,1,0:T(8,128)S(1)}, u32[]{:S(2)}, u32[]{:S(2)}) collective-permute-start(f32[18,16,128]{2,1,0:T(8,128)} %get-tuple-element.12), channel_id=1, source_target_pairs={{0,1},{1,64},{64,65},{2,3},{3,66},{66,67},{4,5},{5,68},{68,69},{6,... | collective-permute-start | bytes 442376 | tf_op jit(solution)/shard_map/ppermute | solution.py:147
  17.6 19.9 %collective-permute-start.8 = (f32[10,8,1]{2,1,0:T(8,128)S(1)}, f32[10,8,1]{2,1,0:T(8,128)S(1)}, u32[]{:S(2)}, u32[]{:S(2)}) collective-permute-start(f32[10,8,1]{2,1,0:T(8,128)S(1)} %get-tuple-element.29), channel_id=1, source_target_pairs={{0,64},{1,65},{2,66},{3,67},{4,68},{5,69},{6,70},{7,71},{8,72},{9,... | collective-permute-start | bytes 968 | tf_op jit(solution)/shard_map/ppermute | solution.py:147
  18.9 19.9 %collective-permute-start.11 = (f32[10,8,1]{2,1,0:T(8,128)S(1)}, f32[10,8,1]{2,1,0:T(8,128)S(1)}, u32[]{:S(2)}, u32[]{:S(2)}) collective-permute-start(f32[10,8,1]{2,1,0:T(8,128)S(1)} %get-tuple-element.30), channel_id=1, source_target_pairs={{64,0},{65,1},{66,2},{67,3},{68,4},{69,5},{70,6},{71,7},{72,8},{73... | collective-permute-start | bytes 968 | tf_op jit(solution)/shard_map/ppermute | solution.py:148
  37.4 9.1 %collective-permute-start.3 = (f32[18,16,128]{2,1,0:T(8,128)}, f32[18,16,128]{2,1,0:T(8,128)S(1)}, u32[]{:S(2)}, u32[]{:S(2)}) collective-permute-start(f32[18,16,128]{2,1,0:T(8,128)} %get-tuple-element.13), channel_id=1, source_target_pairs={{1,0},{64,1},{65,64},{3,2},{66,3},{67,66},{5,4},{68,5},{69,68},{7,... | collective-permute-start | bytes 442376 | tf_op jit(solution)/shard_map/ppermute | solution.py:148
  38.7 37.5 %collective-permute-start.10 = (f32[10,1,256]{2,1,0:T(1,128)S(1)}, f32[10,1,256]{2,1,0:T(1,128)S(1)}, u32[]{:S(2)}, u32[]{:S(2)}) collective-permute-start(f32[10,1,256]{2,1,0:T(1,128)S(1)} %get-tuple-element.28), channel_id=1, source_target_pairs={{1,0},{2,1},{3,2},{4,3},{5,4},{6,5},{7,6},{8,7},{9,8},{10,9},{11,1... | collective-permute-start | bytes 30728 | tf_op jit(solution)/shard_map/ppermute | solution.py:148
  41.2 5.3 %copy-start.3 = (f32[18,16,128]{2,1,0:T(8,128)}, f32[18,16,128]{2,1,0:T(8,128)S(1)}, u32[]{:S(2)}) copy-start(f32[18,16,128]{2,1,0:T(8,128)S(1)} %collective-permute-done.2.fleft_ref.wleft_ref) | copy-start | bytes 442372
  41.2 35.0 %collective-permute-start.9 = (f32[10,1,256]{2,1,0:T(1,128)S(1)}, f32[10,1,256]{2,1,0:T(1,128)S(1)}, u32[]{:S(2)}, u32[]{:S(2)}) collective-permute-start(f32[10,1,256]{2,1,0:T(1,128)S(1)} %get-tuple-element.27), channel_id=1, source_target_pairs={{0,1},{1,2},{2,3},{3,4},{4,5},{5,6},{6,7},{7,8},{8,9},{9,10},{10,1... | collective-permute-start | bytes 30728 | tf_op jit(solution)/shard_map/ppermute | solution.py:147
  46.5 0.6 copy-start.4
  46.5 0.9 copy-start
  47.4 0.8 copy-start.1
  71.0 13.7 %collective-permute-start.4 = (f32[16,60,128]{2,1,0:T(8,128)}, f32[16,60,128]{2,1,0:T(8,128)S(1)}, u32[]{:S(2)}, u32[]{:S(2)}) collective-permute-start(f32[16,60,128]{2,1,0:T(8,128)} %get-tuple-element.14), channel_id=1, source_target_pairs={{0,2},{2,4},{4,6},{6,8},{8,10},{10,12},{12,14},{14,16},{16,18},{18... | collective-permute-start | bytes 1474568 | tf_op jit(solution)/shard_map/ppermute | solution.py:147
  72.9 17.3 %collective-permute-start.5 = (f32[16,60,128]{2,1,0:T(8,128)}, f32[16,60,128]{2,1,0:T(8,128)S(1)}, u32[]{:S(2)}, u32[]{:S(2)}) collective-permute-start(f32[16,60,128]{2,1,0:T(8,128)} %get-tuple-element.15), channel_id=1, source_target_pairs={{2,0},{4,2},{6,4},{8,6},{10,8},{12,10},{14,12},{16,14},{18,16},{20... | collective-permute-start | bytes 1474568 | tf_op jit(solution)/shard_map/ppermute | solution.py:148
  76.7 4.5 %collective-permute-start.6 = (f32[16,16,128]{2,1,0:T(8,128)}, f32[16,16,128]{2,1,0:T(8,128)S(1)}, u32[]{:S(2)}, u32[]{:S(2)}) collective-permute-start(f32[16,16,128]{2,1,0:T(8,128)} %get-tuple-element.16), channel_id=1, source_target_pairs={{0,1},{1,64},{64,65},{2,3},{3,66},{66,67},{4,5},{5,68},{68,69},{6,... | collective-permute-start | bytes 393224 | tf_op jit(solution)/shard_map/ppermute | solution.py:147
  78.0 4.2 %collective-permute-start.7 = (f32[16,16,128]{2,1,0:T(8,128)}, f32[16,16,128]{2,1,0:T(8,128)S(1)}, u32[]{:S(2)}, u32[]{:S(2)}) collective-permute-start(f32[16,16,128]{2,1,0:T(8,128)} %get-tuple-element.17), channel_id=1, source_target_pairs={{1,0},{64,1},{65,64},{3,2},{66,3},{67,66},{5,4},{68,5},{69,68},{7,... | collective-permute-start | bytes 393224 | tf_op jit(solution)/shard_map/ppermute | solution.py:148
  81.1 29.2 %copy-start.11 = (s32[8,256]{1,0:T(8,128)S(1)}, s32[8,256]{1,0:T(8,128)}, u32[]{:S(2)}) copy-start(s32[8,256]{1,0:T(8,128)} %param.13) | copy-start | bytes 24580
  81.1 29.3 %copy-start.5 = (f32[8,8,256]{2,1,0:T(8,128)S(1)}, f32[8,8,256]{2,1,0:T(8,128)}, u32[]{:S(2)}) copy-start(f32[8,8,256]{2,1,0:T(8,128)} %param.11) | copy-start | bytes 196612
  81.2 9.0 %copy-start.8 = (f32[16,16,128]{2,1,0:T(8,128)}, f32[16,16,128]{2,1,0:T(8,128)S(1)}, u32[]{:S(2)}) copy-start(f32[16,16,128]{2,1,0:T(8,128)S(1)} %collective-permute-done.6.fleft_ref) | copy-start | bytes 393220
  82.2 8.0 %copy-start.9 = (f32[16,16,128]{2,1,0:T(8,128)}, f32[16,16,128]{2,1,0:T(8,128)S(1)}, u32[]{:S(2)}) copy-start(f32[16,16,128]{2,1,0:T(8,128)S(1)} %collective-permute-done.7.fright_ref) | copy-start | bytes 393220
  84.7 5.5 %copy-start.6 = (f32[16,60,128]{2,1,0:T(8,128)}, f32[16,60,128]{2,1,0:T(8,128)S(1)}, u32[]{:S(2)}) copy-start(f32[16,60,128]{2,1,0:T(8,128)S(1)} %collective-permute-done.4.ftop_ref) | copy-start | bytes 1474564
  90.2 0.8 copy-start.7
  110.7 11.6 %collective-permute-start.12 = (f32[8,8,1]{2,1,0:T(8,128)S(1)}, f32[8,8,1]{2,1,0:T(8,128)S(1)}, u32[]{:S(2)}, u32[]{:S(2)}) collective-permute-start(f32[8,8,1]{2,1,0:T(8,128)S(1)} %get-tuple-element.39), channel_id=1, source_target_pairs={{0,64},{1,65},{2,66},{3,67},{4,68},{5,69},{6,70},{7,71},{8,72},{9,... | collective-permute-start | bytes 776 | tf_op jit(solution)/shard_map/ppermute | solution.py:147
  112.0 10.3 %collective-permute-start.15 = (f32[8,8,1]{2,1,0:T(8,128)S(1)}, f32[8,8,1]{2,1,0:T(8,128)S(1)}, u32[]{:S(2)}, u32[]{:S(2)}) collective-permute-start(f32[8,8,1]{2,1,0:T(8,128)S(1)} %get-tuple-element.40), channel_id=1, source_target_pairs={{64,0},{65,1},{66,2},{67,3},{68,4},{69,5},{70,6},{71,7},{72,8},{73... | collective-permute-start | bytes 776 | tf_op jit(solution)/shard_map/ppermute | solution.py:148
  117.5 4.8 %collective-permute-start.13 = (f32[8,1,256]{2,1,0:T(1,128)S(1)}, f32[8,1,256]{2,1,0:T(1,128)S(1)}, u32[]{:S(2)}, u32[]{:S(2)}) collective-permute-start(f32[8,1,256]{2,1,0:T(1,128)S(1)} %get-tuple-element.41), channel_id=1, source_target_pairs={{0,1},{1,2},{2,3},{3,4},{4,5},{5,6},{6,7},{7,8},{8,9},{9,10},{10,1... | collective-permute-start | bytes 24584 | tf_op jit(solution)/shard_map/ppermute | solution.py:147
  119.6 7.1 %collective-permute-start.14 = (f32[8,1,256]{2,1,0:T(1,128)S(1)}, f32[8,1,256]{2,1,0:T(1,128)S(1)}, u32[]{:S(2)}, u32[]{:S(2)}) collective-permute-start(f32[8,1,256]{2,1,0:T(1,128)S(1)} %get-tuple-element.42), channel_id=1, source_target_pairs={{1,0},{2,1},{3,2},{4,3},{5,4},{6,5},{7,6},{8,7},{9,8},{10,9},{11,1... | collective-permute-start | bytes 24584 | tf_op jit(solution)/shard_map/ppermute | solution.py:148
  127.4 11.3 %collective-permute-start.16 = (f32[8,8,1]{2,1,0:T(8,128)S(1)}, f32[8,8,1]{2,1,0:T(8,128)S(1)}, u32[]{:S(2)}, u32[]{:S(2)}) collective-permute-start(f32[8,8,1]{2,1,0:T(8,128)S(1)} %get-tuple-element.33), channel_id=1, source_target_pairs={{0,64},{1,65},{2,66},{3,67},{4,68},{5,69},{6,70},{7,71},{8,72},{9,... | collective-permute-start | bytes 776 | tf_op jit(solution)/shard_map/ppermute | solution.py:147
  128.7 10.0 %collective-permute-start.19 = (f32[8,8,1]{2,1,0:T(8,128)S(1)}, f32[8,8,1]{2,1,0:T(8,128)S(1)}, u32[]{:S(2)}, u32[]{:S(2)}) collective-permute-start(f32[8,8,1]{2,1,0:T(8,128)S(1)} %get-tuple-element.34), channel_id=1, source_target_pairs={{64,0},{65,1},{66,2},{67,3},{68,4},{69,5},{70,6},{71,7},{72,8},{73... | collective-permute-start | bytes 776 | tf_op jit(solution)/shard_map/ppermute | solution.py:148
  134.2 4.5 %collective-permute-start.17 = (f32[8,1,256]{2,1,0:T(1,128)S(1)}, f32[8,1,256]{2,1,0:T(1,128)S(1)}, u32[]{:S(2)}, u32[]{:S(2)}) collective-permute-start(f32[8,1,256]{2,1,0:T(1,128)S(1)} %get-tuple-element.35), channel_id=1, source_target_pairs={{0,1},{1,2},{2,3},{3,4},{4,5},{5,6},{6,7},{7,8},{8,9},{9,10},{10,1... | collective-permute-start | bytes 24584 | tf_op jit(solution)/shard_map/ppermute | solution.py:147
  136.7 7.1 %collective-permute-start.18 = (f32[8,1,256]{2,1,0:T(1,128)S(1)}, f32[8,1,256]{2,1,0:T(1,128)S(1)}, u32[]{:S(2)}, u32[]{:S(2)}) collective-permute-start(f32[8,1,256]{2,1,0:T(1,128)S(1)} %get-tuple-element.36), channel_id=1, source_target_pairs={{1,0},{2,1},{3,2},{4,3},{5,4},{6,5},{7,6},{8,7},{9,8},{10,9},{11,1... | collective-permute-start | bytes 24584 | tf_op jit(solution)/shard_map/ppermute | solution.py:148

commit v8 on v7

--- a/solution.py
+++ b/solution.py
@@ -50,13 +50,16 @@
         def _():
             for b in range(w_ref.shape[0]):
                 edge_body(w_ref, b, *outs)
+            for b in range(w_ref.shape[0], outs[0].shape[0]):
+                for out in outs:
+                    out[b] = jnp.zeros(out.shape[1:], out.dtype)
 
 
 def edges(f, w=None):
     n, nlev, rows, cols = f.shape
-    nb = 2
+    nb = 4
     nmain = n // nb
-    total = n + (0 if w is None else w.shape[0])
+    total = n + (0 if w is None else nb)
     row_shape = jax.ShapeDtypeStruct((total, nlev, cols), f.dtype)
     col_shape = jax.ShapeDtypeStruct((total, rows, cols), f.dtype)
     rspec = pl.BlockSpec((nb, nlev, cols), lambda i: (i, 0, 0))

time: 146 us -> 145 us (level)
  Pallas kernels: 46.6 us -> 44 us
  waiting for transfers between devices: 30.5 us -> 32 us
    pallas_call x2, Pallas kernels: 19 us -> 16.2 us  [edges(): pl.pallas_call(functools.partial(edge_kernel, nmain), grid=(total // nb,)...]
    ppermute x10, waiting for transfers between devices: 14.6 us -> 16.1 us  [exchange(): before = lax.ppermute(last, axes, shift_pairs(n, 1))]
  transfers between devices with their start and end apart: 20 -> 20, of which waited for: 6 -> 6; matrix products, arithmetic and copies ran while one was open for 1% -> 1% of each run, Pallas kernels for 16% -> 15%
where the time goes in v8:
time: 145 us; the launch traced here: 144 us
  starting transfers between devices  55.7 us (38%)
  Pallas kernels  44 us (30%)
  waiting for transfers between devices  32 us (22%)
  blocking collectives  4.65 us (3%)
  other arithmetic  3.26 us (2%)
  local copies, waits for them, and re-layouts  3.2 us (2%)
    ppermute x10, starting transfers between devices, exchange(): after = lax.ppermute(first, axes, shift_pairs(n, -1))  34.2 us
    pallas_call x2, Pallas kernels, advect_step(): pl.pallas_call(step_kernel, grid=(nsp // SB,), in_specs=[main, pl.BlockSp...  27.7 us
    ppermute x10, starting transfers between devices, exchange(): before = lax.ppermute(last, axes, shift_pairs(n, 1))  21.6 us
    pallas_call x2, Pallas kernels, edges(): pl.pallas_call(functools.partial(edge_kernel, nmain), grid=(total // nb,)...  16.2 us
    ppermute x10, waiting for transfers between devices, exchange(): before = lax.ppermute(last, axes, shift_pairs(n, 1))  16.1 us
    ppermute x10, waiting for transfers between devices, exchange(): after = lax.ppermute(first, axes, shift_pairs(n, -1))  15.9 us
    all_to_all x1, blocking collectives, on_device(): lax.all_to_all(forcing_fields(advected), 'gy', split_axis=1, concat_axis=...  4.65 us
  transfers between devices with their start and end apart: 20, of which 6 were waited for; matrix products, arithmetic and copies ran while one was open for 1% of the time, Pallas kernels for 15%

profile of v8, /device:TPU:31, one launch (start us, length us, event | category | flops | bytes accessed | tf_op | source)
XLA Modules:
  0.0 144.1 jit_solution(12253479479657877604)
XLA Ops:
  0.7 8.6 %shard_map.95 = (f32[20,60,128]{2,1,0:T(8,128)}, f32[20,60,128]{2,1,0:T(8,128)}, f32[20,16,128]{2,1,0:T(8,128)}, f32[20,16,128]{2,1,0:T(8,128)}) custom-call(f32[16,60,16,128]{3,2,1,0:T(8,128)} %f_ref.3, f32[2,60,16,128]{3,2,1,0:T(8,128)} %w_ref.3), custom_call_target="tpu_custom_call" | custom-call | flops 9830400 | bytes 9830400 | tf_op jit(solution)/shard_map/pallas_call | solution.py:72
  9.3 3.4 %collective-permute-start = (f32[20,60,128]{2,1,0:T(8,128)}, f32[20,60,128]{2,1,0:T(8,128)S(1)}, u32[]{:S(2)}, u32[]{:S(2)}) collective-permute-start(f32[20,60,128]{2,1,0:T(8,128)} %get-tuple-element.10), channel_id=1, source_target_pairs={{0,2},{2,4},{4,6},{6,8},{8,10},{10,12},{12,14},{14,16},{16,18},{18... | collective-permute-start | bytes 1843208 | tf_op jit(solution)/shard_map/ppermute | solution.py:150
  12.7 1.9 %collective-permute-start.1 = (f32[20,60,128]{2,1,0:T(8,128)}, f32[20,60,128]{2,1,0:T(8,128)S(1)}, u32[]{:S(2)}, u32[]{:S(2)}) collective-permute-start(f32[20,60,128]{2,1,0:T(8,128)} %get-tuple-element.11), channel_id=1, source_target_pairs={{2,0},{4,2},{6,4},{8,6},{10,8},{12,10},{14,12},{16,14},{18,16},{20... | collective-permute-start | bytes 1843208 | tf_op jit(solution)/shard_map/ppermute | solution.py:151
  14.7 1.3 collective-permute-start.2
  16.0 0.1 select_reduce_fusion.1
  16.1 0.1 fusion.70
  16.2 1.3 collective-permute-start.8
  17.5 6.5 %collective-permute-start.11 = (f32[10,8,1]{2,1,0:T(8,128)S(1)}, f32[10,8,1]{2,1,0:T(8,128)S(1)}, u32[]{:S(2)}, u32[]{:S(2)}) collective-permute-start(f32[10,8,1]{2,1,0:T(8,128)S(1)} %get-tuple-element.30), channel_id=1, source_target_pairs={{64,0},{65,1},{66,2},{67,3},{68,4},{69,5},{70,6},{71,7},{72,8},{73... | collective-permute-start | bytes 968 | tf_op jit(solution)/shard_map/ppermute | solution.py:151
  24.0 13.6 %collective-permute-done.8 = f32[10,8,1]{2,1,0:T(8,128)S(1)} collective-permute-done((f32[10,8,1]{2,1,0:T(8,128)S(1)}, f32[10,8,1]{2,1,0:T(8,128)S(1)}, u32[]{:S(2)}, u32[]{:S(2)}) %collective-permute-start.8) | collective-permute-done | bytes 352 | tf_op jit(solution)/shard_map/ppermute | solution.py:150
  37.6 1.3 collective-permute-start.3
  38.9 0.0 collective-permute-done.11
  38.9 2.5 %collective-permute-start.10 = (f32[10,1,256]{2,1,0:T(1,128)S(1)}, f32[10,1,256]{2,1,0:T(1,128)S(1)}, u32[]{:S(2)}, u32[]{:S(2)}) collective-permute-start(f32[10,1,256]{2,1,0:T(1,128)S(1)} %get-tuple-element.28), channel_id=1, source_target_pairs={{1,0},{2,1},{3,2},{4,3},{5,4},{6,5},{7,6},{8,7},{9,8},{10,9},{11,1... | collective-permute-start | bytes 30728 | tf_op jit(solution)/shard_map/ppermute | solution.py:151
  41.4 0.0 collective-permute-done.2.fleft_ref.wleft_ref
  41.4 5.2 %collective-permute-start.9 = (f32[10,1,256]{2,1,0:T(1,128)S(1)}, f32[10,1,256]{2,1,0:T(1,128)S(1)}, u32[]{:S(2)}, u32[]{:S(2)}) collective-permute-start(f32[10,1,256]{2,1,0:T(1,128)S(1)} %get-tuple-element.27), channel_id=1, source_target_pairs={{0,1},{1,2},{2,3},{3,4},{4,5},{5,6},{6,7},{7,8},{8,9},{9,10},{10,1... | collective-permute-start | bytes 30728 | tf_op jit(solution)/shard_map/ppermute | solution.py:150
  46.7 0.0 collective-permute-done.3.fright_ref.wright_ref
  46.7 0.0 collective-permute-done.ftop_ref.wtop_ref
  46.7 0.0 collective-permute-done.1.fbot_ref.wbot_ref
  46.8 0.6 copy-done.4
  47.4 0.3 copy-done
  47.7 0.9 copy-done.1
  48.5 13.9 %shard_map.96.f_ref = f32[16,60,16,128]{3,2,1,0:T(8,128)} custom-call(f32[16,60,16,128]{3,2,1,0:T(8,128)} %f_ref.3, f32[2,60,16,128]{3,2,1,0:T(8,128)} %w_ref.3, f32[20,60,128]{2,1,0:T(8,128)} %copy-done, f32[20,60,128]{2,1,0:T(8,128)} %copy-done.1, f32[20,60,128]{2,1,0:T(8,128)} %copy-done, f32[20,60,128]{2,1,0:T(8,128)} %copy-done.1, ...), custom_call_target="tpu_custom_call" | custom-call | flops 39321600 | bytes 16711680 | tf_op jit(solution)/shard_map/pallas_call | solution.py:137
  62.4 7.6 %shard_map.97 = (f32[16,60,128]{2,1,0:T(8,128)}, f32[16,60,128]{2,1,0:T(8,128)}, f32[16,16,128]{2,1,0:T(8,128)}, f32[16,16,128]{2,1,0:T(8,128)}) custom-call(f32[16,60,16,128]{3,2,1,0:T(8,128)} %shard_map.96.f_ref), custom_call_target="tpu_custom_call" | custom-call | flops 7864320 | bytes 7864320 | tf_op jit(solution)/shard_map/pallas_call | solution.py:72
  70.0 1.9 %collective-permute-start.4 = (f32[16,60,128]{2,1,0:T(8,128)}, f32[16,60,128]{2,1,0:T(8,128)S(1)}, u32[]{:S(2)}, u32[]{:S(2)}) collective-permute-start(f32[16,60,128]{2,1,0:T(8,128)} %get-tuple-element.14), channel_id=1, source_target_pairs={{0,2},{2,4},{4,6},{6,8},{8,10},{10,12},{12,14},{14,16},{16,18},{18... | collective-permute-start | bytes 1474568 | tf_op jit(solution)/shard_map/ppermute | solution.py:150
  72.0 3.4 %collective-permute-start.5 = (f32[16,60,128]{2,1,0:T(8,128)}, f32[16,60,128]{2,1,0:T(8,128)S(1)}, u32[]{:S(2)}, u32[]{:S(2)}) collective-permute-start(f32[16,60,128]{2,1,0:T(8,128)} %get-tuple-element.15), channel_id=1, source_target_pairs={{2,0},{4,2},{6,4},{8,6},{10,8},{12,10},{14,12},{16,14},{18,16},{20... | collective-permute-start | bytes 1474568 | tf_op jit(solution)/shard_map/ppermute | solution.py:151
  75.3 0.0 collective-permute-done.9
  75.3 0.1 maximum_bitcast_fusion.1
  75.4 0.2 fusion.3
  75.7 0.1 slice.312
  75.7 1.3 collective-permute-start.6
  77.0 3.0 %collective-permute-start.7 = (f32[16,16,128]{2,1,0:T(8,128)}, f32[16,16,128]{2,1,0:T(8,128)S(1)}, u32[]{:S(2)}, u32[]{:S(2)}) collective-permute-start(f32[16,16,128]{2,1,0:T(8,128)} %get-tuple-element.17), channel_id=1, source_target_pairs={{1,0},{64,1},{65,64},{3,2},{66,3},{67,66},{5,4},{68,5},{69,68},{7,... | collective-permute-start | bytes 393224 | tf_op jit(solution)/shard_map/ppermute | solution.py:151
  80.1 0.1 fusion.58
  80.2 0.0 copy-start.11
  80.2 0.0 copy-start.5
  80.2 1.0 collective-permute-done.7.fright_ref
  81.2 2.5 %collective-permute-done.4.ftop_ref = f32[16,60,128]{2,1,0:T(8,128)S(1)} collective-permute-done((f32[16,60,128]{2,1,0:T(8,128)}, f32[16,60,128]{2,1,0:T(8,128)S(1)}, u32[]{:S(2)}, u32[]{:S(2)}) %collective-permute-start.4) | collective-permute-done | bytes 491552 | tf_op jit(solution)/shard_map/ppermute | solution.py:150
  83.8 5.5 %collective-permute-done.5.fbot_ref = f32[16,60,128]{2,1,0:T(8,128)S(1)} collective-permute-done((f32[16,60,128]{2,1,0:T(8,128)}, f32[16,60,128]{2,1,0:T(8,128)S(1)}, u32[]{:S(2)}, u32[]{:S(2)}) %collective-permute-start.5) | collective-permute-done | bytes 491552 | tf_op jit(solution)/shard_map/ppermute | solution.py:151
  89.3 0.8 copy-done.7
  90.1 13.9 %shard_map.98 = f32[16,60,16,128]{3,2,1,0:T(8,128)} custom-call(f32[16,60,16,128]{3,2,1,0:T(8,128)} %shard_map.96.f_ref, f32[2,60,16,128]{3,2,1,0:T(8,128)} %w_ref.3, f32[16,60,128]{2,1,0:T(8,128)} %copy-done.6, f32[16,60,128]{2,1,0:T(8,128)} %copy-done.7, f32[20,60,128]{2,1,0:T(8,128)} %copy-done, f32[20,60,128]{2,1,0:T(8,128)} %copy-done.1, ...), custom_call_target="tpu_custom_call" | custom-call | flops 39321600 | bytes 16711680 | tf_op jit(solution)/shard_map/pallas_call | solution.py:137
  103.9 0.8 compare_select_fusion.17
  104.7 4.7 %all_to_all.15 = f32[3,16,128]{2,0,1:T(4,128)S(1)} all-to-all(f32[3,16,128]{2,0,1:T(4,128)S(1)} %copy.12), channel_id=1, replica_groups=mesh['mp'=2,'gx'=32,'gy'=2] {'gy'}, dimensions={1} | all-to-all | bytes 49152 | tf_op jit(solution)/shard_map/all_to_all | solution.py:253
  109.5 0.2 fusion.12
  109.7 0.1 fusion.75
  109.8 1.3 collective-permute-start.12
  111.1 5.5 %collective-permute-start.15 = (f32[8,8,1]{2,1,0:T(8,128)S(1)}, f32[8,8,1]{2,1,0:T(8,128)S(1)}, u32[]{:S(2)}, u32[]{:S(2)}) collective-permute-start(f32[8,8,1]{2,1,0:T(8,128)S(1)} %get-tuple-element.40), channel_id=1, source_target_pairs={{64,0},{65,1},{66,2},{67,3},{68,4},{69,5},{70,6},{71,7},{72,8},{73... | collective-permute-start | bytes 776 | tf_op jit(solution)/shard_map/ppermute | solution.py:151
  116.6 2.1 %collective-permute-start.13 = (f32[8,1,256]{2,1,0:T(1,128)S(1)}, f32[8,1,256]{2,1,0:T(1,128)S(1)}, u32[]{:S(2)}, u32[]{:S(2)}) collective-permute-start(f32[8,1,256]{2,1,0:T(1,128)S(1)} %get-tuple-element.41), channel_id=1, source_target_pairs={{0,1},{1,2},{2,3},{3,4},{4,5},{5,6},{6,7},{7,8},{8,9},{9,10},{10,1... | collective-permute-start | bytes 24584 | tf_op jit(solution)/shard_map/ppermute | solution.py:150
  118.7 2.7 %collective-permute-start.14 = (f32[8,1,256]{2,1,0:T(1,128)S(1)}, f32[8,1,256]{2,1,0:T(1,128)S(1)}, u32[]{:S(2)}, u32[]{:S(2)}) collective-permute-start(f32[8,1,256]{2,1,0:T(1,128)S(1)} %get-tuple-element.42), channel_id=1, source_target_pairs={{1,0},{2,1},{3,2},{4,3},{5,4},{6,5},{7,6},{8,7},{9,8},{10,9},{11,1... | collective-permute-start | bytes 24584 | tf_op jit(solution)/shard_map/ppermute | solution.py:151
  121.4 0.0 collective-permute-done.13
  121.4 4.3 %collective-permute-done.14 = f32[8,1,256]{2,1,0:T(1,128)S(1)} collective-permute-done((f32[8,1,256]{2,1,0:T(1,128)S(1)}, f32[8,1,256]{2,1,0:T(1,128)S(1)}, u32[]{:S(2)}, u32[]{:S(2)}) %collective-permute-start.14) | collective-permute-done | bytes 8224 | tf_op jit(solution)/shard_map/ppermute | solution.py:151
  125.7 0.2 fusion.6
  125.9 0.1 fusion.59
  126.1 0.1 slice.326
  126.1 0.2 fusion.15
  126.4 0.1 fusion.72
  126.5 1.3 collective-permute-start.16
  127.8 5.5 %collective-permute-start.19 = (f32[8,8,1]{2,1,0:T(8,128)S(1)}, f32[8,8,1]{2,1,0:T(8,128)S(1)}, u32[]{:S(2)}, u32[]{:S(2)}) collective-permute-start(f32[8,8,1]{2,1,0:T(8,128)S(1)} %get-tuple-element.34), channel_id=1, source_target_pairs={{64,0},{65,1},{66,2},{67,3},{68,4},{69,5},{70,6},{71,7},{72,8},{73... | collective-permute-start | bytes 776 | tf_op jit(solution)/shard_map/ppermute | solution.py:151
  133.3 2.5 %collective-permute-start.17 = (f32[8,1,256]{2,1,0:T(1,128)S(1)}, f32[8,1,256]{2,1,0:T(1,128)S(1)}, u32[]{:S(2)}, u32[]{:S(2)}) collective-permute-start(f32[8,1,256]{2,1,0:T(1,128)S(1)} %get-tuple-element.35), channel_id=1, source_target_pairs={{0,1},{1,2},{2,3},{3,4},{4,5},{5,6},{6,7},{7,8},{8,9},{9,10},{10,1... | collective-permute-start | bytes 24584 | tf_op jit(solution)/shard_map/ppermute | solution.py:150
  135.8 1.9 %collective-permute-start.18 = (f32[8,1,256]{2,1,0:T(1,128)S(1)}, f32[8,1,256]{2,1,0:T(1,128)S(1)}, u32[]{:S(2)}, u32[]{:S(2)}) collective-permute-start(f32[8,1,256]{2,1,0:T(1,128)S(1)} %get-tuple-element.36), channel_id=1, source_target_pairs={{1,0},{2,1},{3,2},{4,3},{5,4},{6,5},{7,6},{8,7},{9,8},{10,9},{11,1... | collective-permute-start | bytes 24584 | tf_op jit(solution)/shard_map/ppermute | solution.py:151
  137.7 0.0 collective-permute-done.16
  137.8 0.0 collective-permute-done.17
  137.8 5.1 %collective-permute-done.18 = f32[8,1,256]{2,1,0:T(1,128)S(1)} collective-permute-done((f32[8,1,256]{2,1,0:T(1,128)S(1)}, f32[8,1,256]{2,1,0:T(1,128)S(1)}, u32[]{:S(2)}, u32[]{:S(2)}) %collective-permute-start.18) | collective-permute-done | bytes 8224 | tf_op jit(solution)/shard_map/ppermute | solution.py:151
  142.9 0.2 fusion.9
  143.1 0.1 fusion.60
  143.2 0.1 slice.340
  143.2 0.9 fusion.18
  (44 shorter events, 0.2 us)
Async XLA Ops:
  0.6 15.3 %copy-start.10 = (s32[8,256]{1,0:T(8,128)S(1)}, s32[8,256]{1,0:T(8,128)}, u32[]{:S(2)}) copy-start(s32[8,256]{1,0:T(8,128)} %param.12) | copy-start | bytes 24580
  0.6 15.3 %copy-start.12 = (f32[12]{0:T(128)S(1)}, f32[12]{0:T(128)}, u32[]{:S(2)}) copy-start(f32[12]{0:T(128)} %param.14) | copy-start | bytes 148
  0.7 15.3 %copy-start.13 = (f32[12]{0:T(128)S(1)}, f32[12]{0:T(128)}, u32[]{:S(2)}) copy-start(f32[12]{0:T(128)} %param.15) | copy-start | bytes 148
  0.7 15.4 %copy-start.2 = (f32[8,8,256]{2,1,0:T(8,128)S(1)}, f32[8,8,256]{2,1,0:T(8,128)}, u32[]{:S(2)}) copy-start(f32[8,8,256]{2,1,0:T(8,128)} %param.10) | copy-start | bytes 196612
  9.3 37.5 %collective-permute-start = (f32[20,60,128]{2,1,0:T(8,128)}, f32[20,60,128]{2,1,0:T(8,128)S(1)}, u32[]{:S(2)}, u32[]{:S(2)}) collective-permute-start(f32[20,60,128]{2,1,0:T(8,128)} %get-tuple-element.10), channel_id=1, source_target_pairs={{0,2},{2,4},{4,6},{6,8},{8,10},{10,12},{12,14},{14,16},{16,18},{18... | collective-permute-start | bytes 1843208 | tf_op jit(solution)/shard_map/ppermute | solution.py:150
  12.7 34.0 %collective-permute-start.1 = (f32[20,60,128]{2,1,0:T(8,128)}, f32[20,60,128]{2,1,0:T(8,128)S(1)}, u32[]{:S(2)}, u32[]{:S(2)}) collective-permute-start(f32[20,60,128]{2,1,0:T(8,128)} %get-tuple-element.11), channel_id=1, source_target_pairs={{2,0},{4,2},{6,4},{8,6},{10,8},{12,10},{14,12},{16,14},{18,16},{20... | collective-permute-start | bytes 1843208 | tf_op jit(solution)/shard_map/ppermute | solution.py:151
  14.7 26.8 %collective-permute-start.2 = (f32[20,16,128]{2,1,0:T(8,128)}, f32[20,16,128]{2,1,0:T(8,128)S(1)}, u32[]{:S(2)}, u32[]{:S(2)}) collective-permute-start(f32[20,16,128]{2,1,0:T(8,128)} %get-tuple-element.12), channel_id=1, source_target_pairs={{0,1},{1,64},{64,65},{2,3},{3,66},{66,67},{4,5},{5,68},{68,69},{6,... | collective-permute-start | bytes 491528 | tf_op jit(solution)/shard_map/ppermute | solution.py:150
  16.2 21.4 %collective-permute-start.8 = (f32[10,8,1]{2,1,0:T(8,128)S(1)}, f32[10,8,1]{2,1,0:T(8,128)S(1)}, u32[]{:S(2)}, u32[]{:S(2)}) collective-permute-start(f32[10,8,1]{2,1,0:T(8,128)S(1)} %get-tuple-element.29), channel_id=1, source_target_pairs={{0,64},{1,65},{2,66},{3,67},{4,68},{5,69},{6,70},{7,71},{8,72},{9,... | collective-permute-start | bytes 968 | tf_op jit(solution)/shard_map/ppermute | solution.py:150
  17.5 21.4 %collective-permute-start.11 = (f32[10,8,1]{2,1,0:T(8,128)S(1)}, f32[10,8,1]{2,1,0:T(8,128)S(1)}, u32[]{:S(2)}, u32[]{:S(2)}) collective-permute-start(f32[10,8,1]{2,1,0:T(8,128)S(1)} %get-tuple-element.30), channel_id=1, source_target_pairs={{64,0},{65,1},{66,2},{67,3},{68,4},{69,5},{70,6},{71,7},{72,8},{73... | collective-permute-start | bytes 968 | tf_op jit(solution)/shard_map/ppermute | solution.py:151
  37.6 9.1 %collective-permute-start.3 = (f32[20,16,128]{2,1,0:T(8,128)}, f32[20,16,128]{2,1,0:T(8,128)S(1)}, u32[]{:S(2)}, u32[]{:S(2)}) collective-permute-start(f32[20,16,128]{2,1,0:T(8,128)} %get-tuple-element.13), channel_id=1, source_target_pairs={{1,0},{64,1},{65,64},{3,2},{66,3},{67,66},{5,4},{68,5},{69,68},{7,... | collective-permute-start | bytes 491528 | tf_op jit(solution)/shard_map/ppermute | solution.py:151
  38.9 36.4 %collective-permute-start.10 = (f32[10,1,256]{2,1,0:T(1,128)S(1)}, f32[10,1,256]{2,1,0:T(1,128)S(1)}, u32[]{:S(2)}, u32[]{:S(2)}) collective-permute-start(f32[10,1,256]{2,1,0:T(1,128)S(1)} %get-tuple-element.28), channel_id=1, source_target_pairs={{1,0},{2,1},{3,2},{4,3},{5,4},{6,5},{7,6},{8,7},{9,8},{10,9},{11,1... | collective-permute-start | bytes 30728 | tf_op jit(solution)/shard_map/ppermute | solution.py:151
  41.4 5.3 %copy-start.3 = (f32[20,16,128]{2,1,0:T(8,128)}, f32[20,16,128]{2,1,0:T(8,128)S(1)}, u32[]{:S(2)}) copy-start(f32[20,16,128]{2,1,0:T(8,128)S(1)} %collective-permute-done.2.fleft_ref.wleft_ref) | copy-start | bytes 491524
  41.4 33.9 %collective-permute-start.9 = (f32[10,1,256]{2,1,0:T(1,128)S(1)}, f32[10,1,256]{2,1,0:T(1,128)S(1)}, u32[]{:S(2)}, u32[]{:S(2)}) collective-permute-start(f32[10,1,256]{2,1,0:T(1,128)S(1)} %get-tuple-element.27), channel_id=1, source_target_pairs={{0,1},{1,2},{2,3},{3,4},{4,5},{5,6},{6,7},{7,8},{8,9},{9,10},{10,1... | collective-permute-start | bytes 30728 | tf_op jit(solution)/shard_map/ppermute | solution.py:150
  46.7 0.7 copy-start.4
  46.7 0.9 copy-start
  47.7 0.9 copy-start.1
  70.0 13.7 %collective-permute-start.4 = (f32[16,60,128]{2,1,0:T(8,128)}, f32[16,60,128]{2,1,0:T(8,128)S(1)}, u32[]{:S(2)}, u32[]{:S(2)}) collective-permute-start(f32[16,60,128]{2,1,0:T(8,128)} %get-tuple-element.14), channel_id=1, source_target_pairs={{0,2},{2,4},{4,6},{6,8},{8,10},{10,12},{12,14},{14,16},{16,18},{18... | collective-permute-start | bytes 1474568 | tf_op jit(solution)/shard_map/ppermute | solution.py:150
  72.0 17.3 %collective-permute-start.5 = (f32[16,60,128]{2,1,0:T(8,128)}, f32[16,60,128]{2,1,0:T(8,128)S(1)}, u32[]{:S(2)}, u32[]{:S(2)}) collective-permute-start(f32[16,60,128]{2,1,0:T(8,128)} %get-tuple-element.15), channel_id=1, source_target_pairs={{2,0},{4,2},{6,4},{8,6},{10,8},{12,10},{14,12},{16,14},{18,16},{20... | collective-permute-start | bytes 1474568 | tf_op jit(solution)/shard_map/ppermute | solution.py:151
  75.7 4.5 %collective-permute-start.6 = (f32[16,16,128]{2,1,0:T(8,128)}, f32[16,16,128]{2,1,0:T(8,128)S(1)}, u32[]{:S(2)}, u32[]{:S(2)}) collective-permute-start(f32[16,16,128]{2,1,0:T(8,128)} %get-tuple-element.16), channel_id=1, source_target_pairs={{0,1},{1,64},{64,65},{2,3},{3,66},{66,67},{4,5},{5,68},{68,69},{6,... | collective-permute-start | bytes 393224 | tf_op jit(solution)/shard_map/ppermute | solution.py:150
  77.0 4.2 %collective-permute-start.7 = (f32[16,16,128]{2,1,0:T(8,128)}, f32[16,16,128]{2,1,0:T(8,128)S(1)}, u32[]{:S(2)}, u32[]{:S(2)}) collective-permute-start(f32[16,16,128]{2,1,0:T(8,128)} %get-tuple-element.17), channel_id=1, source_target_pairs={{1,0},{64,1},{65,64},{3,2},{66,3},{67,66},{5,4},{68,5},{69,68},{7,... | collective-permute-start | bytes 393224 | tf_op jit(solution)/shard_map/ppermute | solution.py:151
  80.2 29.2 %copy-start.11 = (s32[8,256]{1,0:T(8,128)S(1)}, s32[8,256]{1,0:T(8,128)}, u32[]{:S(2)}) copy-start(s32[8,256]{1,0:T(8,128)} %param.13) | copy-start | bytes 24580
  80.2 29.3 %copy-start.5 = (f32[8,8,256]{2,1,0:T(8,128)S(1)}, f32[8,8,256]{2,1,0:T(8,128)}, u32[]{:S(2)}) copy-start(f32[8,8,256]{2,1,0:T(8,128)} %param.11) | copy-start | bytes 196612
  80.2 9.0 %copy-start.8 = (f32[16,16,128]{2,1,0:T(8,128)}, f32[16,16,128]{2,1,0:T(8,128)S(1)}, u32[]{:S(2)}) copy-start(f32[16,16,128]{2,1,0:T(8,128)S(1)} %collective-permute-done.6.fleft_ref) | copy-start | bytes 393220
  81.2 8.0 %copy-start.9 = (f32[16,16,128]{2,1,0:T(8,128)}, f32[16,16,128]{2,1,0:T(8,128)S(1)}, u32[]{:S(2)}) copy-start(f32[16,16,128]{2,1,0:T(8,128)S(1)} %collective-permute-done.7.fright_ref) | copy-start | bytes 393220
  83.8 5.5 %copy-start.6 = (f32[16,60,128]{2,1,0:T(8,128)}, f32[16,60,128]{2,1,0:T(8,128)S(1)}, u32[]{:S(2)}) copy-start(f32[16,60,128]{2,1,0:T(8,128)S(1)} %collective-permute-done.4.ftop_ref) | copy-start | bytes 1474564
  89.3 0.8 copy-start.7
  109.8 11.6 %collective-permute-start.12 = (f32[8,8,1]{2,1,0:T(8,128)S(1)}, f32[8,8,1]{2,1,0:T(8,128)S(1)}, u32[]{:S(2)}, u32[]{:S(2)}) collective-permute-start(f32[8,8,1]{2,1,0:T(8,128)S(1)} %get-tuple-element.39), channel_id=1, source_target_pairs={{0,64},{1,65},{2,66},{3,67},{4,68},{5,69},{6,70},{7,71},{8,72},{9,... | collective-permute-start | bytes 776 | tf_op jit(solution)/shard_map/ppermute | solution.py:150
  111.1 10.3 %collective-permute-start.15 = (f32[8,8,1]{2,1,0:T(8,128)S(1)}, f32[8,8,1]{2,1,0:T(8,128)S(1)}, u32[]{:S(2)}, u32[]{:S(2)}) collective-permute-start(f32[8,8,1]{2,1,0:T(8,128)S(1)} %get-tuple-element.40), channel_id=1, source_target_pairs={{64,0},{65,1},{66,2},{67,3},{68,4},{69,5},{70,6},{71,7},{72,8},{73... | collective-permute-start | bytes 776 | tf_op jit(solution)/shard_map/ppermute | solution.py:151
  116.6 4.8 %collective-permute-start.13 = (f32[8,1,256]{2,1,0:T(1,128)S(1)}, f32[8,1,256]{2,1,0:T(1,128)S(1)}, u32[]{:S(2)}, u32[]{:S(2)}) collective-permute-start(f32[8,1,256]{2,1,0:T(1,128)S(1)} %get-tuple-element.41), channel_id=1, source_target_pairs={{0,1},{1,2},{2,3},{3,4},{4,5},{5,6},{6,7},{7,8},{8,9},{9,10},{10,1... | collective-permute-start | bytes 24584 | tf_op jit(solution)/shard_map/ppermute | solution.py:150
  118.7 7.1 %collective-permute-start.14 = (f32[8,1,256]{2,1,0:T(1,128)S(1)}, f32[8,1,256]{2,1,0:T(1,128)S(1)}, u32[]{:S(2)}, u32[]{:S(2)}) collective-permute-start(f32[8,1,256]{2,1,0:T(1,128)S(1)} %get-tuple-element.42), channel_id=1, source_target_pairs={{1,0},{2,1},{3,2},{4,3},{5,4},{6,5},{7,6},{8,7},{9,8},{10,9},{11,1... | collective-permute-start | bytes 24584 | tf_op jit(solution)/shard_map/ppermute | solution.py:151
  126.5 11.3 %collective-permute-start.16 = (f32[8,8,1]{2,1,0:T(8,128)S(1)}, f32[8,8,1]{2,1,0:T(8,128)S(1)}, u32[]{:S(2)}, u32[]{:S(2)}) collective-permute-start(f32[8,8,1]{2,1,0:T(8,128)S(1)} %get-tuple-element.33), channel_id=1, source_target_pairs={{0,64},{1,65},{2,66},{3,67},{4,68},{5,69},{6,70},{7,71},{8,72},{9,... | collective-permute-start | bytes 776 | tf_op jit(solution)/shard_map/ppermute | solution.py:150
  127.8 10.0 %collective-permute-start.19 = (f32[8,8,1]{2,1,0:T(8,128)S(1)}, f32[8,8,1]{2,1,0:T(8,128)S(1)}, u32[]{:S(2)}, u32[]{:S(2)}) collective-permute-start(f32[8,8,1]{2,1,0:T(8,128)S(1)} %get-tuple-element.34), channel_id=1, source_target_pairs={{64,0},{65,1},{66,2},{67,3},{68,4},{69,5},{70,6},{71,7},{72,8},{73... | collective-permute-start | bytes 776 | tf_op jit(solution)/shard_map/ppermute | solution.py:151
  133.3 4.5 %collective-permute-start.17 = (f32[8,1,256]{2,1,0:T(1,128)S(1)}, f32[8,1,256]{2,1,0:T(1,128)S(1)}, u32[]{:S(2)}, u32[]{:S(2)}) collective-permute-start(f32[8,1,256]{2,1,0:T(1,128)S(1)} %get-tuple-element.35), channel_id=1, source_target_pairs={{0,1},{1,2},{2,3},{3,4},{4,5},{5,6},{6,7},{7,8},{8,9},{9,10},{10,1... | collective-permute-start | bytes 24584 | tf_op jit(solution)/shard_map/ppermute | solution.py:150
  135.8 7.1 %collective-permute-start.18 = (f32[8,1,256]{2,1,0:T(1,128)S(1)}, f32[8,1,256]{2,1,0:T(1,128)S(1)}, u32[]{:S(2)}, u32[]{:S(2)}) collective-permute-start(f32[8,1,256]{2,1,0:T(1,128)S(1)} %get-tuple-element.36), channel_id=1, source_target_pairs={{1,0},{2,1},{3,2},{4,3},{5,4},{6,5},{7,6},{8,7},{9,8},{10,9},{11,1... | collective-permute-start | bytes 24584 | tf_op jit(solution)/shard_map/ppermute | solution.py:151

commit v9 on v8

--- a/solution.py
+++ b/solution.py
@@ -7,7 +7,7 @@
 from jax.sharding import PartitionSpec as P
 
 SWEEPS = 3
-SB = 4
+SB = 8
 EB = 4
 
 

time: 145 us -> 145 us (level)
  no operation moved by 1% of the time
where the time goes in v9:
time: 145 us; the launch traced here: 144 us
  starting transfers between devices  55.9 us (39%)
  Pallas kernels  44 us (30%)
  waiting for transfers between devices  31.9 us (22%)
  blocking collectives  4.65 us (3%)
  other arithmetic  3.26 us (2%)
  local copies, waits for them, and re-layouts  3.2 us (2%)
    ppermute x10, starting transfers between devices, exchange(): after = lax.ppermute(first, axes, shift_pairs(n, -1))  34.3 us
    pallas_call x2, Pallas kernels, advect_step(): pl.pallas_call(step_kernel, grid=(nsp // SB,), in_specs=[main, pl.BlockSp...  27.7 us
    ppermute x10, starting transfers between devices, exchange(): before = lax.ppermute(last, axes, shift_pairs(n, 1))  21.6 us
    pallas_call x2, Pallas kernels, edges(): pl.pallas_call(functools.partial(edge_kernel, nmain), grid=(total // nb,)...  16.2 us
    ppermute x10, waiting for transfers between devices, exchange(): before = lax.ppermute(last, axes, shift_pairs(n, 1))  16.1 us
    ppermute x10, waiting for transfers between devices, exchange(): after = lax.ppermute(first, axes, shift_pairs(n, -1))  15.7 us
    all_to_all x1, blocking collectives, on_device(): lax.all_to_all(forcing_fields(advected), 'gy', split_axis=1, concat_axis=...  4.65 us
  transfers between devices with their start and end apart: 20, of which 6 were waited for; matrix products, arithmetic and copies ran while one was open for 1% of the time, Pallas kernels for 15%

profile of v9, /device:TPU:31, one launch (start us, length us, event | category | flops | bytes accessed | tf_op | source)
XLA Modules:
  0.0 144.1 jit_solution(15375736583182391000)
XLA Ops:
  0.7 8.6 %shard_map.95 = (f32[20,60,128]{2,1,0:T(8,128)}, f32[20,60,128]{2,1,0:T(8,128)}, f32[20,16,128]{2,1,0:T(8,128)}, f32[20,16,128]{2,1,0:T(8,128)}) custom-call(f32[16,60,16,128]{3,2,1,0:T(8,128)} %f_ref.3, f32[2,60,16,128]{3,2,1,0:T(8,128)} %w_ref.3), custom_call_target="tpu_custom_call" | custom-call | flops 9830400 | bytes 9830400 | tf_op jit(solution)/shard_map/pallas_call | solution.py:72
  9.3 3.4 %collective-permute-start = (f32[20,60,128]{2,1,0:T(8,128)}, f32[20,60,128]{2,1,0:T(8,128)S(1)}, u32[]{:S(2)}, u32[]{:S(2)}) collective-permute-start(f32[20,60,128]{2,1,0:T(8,128)} %get-tuple-element.10), channel_id=1, source_target_pairs={{0,2},{2,4},{4,6},{6,8},{8,10},{10,12},{12,14},{14,16},{16,18},{18... | collective-permute-start | bytes 1843208 | tf_op jit(solution)/shard_map/ppermute | solution.py:150
  12.7 1.9 %collective-permute-start.1 = (f32[20,60,128]{2,1,0:T(8,128)}, f32[20,60,128]{2,1,0:T(8,128)S(1)}, u32[]{:S(2)}, u32[]{:S(2)}) collective-permute-start(f32[20,60,128]{2,1,0:T(8,128)} %get-tuple-element.11), channel_id=1, source_target_pairs={{2,0},{4,2},{6,4},{8,6},{10,8},{12,10},{14,12},{16,14},{18,16},{20... | collective-permute-start | bytes 1843208 | tf_op jit(solution)/shard_map/ppermute | solution.py:151
  14.7 1.3 collective-permute-start.2
  16.0 0.1 select_reduce_fusion.1
  16.1 0.1 fusion.70
  16.2 1.3 collective-permute-start.8
  17.5 6.5 %collective-permute-start.11 = (f32[10,8,1]{2,1,0:T(8,128)S(1)}, f32[10,8,1]{2,1,0:T(8,128)S(1)}, u32[]{:S(2)}, u32[]{:S(2)}) collective-permute-start(f32[10,8,1]{2,1,0:T(8,128)S(1)} %get-tuple-element.30), channel_id=1, source_target_pairs={{64,0},{65,1},{66,2},{67,3},{68,4},{69,5},{70,6},{71,7},{72,8},{73... | collective-permute-start | bytes 968 | tf_op jit(solution)/shard_map/ppermute | solution.py:151
  24.0 13.6 %collective-permute-done.8 = f32[10,8,1]{2,1,0:T(8,128)S(1)} collective-permute-done((f32[10,8,1]{2,1,0:T(8,128)S(1)}, f32[10,8,1]{2,1,0:T(8,128)S(1)}, u32[]{:S(2)}, u32[]{:S(2)}) %collective-permute-start.8) | collective-permute-done | bytes 352 | tf_op jit(solution)/shard_map/ppermute | solution.py:150
  37.6 1.3 collective-permute-start.3
  38.9 0.0 collective-permute-done.11
  38.9 2.5 %collective-permute-start.10 = (f32[10,1,256]{2,1,0:T(1,128)S(1)}, f32[10,1,256]{2,1,0:T(1,128)S(1)}, u32[]{:S(2)}, u32[]{:S(2)}) collective-permute-start(f32[10,1,256]{2,1,0:T(1,128)S(1)} %get-tuple-element.28), channel_id=1, source_target_pairs={{1,0},{2,1},{3,2},{4,3},{5,4},{6,5},{7,6},{8,7},{9,8},{10,9},{11,1... | collective-permute-start | bytes 30728 | tf_op jit(solution)/shard_map/ppermute | solution.py:151
  41.4 0.0 collective-permute-done.2.fleft_ref.wleft_ref
  41.4 5.2 %collective-permute-start.9 = (f32[10,1,256]{2,1,0:T(1,128)S(1)}, f32[10,1,256]{2,1,0:T(1,128)S(1)}, u32[]{:S(2)}, u32[]{:S(2)}) collective-permute-start(f32[10,1,256]{2,1,0:T(1,128)S(1)} %get-tuple-element.27), channel_id=1, source_target_pairs={{0,1},{1,2},{2,3},{3,4},{4,5},{5,6},{6,7},{7,8},{8,9},{9,10},{10,1... | collective-permute-start | bytes 30728 | tf_op jit(solution)/shard_map/ppermute | solution.py:150
  46.7 0.0 collective-permute-done.3.fright_ref.wright_ref
  46.7 0.0 collective-permute-done.ftop_ref.wtop_ref
  46.8 0.6 copy-done.4
  47.4 0.3 copy-done
  47.7 0.9 copy-done.1
  48.5 13.8 %shard_map.96.f_ref = f32[16,60,16,128]{3,2,1,0:T(8,128)} custom-call(f32[16,60,16,128]{3,2,1,0:T(8,128)} %f_ref.3, f32[2,60,16,128]{3,2,1,0:T(8,128)} %w_ref.3, f32[20,60,128]{2,1,0:T(8,128)} %copy-done, f32[20,60,128]{2,1,0:T(8,128)} %copy-done.1, f32[20,60,128]{2,1,0:T(8,128)} %copy-done, f32[20,60,128]{2,1,0:T(8,128)} %copy-done.1, ...), custom_call_target="tpu_custom_call" | custom-call | flops 39321600 | bytes 16711680 | tf_op jit(solution)/shard_map/pallas_call | solution.py:137
  62.3 7.6 %shard_map.97 = (f32[16,60,128]{2,1,0:T(8,128)}, f32[16,60,128]{2,1,0:T(8,128)}, f32[16,16,128]{2,1,0:T(8,128)}, f32[16,16,128]{2,1,0:T(8,128)}) custom-call(f32[16,60,16,128]{3,2,1,0:T(8,128)} %shard_map.96.f_ref), custom_call_target="tpu_custom_call" | custom-call | flops 7864320 | bytes 7864320 | tf_op jit(solution)/shard_map/pallas_call | solution.py:72
  69.9 1.9 %collective-permute-start.4 = (f32[16,60,128]{2,1,0:T(8,128)}, f32[16,60,128]{2,1,0:T(8,128)S(1)}, u32[]{:S(2)}, u32[]{:S(2)}) collective-permute-start(f32[16,60,128]{2,1,0:T(8,128)} %get-tuple-element.14), channel_id=1, source_target_pairs={{0,2},{2,4},{4,6},{6,8},{8,10},{10,12},{12,14},{14,16},{16,18},{18... | collective-permute-start | bytes 1474568 | tf_op jit(solution)/shard_map/ppermute | solution.py:150
  71.8 3.4 %collective-permute-start.5 = (f32[16,60,128]{2,1,0:T(8,128)}, f32[16,60,128]{2,1,0:T(8,128)S(1)}, u32[]{:S(2)}, u32[]{:S(2)}) collective-permute-start(f32[16,60,128]{2,1,0:T(8,128)} %get-tuple-element.15), channel_id=1, source_target_pairs={{2,0},{4,2},{6,4},{8,6},{10,8},{12,10},{14,12},{16,14},{18,16},{20... | collective-permute-start | bytes 1474568 | tf_op jit(solution)/shard_map/ppermute | solution.py:151
  75.2 0.0 collective-permute-done.10
  75.2 0.1 maximum_bitcast_fusion.1
  75.3 0.2 fusion.3
  75.5 0.1 slice.312
  75.6 1.3 collective-permute-start.6
  76.9 3.2 %collective-permute-start.7 = (f32[16,16,128]{2,1,0:T(8,128)}, f32[16,16,128]{2,1,0:T(8,128)S(1)}, u32[]{:S(2)}, u32[]{:S(2)}) collective-permute-start(f32[16,16,128]{2,1,0:T(8,128)} %get-tuple-element.17), channel_id=1, source_target_pairs={{1,0},{64,1},{65,64},{3,2},{66,3},{67,66},{5,4},{68,5},{69,68},{7,... | collective-permute-start | bytes 393224 | tf_op jit(solution)/shard_map/ppermute | solution.py:151
  80.1 0.1 fusion.58
  80.2 0.0 copy-start.11
  80.3 0.0 copy-start.5
  80.3 0.8 collective-permute-done.7.fright_ref
  81.1 2.5 %collective-permute-done.4.ftop_ref = f32[16,60,128]{2,1,0:T(8,128)S(1)} collective-permute-done((f32[16,60,128]{2,1,0:T(8,128)}, f32[16,60,128]{2,1,0:T(8,128)S(1)}, u32[]{:S(2)}, u32[]{:S(2)}) %collective-permute-start.4) | collective-permute-done | bytes 491552 | tf_op jit(solution)/shard_map/ppermute | solution.py:150
  83.6 5.5 %collective-permute-done.5.fbot_ref = f32[16,60,128]{2,1,0:T(8,128)S(1)} collective-permute-done((f32[16,60,128]{2,1,0:T(8,128)}, f32[16,60,128]{2,1,0:T(8,128)S(1)}, u32[]{:S(2)}, u32[]{:S(2)}) %collective-permute-start.5) | collective-permute-done | bytes 491552 | tf_op jit(solution)/shard_map/ppermute | solution.py:151
  89.2 0.8 copy-done.7
  90.0 14.0 %shard_map.98 = f32[16,60,16,128]{3,2,1,0:T(8,128)} custom-call(f32[16,60,16,128]{3,2,1,0:T(8,128)} %shard_map.96.f_ref, f32[2,60,16,128]{3,2,1,0:T(8,128)} %w_ref.3, f32[16,60,128]{2,1,0:T(8,128)} %copy-done.6, f32[16,60,128]{2,1,0:T(8,128)} %copy-done.7, f32[20,60,128]{2,1,0:T(8,128)} %copy-done, f32[20,60,128]{2,1,0:T(8,128)} %copy-done.1, ...), custom_call_target="tpu_custom_call" | custom-call | flops 39321600 | bytes 16711680 | tf_op jit(solution)/shard_map/pallas_call | solution.py:137
  103.9 0.8 compare_select_fusion.17
  104.7 4.7 %all_to_all.15 = f32[3,16,128]{2,0,1:T(4,128)S(1)} all-to-all(f32[3,16,128]{2,0,1:T(4,128)S(1)} %copy.12), channel_id=1, replica_groups=mesh['mp'=2,'gx'=32,'gy'=2] {'gy'}, dimensions={1} | all-to-all | bytes 49152 | tf_op jit(solution)/shard_map/all_to_all | solution.py:253
  109.4 0.2 fusion.12
  109.7 0.1 fusion.75
  109.8 1.3 collective-permute-start.12
  111.1 5.5 %collective-permute-start.15 = (f32[8,8,1]{2,1,0:T(8,128)S(1)}, f32[8,8,1]{2,1,0:T(8,128)S(1)}, u32[]{:S(2)}, u32[]{:S(2)}) collective-permute-start(f32[8,8,1]{2,1,0:T(8,128)S(1)} %get-tuple-element.40), channel_id=1, source_target_pairs={{64,0},{65,1},{66,2},{67,3},{68,4},{69,5},{70,6},{71,7},{72,8},{73... | collective-permute-start | bytes 776 | tf_op jit(solution)/shard_map/ppermute | solution.py:151
  116.6 2.1 %collective-permute-start.13 = (f32[8,1,256]{2,1,0:T(1,128)S(1)}, f32[8,1,256]{2,1,0:T(1,128)S(1)}, u32[]{:S(2)}, u32[]{:S(2)}) collective-permute-start(f32[8,1,256]{2,1,0:T(1,128)S(1)} %get-tuple-element.41), channel_id=1, source_target_pairs={{0,1},{1,2},{2,3},{3,4},{4,5},{5,6},{6,7},{7,8},{8,9},{9,10},{10,1... | collective-permute-start | bytes 24584 | tf_op jit(solution)/shard_map/ppermute | solution.py:150
  118.6 2.7 %collective-permute-start.14 = (f32[8,1,256]{2,1,0:T(1,128)S(1)}, f32[8,1,256]{2,1,0:T(1,128)S(1)}, u32[]{:S(2)}, u32[]{:S(2)}) collective-permute-start(f32[8,1,256]{2,1,0:T(1,128)S(1)} %get-tuple-element.42), channel_id=1, source_target_pairs={{1,0},{2,1},{3,2},{4,3},{5,4},{6,5},{7,6},{8,7},{9,8},{10,9},{11,1... | collective-permute-start | bytes 24584 | tf_op jit(solution)/shard_map/ppermute | solution.py:151
  121.3 0.0 collective-permute-done.12
  121.4 0.0 collective-permute-done.15
  121.4 4.3 %collective-permute-done.14 = f32[8,1,256]{2,1,0:T(1,128)S(1)} collective-permute-done((f32[8,1,256]{2,1,0:T(1,128)S(1)}, f32[8,1,256]{2,1,0:T(1,128)S(1)}, u32[]{:S(2)}, u32[]{:S(2)}) %collective-permute-start.14) | collective-permute-done | bytes 8224 | tf_op jit(solution)/shard_map/ppermute | solution.py:151
  125.7 0.2 fusion.6
  125.9 0.1 fusion.59
  126.0 0.1 slice.326
  126.1 0.2 fusion.15
  126.4 0.1 fusion.72
  126.4 1.3 collective-permute-start.16
  127.7 5.5 %collective-permute-start.19 = (f32[8,8,1]{2,1,0:T(8,128)S(1)}, f32[8,8,1]{2,1,0:T(8,128)S(1)}, u32[]{:S(2)}, u32[]{:S(2)}) collective-permute-start(f32[8,8,1]{2,1,0:T(8,128)S(1)} %get-tuple-element.34), channel_id=1, source_target_pairs={{64,0},{65,1},{66,2},{67,3},{68,4},{69,5},{70,6},{71,7},{72,8},{73... | collective-permute-start | bytes 776 | tf_op jit(solution)/shard_map/ppermute | solution.py:151
  133.2 2.5 %collective-permute-start.17 = (f32[8,1,256]{2,1,0:T(1,128)S(1)}, f32[8,1,256]{2,1,0:T(1,128)S(1)}, u32[]{:S(2)}, u32[]{:S(2)}) collective-permute-start(f32[8,1,256]{2,1,0:T(1,128)S(1)} %get-tuple-element.35), channel_id=1, source_target_pairs={{0,1},{1,2},{2,3},{3,4},{4,5},{5,6},{6,7},{7,8},{8,9},{9,10},{10,1... | collective-permute-start | bytes 24584 | tf_op jit(solution)/shard_map/ppermute | solution.py:150
  135.8 1.9 %collective-permute-start.18 = (f32[8,1,256]{2,1,0:T(1,128)S(1)}, f32[8,1,256]{2,1,0:T(1,128)S(1)}, u32[]{:S(2)}, u32[]{:S(2)}) collective-permute-start(f32[8,1,256]{2,1,0:T(1,128)S(1)} %get-tuple-element.36), channel_id=1, source_target_pairs={{1,0},{2,1},{3,2},{4,3},{5,4},{6,5},{7,6},{8,7},{9,8},{10,9},{11,1... | collective-permute-start | bytes 24584 | tf_op jit(solution)/shard_map/ppermute | solution.py:151
  137.7 0.0 collective-permute-done.16
  137.7 0.0 collective-permute-done.19
  137.8 5.1 %collective-permute-done.18 = f32[8,1,256]{2,1,0:T(1,128)S(1)} collective-permute-done((f32[8,1,256]{2,1,0:T(1,128)S(1)}, f32[8,1,256]{2,1,0:T(1,128)S(1)}, u32[]{:S(2)}, u32[]{:S(2)}) %collective-permute-start.18) | collective-permute-done | bytes 8224 | tf_op jit(solution)/shard_map/ppermute | solution.py:151
  142.8 0.2 fusion.9
  143.0 0.1 fusion.60
  143.2 0.1 slice.340
  143.2 0.9 fusion.18
  (44 shorter events, 0.2 us)
Async XLA Ops:
  0.6 15.3 %copy-start.10 = (s32[8,256]{1,0:T(8,128)S(1)}, s32[8,256]{1,0:T(8,128)}, u32[]{:S(2)}) copy-start(s32[8,256]{1,0:T(8,128)} %param.12) | copy-start | bytes 24580
  0.6 15.3 %copy-start.12 = (f32[12]{0:T(128)S(1)}, f32[12]{0:T(128)}, u32[]{:S(2)}) copy-start(f32[12]{0:T(128)} %param.14) | copy-start | bytes 148
  0.7 15.3 %copy-start.13 = (f32[12]{0:T(128)S(1)}, f32[12]{0:T(128)}, u32[]{:S(2)}) copy-start(f32[12]{0:T(128)} %param.15) | copy-start | bytes 148
  0.7 15.4 %copy-start.2 = (f32[8,8,256]{2,1,0:T(8,128)S(1)}, f32[8,8,256]{2,1,0:T(8,128)}, u32[]{:S(2)}) copy-start(f32[8,8,256]{2,1,0:T(8,128)} %param.10) | copy-start | bytes 196612
  9.3 37.5 %collective-permute-start = (f32[20,60,128]{2,1,0:T(8,128)}, f32[20,60,128]{2,1,0:T(8,128)S(1)}, u32[]{:S(2)}, u32[]{:S(2)}) collective-permute-start(f32[20,60,128]{2,1,0:T(8,128)} %get-tuple-element.10), channel_id=1, source_target_pairs={{0,2},{2,4},{4,6},{6,8},{8,10},{10,12},{12,14},{14,16},{16,18},{18... | collective-permute-start | bytes 1843208 | tf_op jit(solution)/shard_map/ppermute | solution.py:150
  12.7 34.0 %collective-permute-start.1 = (f32[20,60,128]{2,1,0:T(8,128)}, f32[20,60,128]{2,1,0:T(8,128)S(1)}, u32[]{:S(2)}, u32[]{:S(2)}) collective-permute-start(f32[20,60,128]{2,1,0:T(8,128)} %get-tuple-element.11), channel_id=1, source_target_pairs={{2,0},{4,2},{6,4},{8,6},{10,8},{12,10},{14,12},{16,14},{18,16},{20... | collective-permute-start | bytes 1843208 | tf_op jit(solution)/shard_map/ppermute | solution.py:151
  14.7 26.8 %collective-permute-start.2 = (f32[20,16,128]{2,1,0:T(8,128)}, f32[20,16,128]{2,1,0:T(8,128)S(1)}, u32[]{:S(2)}, u32[]{:S(2)}) collective-permute-start(f32[20,16,128]{2,1,0:T(8,128)} %get-tuple-element.12), channel_id=1, source_target_pairs={{0,1},{1,64},{64,65},{2,3},{3,66},{66,67},{4,5},{5,68},{68,69},{6,... | collective-permute-start | bytes 491528 | tf_op jit(solution)/shard_map/ppermute | solution.py:150
  16.2 21.4 %collective-permute-start.8 = (f32[10,8,1]{2,1,0:T(8,128)S(1)}, f32[10,8,1]{2,1,0:T(8,128)S(1)}, u32[]{:S(2)}, u32[]{:S(2)}) collective-permute-start(f32[10,8,1]{2,1,0:T(8,128)S(1)} %get-tuple-element.29), channel_id=1, source_target_pairs={{0,64},{1,65},{2,66},{3,67},{4,68},{5,69},{6,70},{7,71},{8,72},{9,... | collective-permute-start | bytes 968 | tf_op jit(solution)/shard_map/ppermute | solution.py:150
  17.5 21.4 %collective-permute-start.11 = (f32[10,8,1]{2,1,0:T(8,128)S(1)}, f32[10,8,1]{2,1,0:T(8,128)S(1)}, u32[]{:S(2)}, u32[]{:S(2)}) collective-permute-start(f32[10,8,1]{2,1,0:T(8,128)S(1)} %get-tuple-element.30), channel_id=1, source_target_pairs={{64,0},{65,1},{66,2},{67,3},{68,4},{69,5},{70,6},{71,7},{72,8},{73... | collective-permute-start | bytes 968 | tf_op jit(solution)/shard_map/ppermute | solution.py:151
  37.6 9.1 %collective-permute-start.3 = (f32[20,16,128]{2,1,0:T(8,128)}, f32[20,16,128]{2,1,0:T(8,128)S(1)}, u32[]{:S(2)}, u32[]{:S(2)}) collective-permute-start(f32[20,16,128]{2,1,0:T(8,128)} %get-tuple-element.13), channel_id=1, source_target_pairs={{1,0},{64,1},{65,64},{3,2},{66,3},{67,66},{5,4},{68,5},{69,68},{7,... | collective-permute-start | bytes 491528 | tf_op jit(solution)/shard_map/ppermute | solution.py:151
  38.9 36.3 %collective-permute-start.10 = (f32[10,1,256]{2,1,0:T(1,128)S(1)}, f32[10,1,256]{2,1,0:T(1,128)S(1)}, u32[]{:S(2)}, u32[]{:S(2)}) collective-permute-start(f32[10,1,256]{2,1,0:T(1,128)S(1)} %get-tuple-element.28), channel_id=1, source_target_pairs={{1,0},{2,1},{3,2},{4,3},{5,4},{6,5},{7,6},{8,7},{9,8},{10,9},{11,1... | collective-permute-start | bytes 30728 | tf_op jit(solution)/shard_map/ppermute | solution.py:151
  41.4 5.3 %copy-start.3 = (f32[20,16,128]{2,1,0:T(8,128)}, f32[20,16,128]{2,1,0:T(8,128)S(1)}, u32[]{:S(2)}) copy-start(f32[20,16,128]{2,1,0:T(8,128)S(1)} %collective-permute-done.2.fleft_ref.wleft_ref) | copy-start | bytes 491524
  41.4 33.8 %collective-permute-start.9 = (f32[10,1,256]{2,1,0:T(1,128)S(1)}, f32[10,1,256]{2,1,0:T(1,128)S(1)}, u32[]{:S(2)}, u32[]{:S(2)}) collective-permute-start(f32[10,1,256]{2,1,0:T(1,128)S(1)} %get-tuple-element.27), channel_id=1, source_target_pairs={{0,1},{1,2},{2,3},{3,4},{4,5},{5,6},{6,7},{7,8},{8,9},{9,10},{10,1... | collective-permute-start | bytes 30728 | tf_op jit(solution)/shard_map/ppermute | solution.py:150
  46.7 0.7 copy-start.4
  46.7 0.9 copy-start
  47.7 0.9 copy-start.1
  69.9 13.7 %collective-permute-start.4 = (f32[16,60,128]{2,1,0:T(8,128)}, f32[16,60,128]{2,1,0:T(8,128)S(1)}, u32[]{:S(2)}, u32[]{:S(2)}) collective-permute-start(f32[16,60,128]{2,1,0:T(8,128)} %get-tuple-element.14), channel_id=1, source_target_pairs={{0,2},{2,4},{4,6},{6,8},{8,10},{10,12},{12,14},{14,16},{16,18},{18... | collective-permute-start | bytes 1474568 | tf_op jit(solution)/shard_map/ppermute | solution.py:150
  71.8 17.3 %collective-permute-start.5 = (f32[16,60,128]{2,1,0:T(8,128)}, f32[16,60,128]{2,1,0:T(8,128)S(1)}, u32[]{:S(2)}, u32[]{:S(2)}) collective-permute-start(f32[16,60,128]{2,1,0:T(8,128)} %get-tuple-element.15), channel_id=1, source_target_pairs={{2,0},{4,2},{6,4},{8,6},{10,8},{12,10},{14,12},{16,14},{18,16},{20... | collective-permute-start | bytes 1474568 | tf_op jit(solution)/shard_map/ppermute | solution.py:151
  75.6 4.7 %collective-permute-start.6 = (f32[16,16,128]{2,1,0:T(8,128)}, f32[16,16,128]{2,1,0:T(8,128)S(1)}, u32[]{:S(2)}, u32[]{:S(2)}) collective-permute-start(f32[16,16,128]{2,1,0:T(8,128)} %get-tuple-element.16), channel_id=1, source_target_pairs={{0,1},{1,64},{64,65},{2,3},{3,66},{66,67},{4,5},{5,68},{68,69},{6,... | collective-permute-start | bytes 393224 | tf_op jit(solution)/shard_map/ppermute | solution.py:150
  76.9 4.2 %collective-permute-start.7 = (f32[16,16,128]{2,1,0:T(8,128)}, f32[16,16,128]{2,1,0:T(8,128)S(1)}, u32[]{:S(2)}, u32[]{:S(2)}) collective-permute-start(f32[16,16,128]{2,1,0:T(8,128)} %get-tuple-element.17), channel_id=1, source_target_pairs={{1,0},{64,1},{65,64},{3,2},{66,3},{67,66},{5,4},{68,5},{69,68},{7,... | collective-permute-start | bytes 393224 | tf_op jit(solution)/shard_map/ppermute | solution.py:151
  80.2 29.2 %copy-start.11 = (s32[8,256]{1,0:T(8,128)S(1)}, s32[8,256]{1,0:T(8,128)}, u32[]{:S(2)}) copy-start(s32[8,256]{1,0:T(8,128)} %param.13) | copy-start | bytes 24580
  80.3 29.2 %copy-start.5 = (f32[8,8,256]{2,1,0:T(8,128)S(1)}, f32[8,8,256]{2,1,0:T(8,128)}, u32[]{:S(2)}) copy-start(f32[8,8,256]{2,1,0:T(8,128)} %param.11) | copy-start | bytes 196612
  80.3 8.9 %copy-start.8 = (f32[16,16,128]{2,1,0:T(8,128)}, f32[16,16,128]{2,1,0:T(8,128)S(1)}, u32[]{:S(2)}) copy-start(f32[16,16,128]{2,1,0:T(8,128)S(1)} %collective-permute-done.6.fleft_ref) | copy-start | bytes 393220
  81.1 8.0 %copy-start.9 = (f32[16,16,128]{2,1,0:T(8,128)}, f32[16,16,128]{2,1,0:T(8,128)S(1)}, u32[]{:S(2)}) copy-start(f32[16,16,128]{2,1,0:T(8,128)S(1)} %collective-permute-done.7.fright_ref) | copy-start | bytes 393220
  83.6 5.5 %copy-start.6 = (f32[16,60,128]{2,1,0:T(8,128)}, f32[16,60,128]{2,1,0:T(8,128)S(1)}, u32[]{:S(2)}) copy-start(f32[16,60,128]{2,1,0:T(8,128)S(1)} %collective-permute-done.4.ftop_ref) | copy-start | bytes 1474564
  89.1 0.8 copy-start.7
  109.8 11.6 %collective-permute-start.12 = (f32[8,8,1]{2,1,0:T(8,128)S(1)}, f32[8,8,1]{2,1,0:T(8,128)S(1)}, u32[]{:S(2)}, u32[]{:S(2)}) collective-permute-start(f32[8,8,1]{2,1,0:T(8,128)S(1)} %get-tuple-element.39), channel_id=1, source_target_pairs={{0,64},{1,65},{2,66},{3,67},{4,68},{5,69},{6,70},{7,71},{8,72},{9,... | collective-permute-start | bytes 776 | tf_op jit(solution)/shard_map/ppermute | solution.py:150
  111.1 10.3 %collective-permute-start.15 = (f32[8,8,1]{2,1,0:T(8,128)S(1)}, f32[8,8,1]{2,1,0:T(8,128)S(1)}, u32[]{:S(2)}, u32[]{:S(2)}) collective-permute-start(f32[8,8,1]{2,1,0:T(8,128)S(1)} %get-tuple-element.40), channel_id=1, source_target_pairs={{64,0},{65,1},{66,2},{67,3},{68,4},{69,5},{70,6},{71,7},{72,8},{73... | collective-permute-start | bytes 776 | tf_op jit(solution)/shard_map/ppermute | solution.py:151
  116.6 4.8 %collective-permute-start.13 = (f32[8,1,256]{2,1,0:T(1,128)S(1)}, f32[8,1,256]{2,1,0:T(1,128)S(1)}, u32[]{:S(2)}, u32[]{:S(2)}) collective-permute-start(f32[8,1,256]{2,1,0:T(1,128)S(1)} %get-tuple-element.41), channel_id=1, source_target_pairs={{0,1},{1,2},{2,3},{3,4},{4,5},{5,6},{6,7},{7,8},{8,9},{9,10},{10,1... | collective-permute-start | bytes 24584 | tf_op jit(solution)/shard_map/ppermute | solution.py:150
  118.6 7.1 %collective-permute-start.14 = (f32[8,1,256]{2,1,0:T(1,128)S(1)}, f32[8,1,256]{2,1,0:T(1,128)S(1)}, u32[]{:S(2)}, u32[]{:S(2)}) collective-permute-start(f32[8,1,256]{2,1,0:T(1,128)S(1)} %get-tuple-element.42), channel_id=1, source_target_pairs={{1,0},{2,1},{3,2},{4,3},{5,4},{6,5},{7,6},{8,7},{9,8},{10,9},{11,1... | collective-permute-start | bytes 24584 | tf_op jit(solution)/shard_map/ppermute | solution.py:151
  126.4 11.3 %collective-permute-start.16 = (f32[8,8,1]{2,1,0:T(8,128)S(1)}, f32[8,8,1]{2,1,0:T(8,128)S(1)}, u32[]{:S(2)}, u32[]{:S(2)}) collective-permute-start(f32[8,8,1]{2,1,0:T(8,128)S(1)} %get-tuple-element.33), channel_id=1, source_target_pairs={{0,64},{1,65},{2,66},{3,67},{4,68},{5,69},{6,70},{7,71},{8,72},{9,... | collective-permute-start | bytes 776 | tf_op jit(solution)/shard_map/ppermute | solution.py:150
  127.7 10.0 %collective-permute-start.19 = (f32[8,8,1]{2,1,0:T(8,128)S(1)}, f32[8,8,1]{2,1,0:T(8,128)S(1)}, u32[]{:S(2)}, u32[]{:S(2)}) collective-permute-start(f32[8,8,1]{2,1,0:T(8,128)S(1)} %get-tuple-element.34), channel_id=1, source_target_pairs={{64,0},{65,1},{66,2},{67,3},{68,4},{69,5},{70,6},{71,7},{72,8},{73... | collective-permute-start | bytes 776 | tf_op jit(solution)/shard_map/ppermute | solution.py:151
  133.2 4.5 %collective-permute-start.17 = (f32[8,1,256]{2,1,0:T(1,128)S(1)}, f32[8,1,256]{2,1,0:T(1,128)S(1)}, u32[]{:S(2)}, u32[]{:S(2)}) collective-permute-start(f32[8,1,256]{2,1,0:T(1,128)S(1)} %get-tuple-element.35), channel_id=1, source_target_pairs={{0,1},{1,2},{2,3},{3,4},{4,5},{5,6},{6,7},{7,8},{8,9},{9,10},{10,1... | collective-permute-start | bytes 24584 | tf_op jit(solution)/shard_map/ppermute | solution.py:150
  135.8 7.1 %collective-permute-start.18 = (f32[8,1,256]{2,1,0:T(1,128)S(1)}, f32[8,1,256]{2,1,0:T(1,128)S(1)}, u32[]{:S(2)}, u32[]{:S(2)}) collective-permute-start(f32[8,1,256]{2,1,0:T(1,128)S(1)} %get-tuple-element.36), channel_id=1, source_target_pairs={{1,0},{2,1},{3,2},{4,3},{5,4},{6,5},{7,6},{8,7},{9,8},{10,9},{11,1... | collective-permute-start | bytes 24584 | tf_op jit(solution)/shard_map/ppermute | solution.py:151
